TPU v7x, 32 devices: a whole 2x2x4 slice. The times are simulated.
32 devices in a mesh: groups: 2 (over x), tile: 16 (over z, y, core).
Axes of the slice: x: 2, y: 2, z: 4, core: 2. Of those that a mesh axis runs over, the one named last changes fastest.
Arguments:
- hidden_in: bfloat16 [2048, 4096], P('groups', 'tile'), parts along dimension 0, may hold values from -6 to 6
- w_up: bfloat16 [16, 1024, 4096], P('tile'), may hold values from -0.09375 to 0.09375
- w_down: bfloat16 [16, 4096, 1024], P('tile'), may hold values from -0.046875 to 0.046875
- out_grad: bfloat16 [2048, 4096], P('groups', 'tile'), parts along dimension 0, may hold values from -6 to 6
Outputs:
- block_out: bfloat16 [2048, 4096], P('groups', 'tile'), parts along dimension 0
- input_grad: bfloat16 [2048, 4096], P('groups', 'tile'), parts along dimension 0
- grad_up: bfloat16 [16, 2048, 4096], P('tile', 'groups'), parts along dimension 1
- grad_down: bfloat16 [16, 8192, 1024], P('tile', 'groups'), parts along dimension 1
There are 2 independent parts, one for each index of `groups`. A program takes and returns all parts, laid end to end along the dimension named above; an argument that names none is the same for every part. Nothing has to cross between parts.
All inputs are finite; a program needn't handle non-finite values.
Results may differ from a plain program's by a relative error of at most 0.0062.
Values may be sent and summed in bfloat16 or wider, within the bound.
No kernel may reach another device: no remote copies, remote signals or barrier semaphores. Data moves between devices by JAX's collectives and lax.ppermute only.
A program may use at most 256 MiB of HBM per device.

v0:
```python
import jax
import jax.numpy as jnp
from jax import lax
from jax.sharding import PartitionSpec as P

Q = 4


root_half = 0.7071067811865476
inv_root_tau = 0.3989422804014327


def from_partner(value, axis, distance):
    mask = 2**distance
    pairs = [(source, source ^ mask) for source in range(lax.axis_size(axis))]
    return lax.ppermute(value, axis, pairs)


def passed_along(shard, axis, by):
    count = lax.axis_size(axis)
    return lax.ppermute(shard, axis, [(i, (i + by) % count) for i in range(count)])


def gelu_value(values):
    return 0.5 * values * (1.0 + lax.erf(values * root_half))


def gelu_slope(values):
    return (
        0.5 * (1.0 + lax.erf(values * root_half))
        + values * jnp.exp(-0.5 * values * values) * inv_root_tau
    )


def row_collect(piece, row_pos, depth_bits):
    collected = piece
    for bit_pos in range(depth_bits):
        partner = from_partner(collected, "tile", bit_pos)
        upper_side = row_pos // (1 << bit_pos) % 2 == 1
        collected = jnp.where(
            upper_side,
            jnp.concatenate([partner, collected], axis=1),
            jnp.concatenate([collected, partner], axis=1),
        )
    return collected


def row_total(partial_value, row_pos, depth_bits):
    for bit_pos in reversed(range(depth_bits)):
        half_cols = partial_value.shape[1] // 2
        lower_half = partial_value[:, :half_cols]
        upper_half = partial_value[:, half_cols:]
        upper_side = row_pos // (1 << bit_pos) % 2 == 1
        kept_half = jnp.where(upper_side, upper_half, lower_half)
        outgoing = jnp.where(upper_side, lower_half, upper_half)
        partial_value = kept_half + from_partner(outgoing, "tile", bit_pos)
    return partial_value


def cycle_spread(partial_value, cycle_pos, row_width):
    block_rows = partial_value.shape[0] // Q
    shares = lax.optimization_barrier(partial_value.astype(jnp.bfloat16)).reshape(
        Q, block_rows, partial_value.shape[1]
    )
    summed = lax.dynamic_index_in_dim(shares, cycle_pos, 0, keepdims=False).astype(jnp.float32)
    for distance in range(1, Q):
        outgoing = lax.dynamic_index_in_dim(shares, (cycle_pos + distance) % Q, 0, keepdims=False)
        incoming = passed_along(outgoing, "tile", distance * row_width)
        summed = summed + incoming.astype(jnp.float32)
    return summed


def arrange_cycle(pieces, cycle_pos):
    stacked = jnp.stack(pieces[::-1])
    rolled = jnp.roll(stacked, cycle_pos + 1, axis=0)
    return rolled.reshape(-1, stacked.shape[2])


def cycle_join_sums(tile_rows, cycle_pos, row_width):
    pieces = [tile_rows]
    for distance in range(1, Q):
        pieces.append(passed_along(tile_rows, "tile", distance * row_width))
    return arrange_cycle(pieces, cycle_pos)


def on_device(hidden_in, w_up, w_down, out_grad):
    tile_count = lax.axis_size("tile")
    row_width = tile_count // Q
    depth_bits = row_width.bit_length() - 1
    cycle_pos = lax.axis_index("tile") // row_width
    row_pos = lax.axis_index("tile") % row_width
    up_tile = w_up[0]
    down_tile = w_down[0]
    x_rows = row_collect(hidden_in, row_pos, depth_bits)
    preact = cycle_spread(
        jnp.dot(x_rows, up_tile, preferred_element_type=jnp.float32), cycle_pos, row_width
    )
    preact_all = cycle_join_sums(preact, cycle_pos, row_width)
    activation = gelu_value(preact_all).astype(jnp.bfloat16)
    out_part = jnp.dot(activation, down_tile, preferred_element_type=jnp.float32)
    block_out = (hidden_in.astype(jnp.float32) + row_total(out_part, row_pos, depth_bits)).astype(
        jnp.bfloat16
    )
    grad_rows = row_collect(out_grad, row_pos, depth_bits)
    act_part = lax.dot_general(
        grad_rows, down_tile, (((1,), (1,)), ((), ())), preferred_element_type=jnp.float32
    )
    act_grad = cycle_spread(act_part, cycle_pos, row_width)
    pre_grad = (cycle_join_sums(act_grad, cycle_pos, row_width) * gelu_slope(preact_all)).astype(
        jnp.bfloat16
    )
    grad_down = lax.dot_general(
        activation, grad_rows, (((0,), (0,)), ((), ())), preferred_element_type=jnp.float32
    ).astype(jnp.bfloat16)
    grad_up = lax.dot_general(
        x_rows, pre_grad, (((0,), (0,)), ((), ())), preferred_element_type=jnp.float32
    ).astype(jnp.bfloat16)
    back_part = lax.dot_general(
        pre_grad, up_tile, (((1,), (1,)), ((), ())), preferred_element_type=jnp.float32
    )
    input_grad = (out_grad.astype(jnp.float32) + row_total(back_part, row_pos, depth_bits)).astype(
        jnp.bfloat16
    )
    return (block_out, input_grad, grad_up[None], grad_down[None])


def solution(mesh):
    placed = (
        P("groups", "tile"),
        P("tile", None, None),
        P("tile", None, None),
        P("groups", "tile"),
    )
    return jax.shard_map(
        on_device,
        mesh=mesh,
        in_specs=placed,
        out_specs=(
            P("groups", "tile"),
            P("groups", "tile"),
            P("tile", "groups", None),
            P("tile", "groups", None),
        ),
        check_vma=False,
    )
```

profile of v0, /device:TPU:9, one launch (start us, length us, event | category | flops | bytes accessed | tf_op | source)
XLA Modules:
  0.0 1302.1 jit_solution(5898611377544653140)
XLA Ops:
  1.4 1.7 collective-permute-done
  3.1 1.4 maximum_select_fusion.2
  4.6 1.3 collective-permute-start.1
  5.9 23.1 %collective-permute-done.1 = bf16[1024,512]{1,0:T(8,128)(2,1)S(1)} collective-permute-done((bf16[1024,512]{1,0:T(8,128)(2,1)S(1)}, bf16[1024,512]{1,0:T(8,128)(2,1)S(1)}, u32[]{:S(2)}, u32[]{:S(2)}) %collective-permute-start.1) | collective-permute-done | bytes 1048608 | tf_op jit(solution)/shard_map/ppermute | solution.py:16
  29.0 11.6 fusion.38
  40.7 2.8 dynamic-slice_bitcast_fusion.5
  43.5 2.5 copy-done
  45.9 1.3 collective-permute-start.2
  47.4 2.3 collective-permute-start.3
  49.7 2.0 collective-permute-start.10
  51.8 1.5 collective-permute-done.10
  53.5 1.3 collective-permute-start.11
  54.9 37.2 %collective-permute-done.2 = bf16[256,4096]{1,0:T(8,128)(2,1)S(1)} collective-permute-done((bf16[256,4096]{1,0:T(8,128)(2,1)}, bf16[256,4096]{1,0:T(8,128)(2,1)S(1)}, u32[]{:S(2)}, u32[]{:S(2)}) %collective-permute-start.2) | collective-permute-done | bytes 2097184 | tf_op jit(solution)/shard_map/ppermute | solution.py:21
  92.1 48.8 %collective-permute-done.4 = bf16[256,4096]{1,0:T(8,128)(2,1)} collective-permute-done((bf16[256,4096]{1,0:T(8,128)(2,1)}, bf16[256,4096]{1,0:T(8,128)(2,1)}, u32[]{:S(2)}, u32[]{:S(2)}) %collective-permute-start.4) | collective-permute-done | bytes 2097184 | tf_op jit(solution)/shard_map/ppermute | solution.py:21
  140.9 85.2 %collective-permute-done.3 = bf16[256,4096]{1,0:T(8,128)(2,1)} collective-permute-done((bf16[256,4096]{1,0:T(8,128)(2,1)}, bf16[256,4096]{1,0:T(8,128)(2,1)}, u32[]{:S(2)}, u32[]{:S(2)}) %collective-permute-start.3) | collective-permute-done | bytes 2097184 | tf_op jit(solution)/shard_map/ppermute | solution.py:21
  226.1 6.2 fusion.47
  232.3 2.7 collective-permute-start.7
  235.0 14.8 %fusion.41 = bf16[1024,4096]{1,0:T(8,128)(2,1)} fusion(bf16[1,4096,1024]{2,1,0:T(8,128)(2,1)} %param.8, bf16[1024,512]{1,0:T(8,128)(2,1)S(1)} %maximum_select_fusion.3, bf16[1024,512]{1,0:T(8,128)(2,1)S(1)} %collective-permute-done.11, pred[]{:T(512)S(6)} %eq.31), kind=kOutput, calls=%fused_computation.63 | convolution fusion | flops 8603566080 | bytes 18874368 | tf_op jit(solution)/shard_map/dot_general | solution.py:105
  249.7 3.6 dynamic-slice_bitcast_fusion.2
  254.1 1.3 collective-permute-start.14
  255.4 3.5 collective-permute-start.13
  258.9 113.6 %collective-permute-done.12 = bf16[256,4096]{1,0:T(8,128)(2,1)S(1)} collective-permute-done((bf16[256,4096]{1,0:T(8,128)(2,1)S(1)}, bf16[256,4096]{1,0:T(8,128)(2,1)S(1)}, u32[]{:S(2)}, u32[]{:S(2)}) %collective-permute-start.12) | collective-permute-done | bytes 2097184 | tf_op jit(solution)/shard_map/ppermute | solution.py:21
  372.5 3.0 collective-permute-start.5
  375.6 45.4 %collective-permute-done.14 = bf16[256,4096]{1,0:T(8,128)(2,1)S(1)} collective-permute-done((bf16[256,4096]{1,0:T(8,128)(2,1)S(1)}, bf16[256,4096]{1,0:T(8,128)(2,1)S(1)}, u32[]{:S(2)}, u32[]{:S(2)}) %collective-permute-start.14) | collective-permute-done | bytes 2097184 | tf_op jit(solution)/shard_map/ppermute | solution.py:21
  420.9 263.2 %collective-permute-done.13 = bf16[256,4096]{1,0:T(8,128)(2,1)S(1)} collective-permute-done((bf16[256,4096]{1,0:T(8,128)(2,1)S(1)}, bf16[256,4096]{1,0:T(8,128)(2,1)S(1)}, u32[]{:S(2)}, u32[]{:S(2)}) %collective-permute-start.13) | collective-permute-done | bytes 2097184 | tf_op jit(solution)/shard_map/ppermute | solution.py:21
  684.1 4.9 fusion.45
  689.0 3.1 collective-permute-start.16
  692.1 1.5 collective-permute-start.15
  693.6 80.6 %collective-permute-done.6 = f32[256,4096]{1,0:T(8,128)} collective-permute-done((f32[256,4096]{1,0:T(8,128)}, f32[256,4096]{1,0:T(8,128)}, u32[]{:S(2)}, u32[]{:S(2)}) %collective-permute-start.6) | collective-permute-done | bytes 4194336 | tf_op jit(solution)/shard_map/ppermute | solution.py:21
  774.2 185.3 %collective-permute-done.5 = f32[256,4096]{1,0:T(8,128)} collective-permute-done((f32[256,4096]{1,0:T(8,128)}, f32[256,4096]{1,0:T(8,128)}, u32[]{:S(2)}, u32[]{:S(2)}) %collective-permute-start.5) | collective-permute-done | bytes 4194336 | tf_op jit(solution)/shard_map/ppermute | solution.py:21
  959.5 84.3 %collective-permute-done.17 = f32[256,4096]{1,0:T(8,128)} collective-permute-done((f32[256,4096]{1,0:T(8,128)}, f32[256,4096]{1,0:T(8,128)}, u32[]{:S(2)}, u32[]{:S(2)}) %collective-permute-start.17) | collective-permute-done | bytes 4194336 | tf_op jit(solution)/shard_map/ppermute | solution.py:21
  1043.8 89.9 %collective-permute-done.16 = f32[256,4096]{1,0:T(8,128)} collective-permute-done((f32[256,4096]{1,0:T(8,128)}, f32[256,4096]{1,0:T(8,128)}, u32[]{:S(2)}, u32[]{:S(2)}) %collective-permute-start.16) | collective-permute-done | bytes 4194336 | tf_op jit(solution)/shard_map/ppermute | solution.py:21
  1133.7 5.6 collective-permute-done.15
  1139.3 35.9 %fusion.5 = (bf16[4,256,4096]{2,1,0:T(8,128)(2,1)}, f32[4,256,4096]{2,1,0:T(8,128)}, f32[4,256,4096]{2,1,0:T(8,128)}) fusion(s32[]{:T(128)S(6)} %select_n.180, f32[1,256,4096]{2,1,0:T(8,128)} %bitcast.20, f32[1,256,4096]{2,1,0:T(8,128)} %bitcast.19, f32[1,256,4096]{2,1,0:T(8,128)} %bitcast.18, f32[1,256,4096]{2,1,0:T(8,128)} %bitcast.17, ...), kind=kLoop, calls=%fused_computation.23 | loop fusion | flops 100663296 | bytes 75497472 | tf_op jit(solution)/shard_map/convert_element_type | solution.py:109
  1175.2 12.8 fusion.34
  1188.1 1.8 slice_select_fusion
  1189.9 1.2 collective-permute-start.18
  1191.1 5.4 multiply_convert_fusion
  1196.5 16.6 %fusion.29 = (bf16[1024,4096]{1,0:T(8,128)(2,1)}, bf16[1024,4096]{1,0:T(8,128)(2,1)}) fusion(f32[4,256,4096]{2,1,0:T(8,128)S(1)} %bitcast.71, f32[4,256,4096]{2,1,0:T(8,128)} %get-tuple-element.6), kind=kLoop, calls=%fused_computation.49 | loop fusion | flops 54525952 | bytes 50331648 | tf_op jit(solution)/shard_map/convert_element_type | solution.py:99
  1213.1 12.7 fusion.32
  1227.4 11.4 convert_bitcast_fusion
  1238.9 2.5 select_add_fusion
  1241.4 1.1 slice_select_fusion.2
  1243.3 38.6 %collective-permute-done.8 = f32[1024,512]{1,0:T(8,128)} collective-permute-done((f32[1024,512]{1,0:T(8,128)S(1)}, f32[1024,512]{1,0:T(8,128)}, u32[]{:S(2)}, u32[]{:S(2)}) %collective-permute-start.8) | collective-permute-done | bytes 2097184 | tf_op jit(solution)/shard_map/ppermute | solution.py:16
  1281.9 2.4 select_add_fusion.1
  1284.4 1.4 collective-permute-start.9
  1285.8 14.1 %convert_bitcast_fusion.1 = bf16[1,1024,4096]{2,1,0:T(8,128)(2,1)} fusion(bf16[1024,4096]{1,0:T(8,128)(2,1)S(1)} %bitcast.78, bf16[1024,512]{1,0:T(8,128)(2,1)} %copy-done.4, bf16[1024,512]{1,0:T(8,128)(2,1)} %copy-done.7, pred[]{:T(512)S(6)} %eq.31), kind=kOutput, calls=%fused_computation.61 | convolution fusion | flops 8603566080 | bytes 18874368 | tf_op jit(solution)/shard_map/dot_general | solution.py:115
  1299.9 1.1 add_convert_fusion
  (49 shorter events, 5.5 us)
Async XLA Ops:
  0.6 2.5 collective-permute-start
  4.6 36.1 %copy-start.4 = (bf16[1024,512]{1,0:T(8,128)(2,1)}, bf16[1024,512]{1,0:T(8,128)(2,1)S(1)}, u32[]{:S(2)}) copy-start(bf16[1024,512]{1,0:T(8,128)(2,1)S(1)} %maximum_select_fusion.2) | copy-start | bytes 3145732
  4.6 24.4 %collective-permute-start.1 = (bf16[1024,512]{1,0:T(8,128)(2,1)S(1)}, bf16[1024,512]{1,0:T(8,128)(2,1)S(1)}, u32[]{:S(2)}, u32[]{:S(2)}) collective-permute-start(bf16[1024,512]{1,0:T(8,128)(2,1)S(1)} %maximum_select_fusion.2), channel_id=1, source_target_pairs={{0,2},{1,3},{2,0},{3,1},{4,6},{5,7},{6,4},{7,5},{8,10},{9,11},{10,... | collective-permute-start | bytes 3145736 | tf_op jit(solution)/shard_map/ppermute | solution.py:16
  29.0 11.6 copy-start.7
  40.6 5.3 copy-start
  40.7 9.1 copy-start.2
  45.9 46.1 %collective-permute-start.2 = (bf16[256,4096]{1,0:T(8,128)(2,1)}, bf16[256,4096]{1,0:T(8,128)(2,1)S(1)}, u32[]{:S(2)}, u32[]{:S(2)}) collective-permute-start(bf16[256,4096]{1,0:T(8,128)(2,1)} %get-tuple-element.10), channel_id=1, source_target_pairs={{0,4},{1,5},{2,6},{3,7},{4,8},{5,9},{6,10},{7,11},{8,12},{9,13},{1... | collective-permute-start | bytes 6291464 | tf_op jit(solution)/shard_map/ppermute | solution.py:21
  47.2 93.6 %collective-permute-start.4 = (bf16[256,4096]{1,0:T(8,128)(2,1)}, bf16[256,4096]{1,0:T(8,128)(2,1)}, u32[]{:S(2)}, u32[]{:S(2)}) collective-permute-start(bf16[256,4096]{1,0:T(8,128)(2,1)} %get-tuple-element.11), channel_id=1, source_target_pairs={{0,12},{1,13},{2,14},{3,15},{4,0},{5,1},{6,2},{7,3},{8,4},{9,5},{1... | collective-permute-start | bytes 6291464 | tf_op jit(solution)/shard_map/ppermute | solution.py:21
  47.4 178.7 %collective-permute-start.3 = (bf16[256,4096]{1,0:T(8,128)(2,1)}, bf16[256,4096]{1,0:T(8,128)(2,1)}, u32[]{:S(2)}, u32[]{:S(2)}) collective-permute-start(bf16[256,4096]{1,0:T(8,128)(2,1)} %get-tuple-element.12), channel_id=1, source_target_pairs={{0,8},{1,9},{2,10},{3,11},{4,12},{5,13},{6,14},{7,15},{8,0},{9,1},... | collective-permute-start | bytes 6291464 | tf_op jit(solution)/shard_map/ppermute | solution.py:21
  49.7 3.6 collective-permute-start.10
  53.5 181.4 %copy-start.5 = (bf16[1024,512]{1,0:T(8,128)(2,1)}, bf16[1024,512]{1,0:T(8,128)(2,1)S(1)}, u32[]{:S(2)}) copy-start(bf16[1024,512]{1,0:T(8,128)(2,1)S(1)} %maximum_select_fusion.3) | copy-start | bytes 3145732
  53.5 181.4 %collective-permute-start.11 = (bf16[1024,512]{1,0:T(8,128)(2,1)S(1)}, bf16[1024,512]{1,0:T(8,128)(2,1)S(1)}, u32[]{:S(2)}, u32[]{:S(2)}) collective-permute-start(bf16[1024,512]{1,0:T(8,128)(2,1)S(1)} %maximum_select_fusion.3), channel_id=1, source_target_pairs={{0,2},{1,3},{2,0},{3,1},{4,6},{5,7},{6,4},{7,5},{8,10},{9,11},{10,... | collective-permute-start | bytes 3145736 | tf_op jit(solution)/shard_map/ppermute | solution.py:16
  232.3 459.8 %collective-permute-start.7 = (f32[256,4096]{1,0:T(8,128)}, f32[256,4096]{1,0:T(8,128)}, u32[]{:S(2)}, u32[]{:S(2)}) collective-permute-start(f32[256,4096]{1,0:T(8,128)} %fusion.47), channel_id=1, source_target_pairs={{0,4},{1,5},{2,6},{3,7},{4,8},{5,9},{6,10},{7,11},{8,12},{9,13},{1... | collective-permute-start | bytes 12582920 | tf_op jit(solution)/shard_map/ppermute | solution.py:21
  235.0 14.8 %copy-start.8 = (bf16[1024,512]{1,0:T(8,128)(2,1)}, bf16[1024,512]{1,0:T(8,128)(2,1)S(1)}, u32[]{:S(2)}) copy-start(bf16[1024,512]{1,0:T(8,128)(2,1)S(1)} %collective-permute-done.11) | copy-start | bytes 3145732
  253.4 119.1 %collective-permute-start.12 = (bf16[256,4096]{1,0:T(8,128)(2,1)S(1)}, bf16[256,4096]{1,0:T(8,128)(2,1)S(1)}, u32[]{:S(2)}, u32[]{:S(2)}) collective-permute-start(bf16[256,4096]{1,0:T(8,128)(2,1)S(1)} %get-tuple-element.13), channel_id=1, source_target_pairs={{0,4},{1,5},{2,6},{3,7},{4,8},{5,9},{6,10},{7,11},{8,12},{9,13},{1... | collective-permute-start | bytes 6291464 | tf_op jit(solution)/shard_map/ppermute | solution.py:21
  254.1 166.8 %collective-permute-start.14 = (bf16[256,4096]{1,0:T(8,128)(2,1)S(1)}, bf16[256,4096]{1,0:T(8,128)(2,1)S(1)}, u32[]{:S(2)}, u32[]{:S(2)}) collective-permute-start(bf16[256,4096]{1,0:T(8,128)(2,1)S(1)} %get-tuple-element.14), channel_id=1, source_target_pairs={{0,12},{1,13},{2,14},{3,15},{4,0},{5,1},{6,2},{7,3},{8,4},{9,5},{1... | collective-permute-start | bytes 6291464 | tf_op jit(solution)/shard_map/ppermute | solution.py:21
  255.4 428.7 %collective-permute-start.13 = (bf16[256,4096]{1,0:T(8,128)(2,1)S(1)}, bf16[256,4096]{1,0:T(8,128)(2,1)S(1)}, u32[]{:S(2)}, u32[]{:S(2)}) collective-permute-start(bf16[256,4096]{1,0:T(8,128)(2,1)S(1)} %get-tuple-element.15), channel_id=1, source_target_pairs={{0,8},{1,9},{2,10},{3,11},{4,12},{5,13},{6,14},{7,15},{8,0},{9,1},... | collective-permute-start | bytes 6291464 | tf_op jit(solution)/shard_map/ppermute | solution.py:21
  258.9 515.3 %collective-permute-start.6 = (f32[256,4096]{1,0:T(8,128)}, f32[256,4096]{1,0:T(8,128)}, u32[]{:S(2)}, u32[]{:S(2)}) collective-permute-start(f32[256,4096]{1,0:T(8,128)} %fusion.47), channel_id=1, source_target_pairs={{0,8},{1,9},{2,10},{3,11},{4,12},{5,13},{6,14},{7,15},{8,0},{9,1},... | collective-permute-start | bytes 12582920 | tf_op jit(solution)/shard_map/ppermute | solution.py:21
  372.5 587.0 %collective-permute-start.5 = (f32[256,4096]{1,0:T(8,128)}, f32[256,4096]{1,0:T(8,128)}, u32[]{:S(2)}, u32[]{:S(2)}) collective-permute-start(f32[256,4096]{1,0:T(8,128)} %fusion.47), channel_id=1, source_target_pairs={{0,12},{1,13},{2,14},{3,15},{4,0},{5,1},{6,2},{7,3},{8,4},{9,5},{1... | collective-permute-start | bytes 12582920 | tf_op jit(solution)/shard_map/ppermute | solution.py:21
  689.0 354.8 %collective-permute-start.17 = (f32[256,4096]{1,0:T(8,128)}, f32[256,4096]{1,0:T(8,128)}, u32[]{:S(2)}, u32[]{:S(2)}) collective-permute-start(f32[256,4096]{1,0:T(8,128)} %fusion.45), channel_id=1, source_target_pairs={{0,4},{1,5},{2,6},{3,7},{4,8},{5,9},{6,10},{7,11},{8,12},{9,13},{1... | collective-permute-start | bytes 12582920 | tf_op jit(solution)/shard_map/ppermute | solution.py:21
  689.0 444.7 %collective-permute-start.16 = (f32[256,4096]{1,0:T(8,128)}, f32[256,4096]{1,0:T(8,128)}, u32[]{:S(2)}, u32[]{:S(2)}) collective-permute-start(f32[256,4096]{1,0:T(8,128)} %fusion.45), channel_id=1, source_target_pairs={{0,8},{1,9},{2,10},{3,11},{4,12},{5,13},{6,14},{7,15},{8,0},{9,1},... | collective-permute-start | bytes 12582920 | tf_op jit(solution)/shard_map/ppermute | solution.py:21
  692.1 447.2 %collective-permute-start.15 = (f32[256,4096]{1,0:T(8,128)}, f32[256,4096]{1,0:T(8,128)}, u32[]{:S(2)}, u32[]{:S(2)}) collective-permute-start(f32[256,4096]{1,0:T(8,128)} %fusion.45), channel_id=1, source_target_pairs={{0,12},{1,13},{2,14},{3,15},{4,0},{5,1},{6,2},{7,3},{8,4},{9,5},{1... | collective-permute-start | bytes 12582920 | tf_op jit(solution)/shard_map/ppermute | solution.py:21
  1175.2 15.9 %slice-start = ((s8[16777216]{0:T(1024)(128)(4,1)}), s8[4194304]{0:T(1024)(128)(4,1)S(1)}, s32[]{:S(2)}) async-start(s8[16777216]{0:T(1024)(128)(4,1)} %bitcast.70), calls=%async_computation | async-start | bytes 8388608
  1175.2 15.9 %slice-start.1 = ((s8[16777216]{0:T(1024)(128)(4,1)}), s8[4194304]{0:T(1024)(128)(4,1)S(1)}, s32[]{:S(2)}) async-start(s8[16777216]{0:T(1024)(128)(4,1)} %bitcast.70), calls=%async_computation.1 | async-start | bytes 8388608
  1175.2 15.9 %slice-start.2 = ((s8[16777216]{0:T(1024)(128)(4,1)}), s8[4194304]{0:T(1024)(128)(4,1)S(1)}, s32[]{:S(2)}) async-start(s8[16777216]{0:T(1024)(128)(4,1)} %bitcast.70), calls=%async_computation.2 | async-start | bytes 8388608
  1175.2 15.9 %slice-start.3 = ((s8[16777216]{0:T(1024)(128)(4,1)}), s8[4194304]{0:T(1024)(128)(4,1)S(1)}, s32[]{:S(2)}) async-start(s8[16777216]{0:T(1024)(128)(4,1)} %bitcast.70), calls=%async_computation.3 | async-start | bytes 8388608
  1189.9 48.9 %collective-permute-start.18 = (f32[1024,512]{1,0:T(8,128)}, f32[1024,512]{1,0:T(8,128)}, u32[]{:S(2)}, u32[]{:S(2)}) collective-permute-start(f32[1024,512]{1,0:T(8,128)} %slice_select_fusion), channel_id=1, source_target_pairs={{0,2},{1,3},{2,0},{3,1},{4,6},{5,7},{6,4},{7,5},{8,10},{9,11},{10,... | collective-permute-start | bytes 6291464 | tf_op jit(solution)/shard_map/ppermute | solution.py:16
  1213.1 13.6 %copy-start.1 = (bf16[1024,4096]{1,0:T(8,128)(2,1)S(1)}, bf16[1024,4096]{1,0:T(8,128)(2,1)}, u32[]{:S(2)}) copy-start(bf16[1024,4096]{1,0:T(8,128)(2,1)} %get-tuple-element.8) | copy-start | bytes 25165828
  1225.9 1.2 copy-start.6
  1225.9 1.5 copy-start.9
  1226.4 55.5 %collective-permute-start.8 = (f32[1024,512]{1,0:T(8,128)S(1)}, f32[1024,512]{1,0:T(8,128)}, u32[]{:S(2)}, u32[]{:S(2)}) collective-permute-start(f32[1024,512]{1,0:T(8,128)S(1)} %slice_select_fusion.1), channel_id=1, source_target_pairs={{0,2},{1,3},{2,0},{3,1},{4,6},{5,7},{6,4},{7,5},{8,10},{9,11},{10,... | collective-permute-start | bytes 6291464 | tf_op jit(solution)/shard_map/ppermute | solution.py:16
  1238.9 46.9 %slice-start.4 = ((s8[8388608]{0:T(1024)(128)(4,1)}), s8[4194304]{0:T(1024)(128)(4,1)S(1)}, s32[]{:S(2)}) async-start(s8[8388608]{0:T(1024)(128)(4,1)} %bitcast.77), calls=%async_computation.4 | async-start | bytes 8388608
  1242.5 43.3 %slice-start.5 = ((s8[8388608]{0:T(1024)(128)(4,1)}), s8[4194304]{0:T(1024)(128)(4,1)S(1)}, s32[]{:S(2)}) async-start(s8[8388608]{0:T(1024)(128)(4,1)} %bitcast.77), calls=%async_computation.5 | async-start | bytes 8388608
  1242.5 57.4 %collective-permute-start.19 = (f32[1024,256]{1,0:T(8,128)}, f32[1024,256]{1,0:T(8,128)S(1)}, u32[]{:S(2)}, u32[]{:S(2)}) collective-permute-start(f32[1024,256]{1,0:T(8,128)} %slice_select_fusion.2), channel_id=1, source_target_pairs={{0,1},{1,0},{2,3},{3,2},{4,5},{5,4},{6,7},{7,6},{8,9},{9,8},{10,11... | collective-permute-start | bytes 3145736 | tf_op jit(solution)/shard_map/ppermute | solution.py:16
  1284.4 16.7 %collective-permute-start.9 = (f32[1024,256]{1,0:T(8,128)S(1)}, f32[1024,256]{1,0:T(8,128)S(1)}, u32[]{:S(2)}, u32[]{:S(2)}) collective-permute-start(f32[1024,256]{1,0:T(8,128)S(1)} %slice_select_fusion.3), channel_id=1, source_target_pairs={{0,1},{1,0},{2,3},{3,2},{4,5},{5,4},{6,7},{7,6},{8,9},{9,8},{10,11... | collective-permute-start | bytes 3145736 | tf_op jit(solution)/shard_map/ppermute | solution.py:16
  1299.9 1.1 copy-start.3
where the time goes:
time: 1300 us
  waiting for transfers between devices  1100 us (85%)
  other arithmetic  81.2 us (6%)
  matrix products  77.5 us (6%)
  starting transfers between devices  28.7 us (2%)
    ppermute x12, waiting for transfers between devices, passed_along(): lax.ppermute(shard, axis, [(i, (i + by) % count) for i in range(count)])  1040 us
    ppermute x8, waiting for transfers between devices, from_partner(): return lax.ppermute(value, axis, pairs)  65 us
    convert_element_type x1, other arithmetic, on_device(): (cycle_join_sums(act_grad, cycle_pos, row_width) * gelu_slope(preact_all)...  35.9 us
  transfers between devices with their start and end apart: 20, of which 15 were waited for; matrix products, arithmetic and copies ran while one was open for 8% of the time, Pallas kernels for 0%

commit v1 on v0

v1 whole, which is shorter than its diff:
```python
import jax
import jax.numpy as jnp
import numpy as np
from jax import lax
from jax.sharding import Mesh
from jax.sharding import PartitionSpec as P


root_half = 0.7071067811865476
inv_root_tau = 0.3989422804014327


def gelu_value(values):
    return 0.5 * values * (1.0 + lax.erf(values * root_half))


def gelu_slope(values):
    return (
        0.5 * (1.0 + lax.erf(values * root_half))
        + values * jnp.exp(-0.5 * values * values) * inv_root_tau
    )


def cycle_reduce(terms):
    count = lax.axis_size("r")
    pos = lax.axis_index("r")
    block_rows = terms.shape[0] // count
    shares = terms.reshape(count, block_rows, terms.shape[1])
    summed = lax.dynamic_index_in_dim(shares, pos, 0, keepdims=False).astype(jnp.float32)
    for distance in range(1, count):
        outgoing = lax.dynamic_index_in_dim(shares, (pos + distance) % count, 0, keepdims=False)
        incoming = lax.ppermute(
            outgoing, "r", [(i, (i + distance) % count) for i in range(count)]
        )
        summed = summed + incoming.astype(jnp.float32)
    return summed


def on_device(hidden_in, w_up, w_down, out_grad):
    up_tile = w_up[0]
    down_tile = w_down[0]
    x_rows = lax.all_gather(hidden_in, "p", axis=1, tiled=True)
    up_terms = jnp.dot(x_rows, up_tile, preferred_element_type=jnp.float32).astype(jnp.bfloat16)
    preact = cycle_reduce(up_terms)
    activation = lax.all_gather(gelu_value(preact).astype(jnp.bfloat16), "r", axis=0, tiled=True)
    out_part = jnp.dot(activation, down_tile, preferred_element_type=jnp.float32)
    block_out = (
        hidden_in.astype(jnp.float32)
        + lax.psum_scatter(out_part, "p", scatter_dimension=1, tiled=True)
    ).astype(jnp.bfloat16)

    grad_rows = lax.all_gather(out_grad, "p", axis=1, tiled=True)
    grad_terms = lax.dot_general(
        grad_rows, down_tile, (((1,), (1,)), ((), ())), preferred_element_type=jnp.float32
    ).astype(jnp.bfloat16)
    act_grad = cycle_reduce(grad_terms)
    pre_grad = lax.all_gather(
        (act_grad * gelu_slope(preact)).astype(jnp.bfloat16), "r", axis=0, tiled=True
    )
    grad_down = lax.dot_general(
        activation, grad_rows, (((0,), (0,)), ((), ())), preferred_element_type=jnp.float32
    ).astype(jnp.bfloat16)
    grad_up = lax.dot_general(
        x_rows, pre_grad, (((0,), (0,)), ((), ())), preferred_element_type=jnp.float32
    ).astype(jnp.bfloat16)
    back_part = lax.dot_general(
        pre_grad, up_tile, (((1,), (1,)), ((), ())), preferred_element_type=jnp.float32
    )
    input_grad = (
        out_grad.astype(jnp.float32)
        + lax.psum_scatter(back_part, "p", scatter_dimension=1, tiled=True)
    ).astype(jnp.bfloat16)
    return (block_out, input_grad, grad_up[None], grad_down[None])


def solution(mesh):
    groups = mesh.shape["groups"]
    tile = mesh.shape["tile"]

    def run(hidden_in, w_up, w_down, out_grad):
        width_blocks = hidden_in.shape[1] // w_up.shape[1]
        grid = Mesh(
            np.asarray(mesh.devices).reshape(groups, width_blocks, tile // width_blocks),
            ("groups", "r", "p"),
        )
        cells = ("r", "p")
        return jax.shard_map(
            on_device,
            mesh=grid,
            in_specs=(
                P("groups", cells),
                P(cells, None, None),
                P(cells, None, None),
                P("groups", cells),
            ),
            out_specs=(
                P("groups", cells),
                P("groups", cells),
                P(cells, "groups", None),
                P(cells, "groups", None),
            ),
            check_vma=False,
        )(hidden_in, w_up, w_down, out_grad)

    return run
```

time: 1300 us -> 825 us (0.63)
  the two profiles are of different devices: /device:TPU:9 before, /device:TPU:0 now
where the time goes in v1:
time: 825 us
  waiting for transfers between devices  589 us (71%)
  starting transfers between devices  99.1 us (12%)
  matrix products  85.9 us (10%)
  local copies, waits for them, and re-layouts  24.2 us (3%)
  between operations  14.2 us (2%)
  other arithmetic  12.9 us (2%)
    ppermute x6, waiting for transfers between devices, cycle_reduce(): lax.ppermute(outgoing, 'r', [(i, (i + distance) % count) for i in range(c...  246 us
    all_gather x1, waiting for transfers between devices, on_device(): lax.all_gather(gelu_value(preact).astype(jnp.bfloat16), 'r', axis=0, tile...  147 us
    all_gather x1, waiting for transfers between devices, on_device(): lax.all_gather((act_grad * gelu_slope(preact)).astype(jnp.bfloat16), 'r',...  134 us
    ppermute x6, starting transfers between devices, cycle_reduce(): lax.ppermute(outgoing, 'r', [(i, (i + distance) % count) for i in range(c...  98.7 us
    reduce_scatter x1, waiting for transfers between devices, on_device(): lax.psum_scatter(back_part, 'p', scatter_dimension=1, tiled=True)  31.2 us
    all_gather x1, waiting for transfers between devices, on_device(): grad_rows = lax.all_gather(out_grad, 'p', axis=1, tiled=True)  26.4 us
    unnamed x13, local copies, waits for them, and re-layouts  18 us
  transfers between devices with their start and end apart: 12, of which 8 were waited for; matrix products, arithmetic and copies ran while one was open for 13% of the time, Pallas kernels for 0%

profile of v1, /device:TPU:0, one launch (start us, length us, event | category | flops | bytes accessed | tf_op | source)
XLA Modules:
  0.0 824.9 jit_solution(5665044001988717116)
XLA Ops:
  7.2 0.0 all-gather.9.cloned.1.call-start
  7.2 0.7 all-gather.9.cloned.1.call-update
  7.9 0.0 all-gather.5.cloned.1.call-start
  7.9 0.7 all-gather.5.cloned.1.call-update
  8.6 0.0 all-gather.7.cloned.1.call-start
  8.7 26.4 %all-gather.9.cloned.1.call-done = bf16[1024,1024]{1,0:T(8,128)(2,1)} async-done(((bf16[1024,256]{1,0:T(8,128)(2,1)}), bf16[1024,1024]{1,0:T(8,128)(2,1)}) %all-gather.9.cloned.1.call-update) | async-done | bytes 2097168 | tf_op jit(solution)/shard_map/all_gather | solution.py:52
  35.1 12.8 %fusion.11 = bf16[1024,4096]{1,0:T(8,128)(2,1)S(1)} fusion(bf16[1024,1024]{1,0:T(8,128)(2,1)} %all-gather.9.cloned.1.call-done, bf16[1,4096,1024]{2,1,0:T(8,128)(2,1)} %param.6), kind=kOutput, calls=%fused_computation.11 | convolution fusion | flops 8594128896 | bytes 18874368 | tf_op jit(solution)/shard_map/dot_general | solution.py:53
  48.0 0.0 copy-start
  48.0 3.1 dynamic-slice_bitcast_fusion.2
  51.1 2.2 copy-done
  53.2 1.5 collective-permute-start.3
  54.7 2.3 collective-permute-start.5
  57.1 0.6 collective-permute-start.4
  57.7 1.9 all-gather.5.cloned.1.call-done
  59.6 12.8 %fusion.8 = bf16[1024,4096]{1,0:T(8,128)(2,1)S(1)} fusion(bf16[1024,1024]{1,0:T(8,128)(2,1)} %all-gather.5.cloned.1.call-done, bf16[1,1024,4096]{2,1,0:T(8,128)(2,1)} %param.5), kind=kOutput, calls=%fused_computation.10 | convolution fusion | flops 8594128896 | bytes 18874368 | tf_op jit(solution)/shard_map/dot_general | solution.py:43
  72.3 0.0 copy-start.1
  72.3 3.1 dynamic-slice_bitcast_fusion.5
  75.4 2.2 copy-done.1
  77.6 1.5 collective-permute-start
  79.1 2.3 collective-permute-start.2
  81.4 22.3 %collective-permute-done.3 = bf16[256,4096]{1,0:T(8,128)(2,1)S(1)} collective-permute-done((bf16[256,4096]{1,0:T(8,128)(2,1)}, bf16[256,4096]{1,0:T(8,128)(2,1)S(1)}, u32[]{:S(2)}, u32[]{:S(2)}) %collective-permute-start.3) | collective-permute-done | bytes 2097184 | tf_op jit(solution)/shard_map/ppermute | solution.py:32
  103.8 90.4 %collective-permute-start.1 = (bf16[256,4096]{1,0:T(8,128)(2,1)}, bf16[256,4096]{1,0:T(8,128)(2,1)}, u32[]{:S(2)}, u32[]{:S(2)}) collective-permute-start(bf16[256,4096]{1,0:T(8,128)(2,1)} %get-tuple-element.15), channel_id=1, source_target_pairs={{0,8},{4,12},{8,0},{12,4},{1,9},{5,13},{9,1},{13,5},{2,10},{6,14},... | collective-permute-start | bytes 6291464 | tf_op jit(solution)/shard_map/ppermute | solution.py:32
  194.2 0.0 collective-permute-done.5
  194.2 89.5 %collective-permute-done.4 = bf16[256,4096]{1,0:T(8,128)(2,1)} collective-permute-done((bf16[256,4096]{1,0:T(8,128)(2,1)}, bf16[256,4096]{1,0:T(8,128)(2,1)}, u32[]{:S(2)}, u32[]{:S(2)}) %collective-permute-start.4) | collective-permute-done | bytes 2097184 | tf_op jit(solution)/shard_map/ppermute | solution.py:32
  283.7 0.0 collective-permute-done
  283.7 0.0 collective-permute-done.2
  283.7 134.1 %collective-permute-done.1 = bf16[256,4096]{1,0:T(8,128)(2,1)} collective-permute-done((bf16[256,4096]{1,0:T(8,128)(2,1)}, bf16[256,4096]{1,0:T(8,128)(2,1)}, u32[]{:S(2)}, u32[]{:S(2)}) %collective-permute-start.1) | collective-permute-done | bytes 2097184 | tf_op jit(solution)/shard_map/ppermute | solution.py:32
  417.7 8.6 %fusion.19 = (bf16[256,4096]{1,0:T(8,128)(2,1)}, bf16[256,4096]{1,0:T(8,128)(2,1)}) fusion(bf16[256,4096]{1,0:T(8,128)(2,1)} %collective-permute-done.5, bf16[256,4096]{1,0:T(8,128)(2,1)} %collective-permute-done.4, bf16[256,4096]{1,0:T(8,128)(2,1)S(1)} %collective-permute-done.3, bf16[4,256,4096]{2,1,0:T(8,128)(2,1)} %bitcast.53, s32[]{:T(128)S(6)} %select_n.38, ...), kind=kLoop, calls=%fused_computation.18 | loop fusion | flops 28311552 | bytes 20971524 | tf_op jit(solution)/shard_map/convert_element_type | solution.py:58
  426.3 0.0 all-gather.7.cloned.1.call-update
  426.4 0.0 all-gather.11.cloned.1.call-start
  426.4 0.5 all-gather.11.cloned.1.call-update
  426.9 0.2 reduce-scatter.3.cloned.1.call-start
  427.2 147.2 %all-gather.7.cloned.1.call-done = bf16[1024,4096]{1,0:T(8,128)(2,1)} async-done(((bf16[256,4096]{1,0:T(8,128)(2,1)}), bf16[1024,4096]{1,0:T(8,128)(2,1)}) %all-gather.7.cloned.1.call-update) | async-done | bytes 8388624 | tf_op jit(solution)/shard_map/all_gather | solution.py:45
  574.3 15.0 %fusion.2 = f32[1024,1024]{1,0:T(8,128)} fusion(bf16[1024,4096]{1,0:T(8,128)(2,1)} %all-gather.7.cloned.1.call-done, bf16[1,4096,1024]{2,1,0:T(8,128)(2,1)} %param.6), kind=kOutput, calls=%fused_computation.2 | convolution fusion | flops 8589934592 | bytes 20971520 | tf_op jit(solution)/shard_map/dot_general | solution.py:46
  589.4 0.0 reduce-scatter.3.cloned.1.call-update
  589.4 0.0 reduce-scatter.5.cloned.1.call-start
  589.5 134.2 %all-gather.11.cloned.1.call-done = bf16[1024,4096]{1,0:T(8,128)(2,1)} async-done(((bf16[256,4096]{1,0:T(8,128)(2,1)}), bf16[1024,4096]{1,0:T(8,128)(2,1)}) %all-gather.11.cloned.1.call-update) | async-done | bytes 8388624 | tf_op jit(solution)/shard_map/all_gather | solution.py:57
  723.7 15.1 %fusion.4 = f32[1024,1024]{1,0:T(8,128)} fusion(bf16[1024,4096]{1,0:T(8,128)(2,1)} %all-gather.11.cloned.1.call-done, bf16[1,1024,4096]{2,1,0:T(8,128)(2,1)} %param.5), kind=kOutput, calls=%fused_computation.4 | convolution fusion | flops 8589934592 | bytes 20971520 | tf_op jit(solution)/shard_map/dot_general | solution.py:66
  738.8 0.0 reduce-scatter.5.cloned.1.call-update
  738.8 1.6 copy-done.5
  740.3 15.2 %convert_bitcast_fusion.1 = bf16[1,1024,4096]{1,2,0:T(8,128)(2,1)} fusion(bf16[1024,4096]{1,0:T(8,128)(2,1)} %all-gather.11.cloned.1.call-done, bf16[1024,1024]{1,0:T(8,128)(2,1)S(1)} %copy-done.5), kind=kOutput, calls=%fused_computation.9 | convolution fusion | flops 8594128896 | bytes 18874368 | tf_op jit(solution)/shard_map/dot_general | solution.py:63
  755.6 12.1 %copy.8 = bf16[1,1024,4096]{2,1,0:T(8,128)(2,1)} copy(bf16[1,1024,4096]{1,2,0:T(8,128)(2,1)} %convert_bitcast_fusion.1) | data formatting | bytes 16777216
  767.6 15.0 %convert_bitcast_fusion = bf16[1,4096,1024]{2,1,0:T(8,128)(2,1)} fusion(bf16[1024,4096]{1,0:T(8,128)(2,1)} %all-gather.7.cloned.1.call-done, bf16[1024,1024]{1,0:T(8,128)(2,1)S(1)} %copy-done.4), kind=kOutput, calls=%fused_computation.8 | convolution fusion | flops 8594128896 | bytes 18874368 | tf_op jit(solution)/shard_map/dot_general | solution.py:60
  782.6 0.0 copy-done.2
  782.6 2.1 add_convert_fusion.1
  784.7 31.2 %reduce-scatter.5.cloned.1.call-done = f32[1024,256]{1,0:T(8,128)} async-done(((f32[1024,1024]{1,0:T(8,128)}), f32[1024,256]{1,0:T(8,128)}) %reduce-scatter.5.cloned.1.call-update) | async-done | bytes 1048592 | tf_op jit(solution)/shard_map/reduce_scatter | solution.py:71
  815.9 0.0 copy-done.3
  815.9 2.1 add_convert_fusion
  (6 shorter events, 0.0 us)
Async XLA Ops:
  7.2 28.0 %all-gather.9.cloned.1.call-start = ((), (), s32[]{:S(2)}) async-start(), calls=%async_computation.5 | async-start | bytes 2621440 | tf_op jit(solution)/shard_map/all_gather | solution.py:52
  7.9 51.7 %all-gather.5.cloned.1.call-start = ((), (), s32[]{:S(2)}) async-start(), calls=%async_computation.2 | async-start | bytes 2621440 | tf_op jit(solution)/shard_map/all_gather | solution.py:42
  8.6 565.7 %all-gather.7.cloned.1.call-start = ((), (), s32[]{:S(2)}) async-start(), calls=%async_computation.3 | async-start | bytes 10485760 | tf_op jit(solution)/shard_map/all_gather | solution.py:45
  48.0 5.3 copy-start
  53.2 50.5 %collective-permute-start.3 = (bf16[256,4096]{1,0:T(8,128)(2,1)}, bf16[256,4096]{1,0:T(8,128)(2,1)S(1)}, u32[]{:S(2)}, u32[]{:S(2)}) collective-permute-start(bf16[256,4096]{1,0:T(8,128)(2,1)} %get-tuple-element.10), channel_id=1, source_target_pairs={{0,4},{4,8},{8,12},{12,0},{1,5},{5,9},{9,13},{13,1},{2,6},{6,10},{... | collective-permute-start | bytes 6291464 | tf_op jit(solution)/shard_map/ppermute | solution.py:32
  54.7 139.4 %collective-permute-start.5 = (bf16[256,4096]{1,0:T(8,128)(2,1)}, bf16[256,4096]{1,0:T(8,128)(2,1)}, u32[]{:S(2)}, u32[]{:S(2)}) collective-permute-start(bf16[256,4096]{1,0:T(8,128)(2,1)} %get-tuple-element.11), channel_id=1, source_target_pairs={{0,12},{4,0},{8,4},{12,8},{1,13},{5,1},{9,5},{13,9},{2,14},{6,2},{... | collective-permute-start | bytes 6291464 | tf_op jit(solution)/shard_map/ppermute | solution.py:32
  57.1 226.6 %collective-permute-start.4 = (bf16[256,4096]{1,0:T(8,128)(2,1)}, bf16[256,4096]{1,0:T(8,128)(2,1)}, u32[]{:S(2)}, u32[]{:S(2)}) collective-permute-start(bf16[256,4096]{1,0:T(8,128)(2,1)} %get-tuple-element.12), channel_id=1, source_target_pairs={{0,8},{4,12},{8,0},{12,4},{1,9},{5,13},{9,1},{13,5},{2,10},{6,14},... | collective-permute-start | bytes 6291464 | tf_op jit(solution)/shard_map/ppermute | solution.py:32
  72.3 5.3 copy-start.1
  77.6 206.1 %collective-permute-start = (bf16[256,4096]{1,0:T(8,128)(2,1)}, bf16[256,4096]{1,0:T(8,128)(2,1)}, u32[]{:S(2)}, u32[]{:S(2)}) collective-permute-start(bf16[256,4096]{1,0:T(8,128)(2,1)} %get-tuple-element.13), channel_id=1, source_target_pairs={{0,4},{4,8},{8,12},{12,0},{1,5},{5,9},{9,13},{13,1},{2,6},{6,10},{... | collective-permute-start | bytes 6291464 | tf_op jit(solution)/shard_map/ppermute | solution.py:32
  79.1 204.6 %collective-permute-start.2 = (bf16[256,4096]{1,0:T(8,128)(2,1)}, bf16[256,4096]{1,0:T(8,128)(2,1)}, u32[]{:S(2)}, u32[]{:S(2)}) collective-permute-start(bf16[256,4096]{1,0:T(8,128)(2,1)} %get-tuple-element.14), channel_id=1, source_target_pairs={{0,12},{4,0},{8,4},{12,8},{1,13},{5,1},{9,5},{13,9},{2,14},{6,2},{... | collective-permute-start | bytes 6291464 | tf_op jit(solution)/shard_map/ppermute | solution.py:32
  103.8 314.0 %collective-permute-start.1 = (bf16[256,4096]{1,0:T(8,128)(2,1)}, bf16[256,4096]{1,0:T(8,128)(2,1)}, u32[]{:S(2)}, u32[]{:S(2)}) collective-permute-start(bf16[256,4096]{1,0:T(8,128)(2,1)} %get-tuple-element.15), channel_id=1, source_target_pairs={{0,8},{4,12},{8,0},{12,4},{1,9},{5,13},{9,1},{13,5},{2,10},{6,14},... | collective-permute-start | bytes 6291464 | tf_op jit(solution)/shard_map/ppermute | solution.py:32
  426.4 297.3 %all-gather.11.cloned.1.call-start = ((), (), s32[]{:S(2)}) async-start(), calls=%async_computation.6 | async-start | bytes 10485760 | tf_op jit(solution)/shard_map/all_gather | solution.py:57
  426.9 355.6 %reduce-scatter.3.cloned.1.call-start = ((), (), s32[]{:S(2)}) async-start(), calls=%async_computation.4 | async-start | bytes 5242880 | tf_op jit(solution)/shard_map/reduce_scatter | solution.py:49
  589.4 226.5 %reduce-scatter.5.cloned.1.call-start = ((), (), s32[]{:S(2)}) async-start(), calls=%async_computation.7 | async-start | bytes 5242880 | tf_op jit(solution)/shard_map/reduce_scatter | solution.py:71
  738.7 1.6 copy-start.5
  755.6 12.1 %copy-start.4 = (bf16[1024,1024]{1,0:T(8,128)(2,1)S(1)}, bf16[1024,1024]{1,0:T(8,128)(2,1)}, u32[]{:S(2)}) copy-start(bf16[1024,1024]{1,0:T(8,128)(2,1)} %all-gather.9.cloned.1.call-done) | copy-start | bytes 6291460
  767.6 15.0 %copy-start.2 = (bf16[1024,256]{1,0:T(8,128)(2,1)S(1)}, bf16[1024,256]{1,0:T(8,128)(2,1)}, u32[]{:S(2)}) copy-start(bf16[1024,256]{1,0:T(8,128)(2,1)} %param.4) | copy-start | bytes 1572868
  767.6 48.3 %copy-start.3 = (bf16[1024,256]{1,0:T(8,128)(2,1)S(1)}, bf16[1024,256]{1,0:T(8,128)(2,1)}, u32[]{:S(2)}) copy-start(bf16[1024,256]{1,0:T(8,128)(2,1)} %param.7) | copy-start | bytes 1572868
Sparse Core Ops, SparseCore 0:
  9.6 25.5 all-gather.8
  36.7 22.8 all-gather.4
  426.5 147.8 all-gather.6
  575.8 147.8 all-gather.10
  726.0 42.7 reduce-scatter.2
  771.4 44.5 reduce-scatter.4

commit v2 on v1

--- a/solution.py
+++ b/solution.py
@@ -21,19 +21,50 @@
     )
 
 
-def cycle_reduce(terms):
+def line_reduce(terms):
     count = lax.axis_size("r")
     pos = lax.axis_index("r")
     block_rows = terms.shape[0] // count
     shares = terms.reshape(count, block_rows, terms.shape[1])
-    summed = lax.dynamic_index_in_dim(shares, pos, 0, keepdims=False).astype(jnp.float32)
-    for distance in range(1, count):
-        outgoing = lax.dynamic_index_in_dim(shares, (pos + distance) % count, 0, keepdims=False)
-        incoming = lax.ppermute(
-            outgoing, "r", [(i, (i + distance) % count) for i in range(count)]
+    up_in = jnp.zeros((block_rows, terms.shape[1]), jnp.float32)
+    down_in = jnp.zeros((block_rows, terms.shape[1]), jnp.float32)
+    for step in range(count - 1):
+        up_block = jnp.clip(count - 1 - step + pos, 0, count - 1)
+        up_out = (up_in + lax.dynamic_index_in_dim(shares, up_block, 0, keepdims=False)).astype(
+            jnp.bfloat16
         )
-        summed = summed + incoming.astype(jnp.float32)
-    return summed
+        down_block = jnp.clip(pos + step - (count - 1), 0, count - 1)
+        down_out = (
+            down_in + lax.dynamic_index_in_dim(shares, down_block, 0, keepdims=False)
+        ).astype(jnp.bfloat16)
+        up_in = lax.ppermute(
+            up_out, "r", [(i, i + 1) for i in range(0, step + 1)]
+        ).astype(jnp.float32)
+        down_in = lax.ppermute(
+            down_out, "r", [(i, i - 1) for i in range(count - 1 - step, count)]
+        ).astype(jnp.float32)
+    own = lax.dynamic_index_in_dim(shares, pos, 0, keepdims=False).astype(jnp.float32)
+    return up_in + own + down_in
+
+
+def line_gather(block):
+    count = lax.axis_size("r")
+    pos = lax.axis_index("r")
+    ups, downs = [], []
+    up_out = down_out = block
+    for step in range(count - 1):
+        up_out = lax.ppermute(up_out, "r", [(i, i + 1) for i in range(step, count - 1)])
+        down_out = lax.ppermute(down_out, "r", [(i, i - 1) for i in range(1, count - step)])
+        ups.append(up_out)
+        downs.append(down_out)
+    cases = [block] + ups + downs
+    pieces = []
+    for k in range(count):
+        which = jnp.where(
+            pos == k, 0, jnp.where(pos > k, pos - k, count - 1 + k - pos)
+        ).astype(jnp.int32)
+        pieces.append(lax.select_n(which, *cases))
+    return jnp.concatenate(pieces, axis=0)
 
 
 def on_device(hidden_in, w_up, w_down, out_grad):
@@ -41,8 +72,8 @@
     down_tile = w_down[0]
     x_rows = lax.all_gather(hidden_in, "p", axis=1, tiled=True)
     up_terms = jnp.dot(x_rows, up_tile, preferred_element_type=jnp.float32).astype(jnp.bfloat16)
-    preact = cycle_reduce(up_terms)
-    activation = lax.all_gather(gelu_value(preact).astype(jnp.bfloat16), "r", axis=0, tiled=True)
+    preact = line_reduce(up_terms)
+    activation = line_gather(gelu_value(preact).astype(jnp.bfloat16))
     out_part = jnp.dot(activation, down_tile, preferred_element_type=jnp.float32)
     block_out = (
         hidden_in.astype(jnp.float32)
@@ -53,10 +84,8 @@
     grad_terms = lax.dot_general(
         grad_rows, down_tile, (((1,), (1,)), ((), ())), preferred_element_type=jnp.float32
     ).astype(jnp.bfloat16)
-    act_grad = cycle_reduce(grad_terms)
-    pre_grad = lax.all_gather(
-        (act_grad * gelu_slope(preact)).astype(jnp.bfloat16), "r", axis=0, tiled=True
-    )
+    act_grad = line_reduce(grad_terms)
+    pre_grad = line_gather((act_grad * gelu_slope(preact)).astype(jnp.bfloat16))
     grad_down = lax.dot_general(
         activation, grad_rows, (((0,), (0,)), ((), ())), preferred_element_type=jnp.float32
     ).astype(jnp.bfloat16)

time: 825 us -> 707 us (0.86); the launches traced: 825 us -> 697 us
  waiting for transfers between devices: 589 us -> 442 us
  other arithmetic: 12.9 us -> 58.9 us
  starting transfers between devices: 99.1 us -> 73 us
    all_gather x2 -> x0, waiting for transfers between devices: 281 us -> none  [the longest x1 147 us: on_device(): lax.all_gather(gelu_value(preact).astype(jnp.bfloat16), 'r', axis=0, tile...]
    ppermute x6 -> x24, waiting for transfers between devices: 246 us -> 409 us  [the longest x6 222 us: line_gather(): lax.ppermute(down_out, 'r', [(i, i - 1) for i in range(1, count - step)])]
    reduce_scatter x1, waiting for transfers between devices: 31.2 us -> 3.23 us  [on_device(): lax.psum_scatter(back_part, 'p', scatter_dimension=1, tiled=True)]
    ppermute x6 -> x24, starting transfers between devices: 98.7 us -> 72.9 us  [the longest x6 31 us: line_reduce(): lax.ppermute(up_out, 'r', [(i, i + 1) for i in range(0, step + 1)])]
    convert_element_type x1 -> x5, other arithmetic: 8.6 us -> 32.7 us  [the longest x4 26.4 us: line_reduce(): (up_in + lax.dynamic_index_in_dim(shares, up_block, 0, keepdims=False)).a...]
    select_n x0 -> x4, other arithmetic: none -> 21.9 us  [line_gather(): pieces.append(lax.select_n(which, *cases))]
    unnamed x13 -> x37, local copies, waits for them, and re-layouts: 18 us -> 19.2 us
  transfers between devices with their start and end apart: 12 -> 28, of which waited for: 8 -> 16; matrix products, arithmetic and copies ran while one was open for 13% -> 22% of each run, Pallas kernels for 0% -> 0%
where the time goes in v2:
time: 707 us; the launch traced here: 697 us
  waiting for transfers between devices  442 us (63%)
  matrix products  84.5 us (12%)
  starting transfers between devices  73 us (10%)
  other arithmetic  58.9 us (8%)
  local copies, waits for them, and re-layouts  25 us (4%)
  between operations  14.3 us (2%)
    ppermute x6, waiting for transfers between devices, line_gather(): lax.ppermute(down_out, 'r', [(i, i - 1) for i in range(1, count - step)])  222 us
    ppermute x6, waiting for transfers between devices, line_reduce(): lax.ppermute(up_out, 'r', [(i, i + 1) for i in range(0, step + 1)])  175 us
    ppermute x6, starting transfers between devices, line_reduce(): lax.ppermute(up_out, 'r', [(i, i + 1) for i in range(0, step + 1)])  31 us
    all_gather x1, waiting for transfers between devices, on_device(): grad_rows = lax.all_gather(out_grad, 'p', axis=1, tiled=True)  26.4 us
    convert_element_type x4, other arithmetic, line_reduce(): (up_in + lax.dynamic_index_in_dim(shares, up_block, 0, keepdims=False)).a...  26.4 us
    ppermute x6, starting transfers between devices, line_gather(): lax.ppermute(up_out, 'r', [(i, i + 1) for i in range(step, count - 1)])  23.6 us
    select_n x4, other arithmetic, line_gather(): pieces.append(lax.select_n(which, *cases))  21.9 us
    unnamed x37, local copies, waits for them, and re-layouts  19.2 us
  transfers between devices with their start and end apart: 28, of which 16 were waited for; matrix products, arithmetic and copies ran while one was open for 22% of the time, Pallas kernels for 0%

profile of v2, /device:TPU:0, one launch (start us, length us, event | category | flops | bytes accessed | tf_op | source)
XLA Modules:
  0.0 697.2 jit_solution(5317251191225004267)
XLA Ops:
  8.7 26.4 %all-gather.5.cloned.1.call-done = bf16[1024,1024]{1,0:T(8,128)(2,1)} async-done(((bf16[1024,256]{1,0:T(8,128)(2,1)}), bf16[1024,1024]{1,0:T(8,128)(2,1)}) %all-gather.5.cloned.1.call-update) | async-done | bytes 2097168 | tf_op jit(solution)/shard_map/all_gather | solution.py:83
  35.1 12.8 %fusion.11 = bf16[1024,4096]{1,0:T(8,128)(2,1)S(1)} fusion(bf16[1024,1024]{1,0:T(8,128)(2,1)} %all-gather.5.cloned.1.call-done, bf16[1,4096,1024]{2,1,0:T(8,128)(2,1)} %param.6), kind=kOutput, calls=%fused_computation.13 | convolution fusion | flops 8594128896 | bytes 18874368 | tf_op jit(solution)/shard_map/dot_general | solution.py:84
  48.0 3.0 dynamic-slice_bitcast_fusion.1
  52.6 3.5 collective-permute-start.12
  56.1 2.0 collective-permute-start.15
  59.6 12.8 %fusion.8 = bf16[1024,4096]{1,0:T(8,128)(2,1)S(1)} fusion(bf16[1024,1024]{1,0:T(8,128)(2,1)} %all-gather.3.cloned.1.call-done, bf16[1,1024,4096]{2,1,0:T(8,128)(2,1)} %param.5), kind=kOutput, calls=%fused_computation.12 | convolution fusion | flops 8594128896 | bytes 18874368 | tf_op jit(solution)/shard_map/dot_general | solution.py:74
  72.3 2.8 dynamic-slice_bitcast_fusion.3
  77.0 4.8 collective-permute-start
  83.7 18.6 %collective-permute-done.12 = bf16[256,4096]{1,0:T(8,128)(2,1)S(1)} collective-permute-done((bf16[256,4096]{1,0:T(8,128)(2,1)}, bf16[256,4096]{1,0:T(8,128)(2,1)S(1)}, u32[]{:S(2)}, u32[]{:S(2)}) %collective-permute-start.12) | collective-permute-done | bytes 2097184 | tf_op jit(solution)/shard_map/ppermute | solution.py:40
  102.3 6.7 fusion.24
  109.0 4.4 collective-permute-start.13
  113.4 2.0 collective-permute-start.16
  115.4 31.8 %collective-permute-done = bf16[256,4096]{1,0:T(8,128)(2,1)} collective-permute-done((bf16[256,4096]{1,0:T(8,128)(2,1)}, bf16[256,4096]{1,0:T(8,128)(2,1)}, u32[]{:S(2)}, u32[]{:S(2)}) %collective-permute-start) | collective-permute-done | bytes 2097184 | tf_op jit(solution)/shard_map/ppermute | solution.py:40
  147.2 6.0 fusion.29
  153.2 5.8 collective-permute-start.1
  160.9 31.2 %collective-permute-done.13 = bf16[256,4096]{1,0:T(8,128)(2,1)S(1)} collective-permute-done((bf16[256,4096]{1,0:T(8,128)(2,1)}, bf16[256,4096]{1,0:T(8,128)(2,1)S(1)}, u32[]{:S(2)}, u32[]{:S(2)}) %collective-permute-start.13) | collective-permute-done | bytes 2097184 | tf_op jit(solution)/shard_map/ppermute | solution.py:40
  192.2 6.5 fusion.23
  200.0 6.3 collective-permute-start.14
  206.2 30.9 %collective-permute-done.1 = bf16[256,4096]{1,0:T(8,128)(2,1)} collective-permute-done((bf16[256,4096]{1,0:T(8,128)(2,1)}, bf16[256,4096]{1,0:T(8,128)(2,1)}, u32[]{:S(2)}, u32[]{:S(2)}) %collective-permute-start.1) | collective-permute-done | bytes 2097184 | tf_op jit(solution)/shard_map/ppermute | solution.py:40
  237.1 7.2 %fusion.28 = (bf16[256,4096]{1,0:T(8,128)(2,1)}, bf16[256,4096]{1,0:T(8,128)(2,1)}) fusion(bf16[256,4096]{1,0:T(8,128)(2,1)} %collective-permute-done.1, bf16[4,256,4096]{2,1,0:T(8,128)(2,1)} %bitcast.79, s32[]{:T(128)S(6)} %min.27, s32[]{:T(128)S(6)} %min.30, bf16[256,4096]{1,0:T(8,128)(2,1)} %collective-permute-done.4), kind=kLoop, calls=%fused_computation.38 | loop fusion | flops 8388608 | bytes 12582920 | tf_op jit(solution)/shard_map/convert_element_type | solution.py:33
  245.6 6.3 collective-permute-start.2
  252.0 30.1 %collective-permute-done.14 = bf16[256,4096]{1,0:T(8,128)(2,1)} collective-permute-done((bf16[256,4096]{1,0:T(8,128)(2,1)}, bf16[256,4096]{1,0:T(8,128)(2,1)}, u32[]{:S(2)}, u32[]{:S(2)}) %collective-permute-start.14) | collective-permute-done | bytes 2097184 | tf_op jit(solution)/shard_map/ppermute | solution.py:40
  282.0 11.6 %collective-permute-done.5 = bf16[256,4096]{1,0:T(8,128)(2,1)} collective-permute-done((bf16[256,4096]{1,0:T(8,128)(2,1)}, bf16[256,4096]{1,0:T(8,128)(2,1)}, u32[]{:S(2)}, u32[]{:S(2)}) %collective-permute-start.5) | collective-permute-done | bytes 2097184 | tf_op jit(solution)/shard_map/ppermute | solution.py:43
  293.6 32.7 %collective-permute-done.2 = bf16[256,4096]{1,0:T(8,128)(2,1)} collective-permute-done((bf16[256,4096]{1,0:T(8,128)(2,1)}, bf16[256,4096]{1,0:T(8,128)(2,1)}, u32[]{:S(2)}, u32[]{:S(2)}) %collective-permute-start.2) | collective-permute-done | bytes 2097184 | tf_op jit(solution)/shard_map/ppermute | solution.py:40
  326.3 6.3 fusion.19
  334.0 5.2 collective-permute-start.6
  339.1 43.2 %collective-permute-done.9 = bf16[256,4096]{1,0:T(8,128)(2,1)S(1)} collective-permute-done((bf16[256,4096]{1,0:T(8,128)(2,1)S(1)}, bf16[256,4096]{1,0:T(8,128)(2,1)S(1)}, u32[]{:S(2)}, u32[]{:S(2)}) %collective-permute-start.9) | collective-permute-done | bytes 2097184 | tf_op jit(solution)/shard_map/ppermute | solution.py:57
  383.6 2.0 collective-permute-start.7
  386.9 11.4 %collective-permute-start.18 = (bf16[256,4096]{1,0:T(8,128)(2,1)S(1)}, bf16[256,4096]{1,0:T(8,128)(2,1)}, u32[]{:S(2)}, u32[]{:S(2)}) collective-permute-start(bf16[256,4096]{1,0:T(8,128)(2,1)S(1)} %get-tuple-element.16), channel_id=1, source_target_pairs={{0,4},{4,8},{8,12},{1,5},{5,9},{9,13},{2,6},{6,10},{10,14},{3,7},{... | collective-permute-start | bytes 6291464 | tf_op jit(solution)/shard_map/ppermute | solution.py:56
  398.3 34.8 %collective-permute-done.10 = bf16[256,4096]{1,0:T(8,128)(2,1)} collective-permute-done((bf16[256,4096]{1,0:T(8,128)(2,1)S(1)}, bf16[256,4096]{1,0:T(8,128)(2,1)}, u32[]{:S(2)}, u32[]{:S(2)}) %collective-permute-start.10) | collective-permute-done | bytes 2097184 | tf_op jit(solution)/shard_map/ppermute | solution.py:57
  434.4 2.0 collective-permute-start.8
  436.5 41.6 %collective-permute-done.21 = bf16[256,4096]{1,0:T(8,128)(2,1)} collective-permute-done((bf16[256,4096]{1,0:T(8,128)(2,1)S(1)}, bf16[256,4096]{1,0:T(8,128)(2,1)}, u32[]{:S(2)}, u32[]{:S(2)}) %collective-permute-start.21) | collective-permute-done | bytes 2097184 | tf_op jit(solution)/shard_map/ppermute | solution.py:57
  479.4 2.0 collective-permute-start.19
  481.4 41.6 %collective-permute-done.11 = bf16[256,4096]{1,0:T(8,128)(2,1)} collective-permute-done((bf16[256,4096]{1,0:T(8,128)(2,1)}, bf16[256,4096]{1,0:T(8,128)(2,1)}, u32[]{:S(2)}, u32[]{:S(2)}) %collective-permute-start.11) | collective-permute-done | bytes 2097184 | tf_op jit(solution)/shard_map/ppermute | solution.py:57
  523.0 5.7 select_select_fusion.7
  528.8 5.6 select_select_fusion.6
  536.4 14.2 %fusion.2 = f32[1024,1024]{1,0:T(8,128)} fusion(bf16[1,4096,1024]{2,1,0:T(8,128)(2,1)} %param.6, bf16[256,4096]{1,0:T(8,128)(2,1)S(1)} %get-tuple-element.13, bf16[256,4096]{1,0:T(8,128)(2,1)S(1)} %get-tuple-element.15, bf16[256,4096]{1,0:T(8,128)(2,1)S(1)} %get-tuple-element.14, bf16[256,4096]{1,0:T(8,128)(2,1)S(1)} %get-tuple-element.12), kind=kOutput, calls=%fused_computation.4 | convolution fusion | flops 8623489024 | bytes 20971520 | tf_op jit(solution)/shard_map/dot_general | solution.py:77
  550.6 15.4 %collective-permute-done.22 = bf16[256,4096]{1,0:T(8,128)(2,1)} collective-permute-done((bf16[256,4096]{1,0:T(8,128)(2,1)}, bf16[256,4096]{1,0:T(8,128)(2,1)}, u32[]{:S(2)}, u32[]{:S(2)}) %collective-permute-start.22) | collective-permute-done | bytes 2097184 | tf_op jit(solution)/shard_map/ppermute | solution.py:57
  568.3 45.5 %collective-permute-done.23 = bf16[256,4096]{1,0:T(8,128)(2,1)S(1)} collective-permute-done((bf16[256,4096]{1,0:T(8,128)(2,1)}, bf16[256,4096]{1,0:T(8,128)(2,1)S(1)}, u32[]{:S(2)}, u32[]{:S(2)}) %collective-permute-start.23) | collective-permute-done | bytes 2097184 | tf_op jit(solution)/shard_map/ppermute | solution.py:57
  613.9 5.3 select_select_fusion.3
  619.1 5.3 select_select_fusion.2
  624.5 17.1 %fusion.4 = f32[1024,1024]{1,0:T(8,128)} fusion(bf16[1,1024,4096]{2,1,0:T(8,128)(2,1)} %param.5, bf16[256,4096]{1,0:T(8,128)(2,1)} %get-tuple-element.9, bf16[256,4096]{1,0:T(8,128)(2,1)} %get-tuple-element.11, bf16[256,4096]{1,0:T(8,128)(2,1)} %get-tuple-element.10, bf16[256,4096]{1,0:T(8,128)(2,1)} %get-tuple-element.8), kind=kOutput, calls=%fused_computation.6 | convolution fusion | flops 8623489024 | bytes 20971520 | tf_op jit(solution)/shard_map/dot_general | solution.py:95
  643.1 13.7 %convert_bitcast_fusion.1 = bf16[1,1024,4096]{1,2,0:T(8,128)(2,1)} fusion(bf16[1024,1024]{1,0:T(8,128)(2,1)} %all-gather.3.cloned.1.call-done, bf16[256,4096]{1,0:T(8,128)(2,1)} %get-tuple-element.9, bf16[256,4096]{1,0:T(8,128)(2,1)} %get-tuple-element.11, bf16[256,4096]{1,0:T(8,128)(2,1)} %get-tuple-element.10, bf16[256,4096]{1,0:T(8,128)(2,1)S(1)} %copy-done.17), kind=kOutput, calls=%fused_computation.11 | convolution fusion | flops 8627683328 | bytes 18874368 | tf_op jit(solution)/shard_map/dot_general | solution.py:92
  656.8 12.1 %copy.8 = bf16[1,1024,4096]{2,1,0:T(8,128)(2,1)} copy(bf16[1,1024,4096]{1,2,0:T(8,128)(2,1)} %convert_bitcast_fusion.1) | data formatting | bytes 16777216
  668.9 14.0 %convert_bitcast_fusion = bf16[1,4096,1024]{2,1,0:T(8,128)(2,1)} fusion(bf16[1024,1024]{1,0:T(8,128)(2,1)} %all-gather.5.cloned.1.call-done, bf16[256,4096]{1,0:T(8,128)(2,1)} %copy-done.14, bf16[256,4096]{1,0:T(8,128)(2,1)} %copy-done.16, bf16[256,4096]{1,0:T(8,128)(2,1)} %copy-done.15, bf16[256,4096]{1,0:T(8,128)(2,1)S(1)} %copy-done.13), kind=kOutput, calls=%fused_computation.10 | convolution fusion | flops 8627683328 | bytes 18874368 | tf_op jit(solution)/shard_map/dot_general | solution.py:89
  682.9 2.2 add_convert_fusion.1
  685.1 3.2 reduce-scatter.5.cloned.1.call-done
  688.3 2.1 add_convert_fusion
  (68 shorter events, 25.3 us)
Async XLA Ops:
  7.2 28.0 %all-gather.5.cloned.1.call-start = ((), (), s32[]{:S(2)}) async-start(), calls=%async_computation.4 | async-start | bytes 2621440 | tf_op jit(solution)/shard_map/all_gather | solution.py:83
  7.9 51.7 %all-gather.3.cloned.1.call-start = ((), (), s32[]{:S(2)}) async-start(), calls=%async_computation.2 | async-start | bytes 2621440 | tf_op jit(solution)/shard_map/all_gather | solution.py:73
  8.6 674.3 %reduce-scatter.3.cloned.1.call-start = ((), (), s32[]{:S(2)}) async-start(), calls=%async_computation.3 | async-start | bytes 5242880 | tf_op jit(solution)/shard_map/reduce_scatter | solution.py:80
  48.0 4.7 copy-start
  52.6 49.7 %collective-permute-start.12 = (bf16[256,4096]{1,0:T(8,128)(2,1)}, bf16[256,4096]{1,0:T(8,128)(2,1)S(1)}, u32[]{:S(2)}, u32[]{:S(2)}) collective-permute-start(bf16[256,4096]{1,0:T(8,128)(2,1)} %get-tuple-element.22), channel_id=1, source_target_pairs={{0,4},{1,5},{2,6},{3,7},{16,20},{17,21},{18,22},{19,23}} | collective-permute-start | bytes 6291464 | tf_op jit(solution)/shard_map/ppermute | solution.py:40
  56.1 46.1 %collective-permute-start.15 = (bf16[256,4096]{1,0:T(8,128)(2,1)}, bf16[256,4096]{1,0:T(8,128)(2,1)}, u32[]{:S(2)}, u32[]{:S(2)}) collective-permute-start(bf16[256,4096]{1,0:T(8,128)(2,1)} %get-tuple-element.23), channel_id=1, source_target_pairs={{12,8},{13,9},{14,10},{15,11},{28,24},{29,25},{30,26},{31,27}} | collective-permute-start | bytes 6291464 | tf_op jit(solution)/shard_map/ppermute | solution.py:43
  72.3 4.7 copy-start.1
  77.0 70.2 %collective-permute-start = (bf16[256,4096]{1,0:T(8,128)(2,1)}, bf16[256,4096]{1,0:T(8,128)(2,1)}, u32[]{:S(2)}, u32[]{:S(2)}) collective-permute-start(bf16[256,4096]{1,0:T(8,128)(2,1)} %get-tuple-element.28), channel_id=1, source_target_pairs={{0,4},{1,5},{2,6},{3,7},{16,20},{17,21},{18,22},{19,23}} | collective-permute-start | bytes 6291464 | tf_op jit(solution)/shard_map/ppermute | solution.py:40
  81.7 65.5 %collective-permute-start.3 = (bf16[256,4096]{1,0:T(8,128)(2,1)}, bf16[256,4096]{1,0:T(8,128)(2,1)}, u32[]{:S(2)}, u32[]{:S(2)}) collective-permute-start(bf16[256,4096]{1,0:T(8,128)(2,1)} %get-tuple-element.29), channel_id=1, source_target_pairs={{12,8},{13,9},{14,10},{15,11},{28,24},{29,25},{30,26},{31,27}} | collective-permute-start | bytes 6291464 | tf_op jit(solution)/shard_map/ppermute | solution.py:43
  102.3 44.9 %copy-start.2 = (bf16[1024,4096]{1,0:T(8,128)(2,1)S(1)}, bf16[1024,4096]{1,0:T(8,128)(2,1)}, u32[]{:S(2)}) copy-start(bf16[1024,4096]{1,0:T(8,128)(2,1)} %copy-done.1) | copy-start | bytes 25165828
  109.0 83.2 %collective-permute-start.13 = (bf16[256,4096]{1,0:T(8,128)(2,1)}, bf16[256,4096]{1,0:T(8,128)(2,1)S(1)}, u32[]{:S(2)}, u32[]{:S(2)}) collective-permute-start(bf16[256,4096]{1,0:T(8,128)(2,1)} %get-tuple-element.20), channel_id=1, source_target_pairs={{0,4},{4,8},{1,5},{5,9},{2,6},{6,10},{3,7},{7,11},{16,20},{20,24},... | collective-permute-start | bytes 6291464 | tf_op jit(solution)/shard_map/ppermute | solution.py:40
  113.4 78.8 %collective-permute-start.16 = (bf16[256,4096]{1,0:T(8,128)(2,1)}, bf16[256,4096]{1,0:T(8,128)(2,1)}, u32[]{:S(2)}, u32[]{:S(2)}) collective-permute-start(bf16[256,4096]{1,0:T(8,128)(2,1)} %get-tuple-element.21), channel_id=1, source_target_pairs={{8,4},{12,8},{9,5},{13,9},{10,6},{14,10},{11,7},{15,11},{24,20},{2... | collective-permute-start | bytes 6291464 | tf_op jit(solution)/shard_map/ppermute | solution.py:43
  153.2 83.9 %collective-permute-start.1 = (bf16[256,4096]{1,0:T(8,128)(2,1)}, bf16[256,4096]{1,0:T(8,128)(2,1)}, u32[]{:S(2)}, u32[]{:S(2)}) collective-permute-start(bf16[256,4096]{1,0:T(8,128)(2,1)} %get-tuple-element.26), channel_id=1, source_target_pairs={{0,4},{4,8},{1,5},{5,9},{2,6},{6,10},{3,7},{7,11},{16,20},{20,24},... | collective-permute-start | bytes 6291464 | tf_op jit(solution)/shard_map/ppermute | solution.py:40
  159.0 78.1 %collective-permute-start.4 = (bf16[256,4096]{1,0:T(8,128)(2,1)}, bf16[256,4096]{1,0:T(8,128)(2,1)}, u32[]{:S(2)}, u32[]{:S(2)}) collective-permute-start(bf16[256,4096]{1,0:T(8,128)(2,1)} %get-tuple-element.27), channel_id=1, source_target_pairs={{8,4},{12,8},{9,5},{13,9},{10,6},{14,10},{11,7},{15,11},{24,20},{2... | collective-permute-start | bytes 6291464 | tf_op jit(solution)/shard_map/ppermute | solution.py:43
  198.7 53.3 %collective-permute-start.17 = (bf16[256,4096]{1,0:T(8,128)(2,1)}, bf16[256,4096]{1,0:T(8,128)(2,1)S(1)}, u32[]{:S(2)}, u32[]{:S(2)}) collective-permute-start(bf16[256,4096]{1,0:T(8,128)(2,1)} %get-tuple-element.19), channel_id=1, source_target_pairs={{4,0},{8,4},{12,8},{5,1},{9,5},{13,9},{6,2},{10,6},{14,10},{7,3},{... | collective-permute-start | bytes 6291464 | tf_op jit(solution)/shard_map/ppermute | solution.py:43
  200.0 82.1 %collective-permute-start.14 = (bf16[256,4096]{1,0:T(8,128)(2,1)}, bf16[256,4096]{1,0:T(8,128)(2,1)}, u32[]{:S(2)}, u32[]{:S(2)}) collective-permute-start(bf16[256,4096]{1,0:T(8,128)(2,1)} %get-tuple-element.18), channel_id=1, source_target_pairs={{0,4},{4,8},{8,12},{1,5},{5,9},{9,13},{2,6},{6,10},{10,14},{3,7},{... | collective-permute-start | bytes 6291464 | tf_op jit(solution)/shard_map/ppermute | solution.py:40
  244.3 49.3 %collective-permute-start.5 = (bf16[256,4096]{1,0:T(8,128)(2,1)}, bf16[256,4096]{1,0:T(8,128)(2,1)}, u32[]{:S(2)}, u32[]{:S(2)}) collective-permute-start(bf16[256,4096]{1,0:T(8,128)(2,1)} %get-tuple-element.25), channel_id=1, source_target_pairs={{4,0},{8,4},{12,8},{5,1},{9,5},{13,9},{6,2},{10,6},{14,10},{7,3},{... | collective-permute-start | bytes 6291464 | tf_op jit(solution)/shard_map/ppermute | solution.py:43
  245.6 80.7 %collective-permute-start.2 = (bf16[256,4096]{1,0:T(8,128)(2,1)}, bf16[256,4096]{1,0:T(8,128)(2,1)}, u32[]{:S(2)}, u32[]{:S(2)}) collective-permute-start(bf16[256,4096]{1,0:T(8,128)(2,1)} %get-tuple-element.24), channel_id=1, source_target_pairs={{0,4},{4,8},{8,12},{1,5},{5,9},{9,13},{2,6},{6,10},{10,14},{3,7},{... | collective-permute-start | bytes 6291464 | tf_op jit(solution)/shard_map/ppermute | solution.py:40
  251.9 41.7 %copy-start.9 = (bf16[256,4096]{1,0:T(8,128)(2,1)}, bf16[256,4096]{1,0:T(8,128)(2,1)S(1)}, u32[]{:S(2)}) copy-start(bf16[256,4096]{1,0:T(8,128)(2,1)S(1)} %collective-permute-done.17) | copy-start | bytes 6291460
  332.6 53.0 %copy-start.3 = (bf16[256,4096]{1,0:T(8,128)(2,1)}, bf16[256,4096]{1,0:T(8,128)(2,1)S(1)}, u32[]{:S(2)}) copy-start(bf16[256,4096]{1,0:T(8,128)(2,1)S(1)} %get-tuple-element.17) | copy-start | bytes 6291460
  332.7 49.6 %collective-permute-start.9 = (bf16[256,4096]{1,0:T(8,128)(2,1)S(1)}, bf16[256,4096]{1,0:T(8,128)(2,1)S(1)}, u32[]{:S(2)}, u32[]{:S(2)}) collective-permute-start(bf16[256,4096]{1,0:T(8,128)(2,1)S(1)} %get-tuple-element.17), channel_id=1, source_target_pairs={{4,0},{8,4},{12,8},{5,1},{9,5},{13,9},{6,2},{10,6},{14,10},{7,3},{... | collective-permute-start | bytes 6291464 | tf_op jit(solution)/shard_map/ppermute | solution.py:57
  334.0 49.6 %collective-permute-start.6 = (bf16[256,4096]{1,0:T(8,128)(2,1)S(1)}, bf16[256,4096]{1,0:T(8,128)(2,1)S(1)}, u32[]{:S(2)}, u32[]{:S(2)}) collective-permute-start(bf16[256,4096]{1,0:T(8,128)(2,1)S(1)} %get-tuple-element.17), channel_id=1, source_target_pairs={{0,4},{4,8},{8,12},{1,5},{5,9},{9,13},{2,6},{6,10},{10,14},{3,7},{... | collective-permute-start | bytes 6291464 | tf_op jit(solution)/shard_map/ppermute | solution.py:56
  382.3 4.6 copy-start.5
  382.3 50.8 %collective-permute-start.10 = (bf16[256,4096]{1,0:T(8,128)(2,1)S(1)}, bf16[256,4096]{1,0:T(8,128)(2,1)}, u32[]{:S(2)}, u32[]{:S(2)}) collective-permute-start(bf16[256,4096]{1,0:T(8,128)(2,1)S(1)} %collective-permute-done.9), channel_id=1, source_target_pairs={{4,0},{8,4},{5,1},{9,5},{6,2},{10,6},{7,3},{11,7},{20,16},{24,20},... | collective-permute-start | bytes 6291464 | tf_op jit(solution)/shard_map/ppermute | solution.py:57
  383.6 49.5 %copy-start.7 = (bf16[256,4096]{1,0:T(8,128)(2,1)}, bf16[256,4096]{1,0:T(8,128)(2,1)S(1)}, u32[]{:S(2)}) copy-start(bf16[256,4096]{1,0:T(8,128)(2,1)S(1)} %collective-permute-done.6) | copy-start | bytes 6291460
  383.6 50.8 %collective-permute-start.7 = (bf16[256,4096]{1,0:T(8,128)(2,1)S(1)}, bf16[256,4096]{1,0:T(8,128)(2,1)}, u32[]{:S(2)}, u32[]{:S(2)}) collective-permute-start(bf16[256,4096]{1,0:T(8,128)(2,1)S(1)} %collective-permute-done.6), channel_id=1, source_target_pairs={{4,8},{8,12},{5,9},{9,13},{6,10},{10,14},{7,11},{11,15},{20,24},{2... | collective-permute-start | bytes 6291464 | tf_op jit(solution)/shard_map/ppermute | solution.py:56
  385.6 92.4 %collective-permute-start.21 = (bf16[256,4096]{1,0:T(8,128)(2,1)S(1)}, bf16[256,4096]{1,0:T(8,128)(2,1)}, u32[]{:S(2)}, u32[]{:S(2)}) collective-permute-start(bf16[256,4096]{1,0:T(8,128)(2,1)S(1)} %get-tuple-element.16), channel_id=1, source_target_pairs={{4,0},{8,4},{12,8},{5,1},{9,5},{13,9},{6,2},{10,6},{14,10},{7,3},{... | collective-permute-start | bytes 6291464 | tf_op jit(solution)/shard_map/ppermute | solution.py:57
  386.9 92.4 %collective-permute-start.18 = (bf16[256,4096]{1,0:T(8,128)(2,1)S(1)}, bf16[256,4096]{1,0:T(8,128)(2,1)}, u32[]{:S(2)}, u32[]{:S(2)}) collective-permute-start(bf16[256,4096]{1,0:T(8,128)(2,1)S(1)} %get-tuple-element.16), channel_id=1, source_target_pairs={{0,4},{4,8},{8,12},{1,5},{5,9},{9,13},{2,6},{6,10},{10,14},{3,7},{... | collective-permute-start | bytes 6291464 | tf_op jit(solution)/shard_map/ppermute | solution.py:56
  433.1 89.9 %collective-permute-start.11 = (bf16[256,4096]{1,0:T(8,128)(2,1)}, bf16[256,4096]{1,0:T(8,128)(2,1)}, u32[]{:S(2)}, u32[]{:S(2)}) collective-permute-start(bf16[256,4096]{1,0:T(8,128)(2,1)} %collective-permute-done.10), channel_id=1, source_target_pairs={{4,0},{5,1},{6,2},{7,3},{20,16},{21,17},{22,18},{23,19}} | collective-permute-start | bytes 6291464 | tf_op jit(solution)/shard_map/ppermute | solution.py:57
  434.4 88.6 %collective-permute-start.8 = (bf16[256,4096]{1,0:T(8,128)(2,1)}, bf16[256,4096]{1,0:T(8,128)(2,1)}, u32[]{:S(2)}, u32[]{:S(2)}) collective-permute-start(bf16[256,4096]{1,0:T(8,128)(2,1)} %collective-permute-done.7), channel_id=1, source_target_pairs={{8,12},{9,13},{10,14},{11,15},{24,28},{25,29},{26,30},{27,31}} | collective-permute-start | bytes 6291464 | tf_op jit(solution)/shard_map/ppermute | solution.py:56
  436.5 92.2 %copy-start.4 = (bf16[256,4096]{1,0:T(8,128)(2,1)S(1)}, bf16[256,4096]{1,0:T(8,128)(2,1)}, u32[]{:S(2)}) copy-start(bf16[256,4096]{1,0:T(8,128)(2,1)} %copy-done.3) | copy-start | bytes 6291460
  436.5 92.3 %copy-start.6 = (bf16[256,4096]{1,0:T(8,128)(2,1)S(1)}, bf16[256,4096]{1,0:T(8,128)(2,1)}, u32[]{:S(2)}) copy-start(bf16[256,4096]{1,0:T(8,128)(2,1)} %copy-done.5) | copy-start | bytes 6291460
  436.5 92.3 %copy-start.8 = (bf16[256,4096]{1,0:T(8,128)(2,1)S(1)}, bf16[256,4096]{1,0:T(8,128)(2,1)}, u32[]{:S(2)}) copy-start(bf16[256,4096]{1,0:T(8,128)(2,1)} %copy-done.7) | copy-start | bytes 6291460
  478.1 88.0 %collective-permute-start.22 = (bf16[256,4096]{1,0:T(8,128)(2,1)}, bf16[256,4096]{1,0:T(8,128)(2,1)}, u32[]{:S(2)}, u32[]{:S(2)}) collective-permute-start(bf16[256,4096]{1,0:T(8,128)(2,1)} %collective-permute-done.21), channel_id=1, source_target_pairs={{4,0},{8,4},{5,1},{9,5},{6,2},{10,6},{7,3},{11,7},{20,16},{24,20},... | collective-permute-start | bytes 6291464 | tf_op jit(solution)/shard_map/ppermute | solution.py:57
  479.4 88.0 %collective-permute-start.19 = (bf16[256,4096]{1,0:T(8,128)(2,1)}, bf16[256,4096]{1,0:T(8,128)(2,1)}, u32[]{:S(2)}, u32[]{:S(2)}) collective-permute-start(bf16[256,4096]{1,0:T(8,128)(2,1)} %collective-permute-done.18), channel_id=1, source_target_pairs={{4,8},{8,12},{5,9},{9,13},{6,10},{10,14},{7,11},{11,15},{20,24},{2... | collective-permute-start | bytes 6291464 | tf_op jit(solution)/shard_map/ppermute | solution.py:56
  528.7 5.7 copy-start.12
  528.7 5.7 copy-start.14
  534.4 1.4 copy-start.15
  534.4 2.0 copy-start.16
  550.6 137.8 %reduce-scatter.5.cloned.1.call-start = ((), (), s32[]{:S(2)}) async-start(), calls=%async_computation.5 | async-start | bytes 5242880 | tf_op jit(solution)/shard_map/reduce_scatter | solution.py:100
  566.0 47.8 %collective-permute-start.23 = (bf16[256,4096]{1,0:T(8,128)(2,1)}, bf16[256,4096]{1,0:T(8,128)(2,1)S(1)}, u32[]{:S(2)}, u32[]{:S(2)}) collective-permute-start(bf16[256,4096]{1,0:T(8,128)(2,1)} %collective-permute-done.22), channel_id=1, source_target_pairs={{4,0},{5,1},{6,2},{7,3},{20,16},{21,17},{22,18},{23,19}} | collective-permute-start | bytes 6291464 | tf_op jit(solution)/shard_map/ppermute | solution.py:57
  567.3 46.5 %collective-permute-start.20 = (bf16[256,4096]{1,0:T(8,128)(2,1)}, bf16[256,4096]{1,0:T(8,128)(2,1)S(1)}, u32[]{:S(2)}, u32[]{:S(2)}) collective-permute-start(bf16[256,4096]{1,0:T(8,128)(2,1)} %collective-permute-done.19), channel_id=1, source_target_pairs={{8,12},{9,13},{10,14},{11,15},{24,28},{25,29},{26,30},{27,31}} | collective-permute-start | bytes 6291464 | tf_op jit(solution)/shard_map/ppermute | solution.py:56
  641.5 1.6 copy-start.17
  656.8 12.1 %copy-start.13 = (bf16[256,4096]{1,0:T(8,128)(2,1)S(1)}, bf16[256,4096]{1,0:T(8,128)(2,1)}, u32[]{:S(2)}) copy-start(bf16[256,4096]{1,0:T(8,128)(2,1)} %copy-done.12) | copy-start | bytes 6291460
  668.9 14.0 %copy-start.10 = (bf16[1024,256]{1,0:T(8,128)(2,1)S(1)}, bf16[1024,256]{1,0:T(8,128)(2,1)}, u32[]{:S(2)}) copy-start(bf16[1024,256]{1,0:T(8,128)(2,1)} %param.4) | copy-start | bytes 1572868
  682.9 5.4 copy-start.11
Sparse Core Ops, SparseCore 0:
  9.6 25.5 all-gather.4
  36.7 22.8 all-gather.2
  550.7 47.5 reduce-scatter.2
  641.7 46.6 reduce-scatter.4

commit v3 on v1

--- a/solution.py
+++ b/solution.py
@@ -21,42 +21,131 @@
     )
 
 
-def cycle_reduce(terms):
-    count = lax.axis_size("r")
+class LineReduce:
+    def __init__(self, terms):
+        self.count = lax.axis_size("r")
+        self.pos = lax.axis_index("r")
+        rows = terms.shape[0] // self.count
+        self.shares = terms.reshape(self.count, rows, terms.shape[1])
+        self.up_in = jnp.zeros((rows, terms.shape[1]), jnp.float32)
+        self.down_in = jnp.zeros((rows, terms.shape[1]), jnp.float32)
+
+    def senders(self, step):
+        return (0, step), (self.count - 1 - step, self.count - 1)
+
+    def payload(self, step):
+        last = self.count - 1
+        up_block = jnp.clip(last - step + self.pos, 0, last)
+        down_block = jnp.clip(self.pos + step - last, 0, last)
+        up = self.up_in + lax.dynamic_index_in_dim(self.shares, up_block, 0, keepdims=False)
+        down = self.down_in + lax.dynamic_index_in_dim(self.shares, down_block, 0, keepdims=False)
+        return up.astype(jnp.bfloat16), down.astype(jnp.bfloat16)
+
+    def receive(self, step, up, down):
+        self.up_in = up.astype(jnp.float32)
+        self.down_in = down.astype(jnp.float32)
+
+    def result(self):
+        own = lax.dynamic_index_in_dim(self.shares, self.pos, 0, keepdims=False)
+        return self.up_in + own.astype(jnp.float32) + self.down_in
+
+
+class LineGather:
+    def __init__(self, block):
+        self.count = lax.axis_size("r")
+        self.pos = lax.axis_index("r")
+        self.block = block
+        self.up_cur = self.down_cur = block
+        self.ups, self.downs = [], []
+
+    def senders(self, step):
+        return (step, self.count - 2), (1, self.count - 1 - step)
+
+    def payload(self, step):
+        return self.up_cur, self.down_cur
+
+    def receive(self, step, up, down):
+        self.up_cur, self.down_cur = up, down
+        self.ups.append(up)
+        self.downs.append(down)
+
+    def result(self):
+        count, pos = self.count, self.pos
+        cases = [self.block] + self.ups + self.downs
+        pieces = []
+        for k in range(count):
+            which = jnp.where(pos == k, 0, jnp.where(pos > k, pos - k, count - 1 + k - pos))
+            pieces.append(lax.select_n(which.astype(jnp.int32), *cases))
+        return jnp.concatenate(pieces, axis=0)
+
+
+def run_slot(entries):
     pos = lax.axis_index("r")
-    block_rows = terms.shape[0] // count
-    shares = terms.reshape(count, block_rows, terms.shape[1])
-    summed = lax.dynamic_index_in_dim(shares, pos, 0, keepdims=False).astype(jnp.float32)
-    for distance in range(1, count):
-        outgoing = lax.dynamic_index_in_dim(shares, (pos + distance) % count, 0, keepdims=False)
-        incoming = lax.ppermute(
-            outgoing, "r", [(i, (i + distance) % count) for i in range(count)]
-        )
-        summed = summed + incoming.astype(jnp.float32)
-    return summed
+    loads = [entry.payload(step) for entry, step in entries]
+    ranges = [entry.senders(step) for entry, step in entries]
+    received = []
+    for direction, shift in ((0, 1), (1, -1)):
+        combined = None
+        pairs = []
+        for load, rng in zip(loads, ranges):
+            lo, hi = rng[direction]
+            if lo > hi:
+                continue
+            pairs += [(i, i + shift) for i in range(lo, hi + 1)]
+            mine = (pos >= lo) & (pos <= hi)
+            combined = load[direction] if combined is None else jnp.where(mine, load[direction], combined)
+        if combined is None:
+            received.append(None)
+            continue
+        received.append(lax.ppermute(combined, "r", pairs))
+    for (entry, step), load, rng in zip(entries, loads, ranges):
+        parts = []
+        for direction, shift in ((0, 1), (1, -1)):
+            lo, hi = rng[direction]
+            got = received[direction]
+            if got is None or lo > hi:
+                parts.append(jnp.zeros_like(load[direction]))
+                continue
+            mine = (pos >= lo + shift) & (pos <= hi + shift)
+            parts.append(jnp.where(mine, got, jnp.zeros_like(got)))
+        entry.receive(step, *parts)
 
 
 def on_device(hidden_in, w_up, w_down, out_grad):
     up_tile = w_up[0]
     down_tile = w_down[0]
+    count = lax.axis_size("r")
     x_rows = lax.all_gather(hidden_in, "p", axis=1, tiled=True)
     up_terms = jnp.dot(x_rows, up_tile, preferred_element_type=jnp.float32).astype(jnp.bfloat16)
-    preact = cycle_reduce(up_terms)
-    activation = lax.all_gather(gelu_value(preact).astype(jnp.bfloat16), "r", axis=0, tiled=True)
+    grad_rows = lax.all_gather(out_grad, "p", axis=1, tiled=True)
+    grad_terms = lax.dot_general(
+        grad_rows, down_tile, (((1,), (1,)), ((), ())), preferred_element_type=jnp.float32
+    ).astype(jnp.bfloat16)
+
+    up_sum = LineReduce(up_terms)
+    grad_sum = LineReduce(grad_terms)
+    for step in range(count - 1):
+        run_slot([(up_sum, step)])
+    preact = up_sum.result()
+    act_gather = LineGather(gelu_value(preact).astype(jnp.bfloat16))
+    if count > 1:
+        run_slot([(act_gather, 0)])
+    for step in range(1, count - 1):
+        run_slot([(act_gather, step), (grad_sum, step - 1)])
+    if count > 1:
+        run_slot([(grad_sum, count - 2)])
+    act_grad = grad_sum.result()
+    pre_gather = LineGather((act_grad * gelu_slope(preact)).astype(jnp.bfloat16))
+    for step in range(count - 1):
+        run_slot([(pre_gather, step)])
+    activation = act_gather.result()
+    pre_grad = pre_gather.result()
+
     out_part = jnp.dot(activation, down_tile, preferred_element_type=jnp.float32)
     block_out = (
         hidden_in.astype(jnp.float32)
         + lax.psum_scatter(out_part, "p", scatter_dimension=1, tiled=True)
     ).astype(jnp.bfloat16)
-
-    grad_rows = lax.all_gather(out_grad, "p", axis=1, tiled=True)
-    grad_terms = lax.dot_general(
-        grad_rows, down_tile, (((1,), (1,)), ((), ())), preferred_element_type=jnp.float32
-    ).astype(jnp.bfloat16)
-    act_grad = cycle_reduce(grad_terms)
-    pre_grad = lax.all_gather(
-        (act_grad * gelu_slope(preact)).astype(jnp.bfloat16), "r", axis=0, tiled=True
-    )
     grad_down = lax.dot_general(
         activation, grad_rows, (((0,), (0,)), ((), ())), preferred_element_type=jnp.float32
     ).astype(jnp.bfloat16)

time: 825 us -> 663 us (0.80)
  waiting for transfers between devices: 589 us -> 406 us
  other arithmetic: 12.9 us -> 65.7 us
  starting transfers between devices: 99.1 us -> 62.4 us
    all_gather x2 -> x0, waiting for transfers between devices: 281 us -> none  [the longest x1 147 us: on_device(): lax.all_gather(gelu_value(preact).astype(jnp.bfloat16), 'r', axis=0, tile...]
    ppermute x6 -> x20, waiting for transfers between devices: 246 us -> 373 us  [run_slot(): received.append(lax.ppermute(combined, 'r', pairs))]
    ppermute x6 -> x20, starting transfers between devices: 98.7 us -> 62 us  [run_slot(): received.append(lax.ppermute(combined, 'r', pairs))]
    select_n x0 -> x14, other arithmetic: none -> 36.2 us  [the longest x8 24.2 us: result(): pieces.append(lax.select_n(which.astype(jnp.int32), *cases))]
    all_gather x1, waiting for transfers between devices: 26.4 us -> 0.02 us  [on_device(): grad_rows = lax.all_gather(out_grad, 'p', axis=1, tiled=True)]
    reduce_scatter x1, waiting for transfers between devices: 31.2 us -> 4.97 us  [on_device(): lax.psum_scatter(back_part, 'p', scatter_dimension=1, tiled=True)]
    all_gather x1, waiting for transfers between devices: 1.87 us -> 27.2 us  [on_device(): x_rows = lax.all_gather(hidden_in, 'p', axis=1, tiled=True)]
    convert_element_type x0 -> x4, other arithmetic: none -> 19.3 us  [the longest x3 16.1 us: payload(): return (up.astype(jnp.bfloat16), down.astype(jnp.bfloat16))]
  transfers between devices with their start and end apart: 12 -> 24, of which waited for: 8 -> 17; matrix products, arithmetic and copies ran while one was open for 13% -> 18% of each run, Pallas kernels for 0% -> 0%
where the time goes in v3:
time: 663 us; the launch traced here: 655 us
  waiting for transfers between devices  406 us (61%)
  matrix products  84.3 us (13%)
  other arithmetic  65.7 us (10%)
  starting transfers between devices  62.4 us (9%)
  local copies, waits for them, and re-layouts  22.4 us (3%)
  between operations  14.5 us (2%)
    ppermute x20, waiting for transfers between devices, run_slot(): received.append(lax.ppermute(combined, 'r', pairs))  373 us
    ppermute x20, starting transfers between devices, run_slot(): received.append(lax.ppermute(combined, 'r', pairs))  62 us
    all_gather x1, waiting for transfers between devices, on_device(): x_rows = lax.all_gather(hidden_in, 'p', axis=1, tiled=True)  27.2 us
    select_n x8, other arithmetic, result(): pieces.append(lax.select_n(which.astype(jnp.int32), *cases))  24.2 us
    unnamed x59, local copies, waits for them, and re-layouts  20.5 us
    dot_general x1, matrix products, on_device(): lax.dot_general(pre_grad, up_tile, (((1,), (1,)), ((), ())), preferred_el...  17.1 us
    convert_element_type x3, other arithmetic, payload(): return (up.astype(jnp.bfloat16), down.astype(jnp.bfloat16))  16.1 us
    dot_general x1, matrix products, on_device(): jnp.dot(activation, down_tile, preferred_element_type=jnp.float32)  14.2 us
  transfers between devices with their start and end apart: 24, of which 17 were waited for; matrix products, arithmetic and copies ran while one was open for 18% of the time, Pallas kernels for 0%

profile of v3, /device:TPU:0, one launch (start us, length us, event | category | flops | bytes accessed | tf_op | source)
XLA Modules:
  0.0 655.2 jit_solution(402545911586698891)
XLA Ops:
  8.0 27.2 %all-gather.3.cloned.1.call-done = bf16[1024,1024]{1,0:T(8,128)(2,1)} async-done(((bf16[1024,256]{1,0:T(8,128)(2,1)}), bf16[1024,1024]{1,0:T(8,128)(2,1)}) %all-gather.3.cloned.1.call-update) | async-done | bytes 2097168 | tf_op jit(solution)/shard_map/all_gather | solution.py:118
  35.1 12.8 %fusion.8 = bf16[1024,4096]{1,0:T(8,128)(2,1)S(1)} fusion(bf16[1024,1024]{1,0:T(8,128)(2,1)} %all-gather.3.cloned.1.call-done, bf16[1,1024,4096]{2,1,0:T(8,128)(2,1)} %param.5), kind=kOutput, calls=%fused_computation.12 | convolution fusion | flops 8594128896 | bytes 18874368 | tf_op jit(solution)/shard_map/dot_general | solution.py:119
  49.9 2.1 copy-done.14
  51.9 4.7 collective-permute-start
  58.7 42.2 %collective-permute-done = bf16[256,4096]{1,0:T(8,128)(2,1)} collective-permute-done((bf16[256,4096]{1,0:T(8,128)(2,1)}, bf16[256,4096]{1,0:T(8,128)(2,1)}, u32[]{:S(2)}, u32[]{:S(2)}) %collective-permute-start) | collective-permute-done | bytes 2097184 | tf_op jit(solution)/shard_map/ppermute | solution.py:100
  100.9 6.2 fusion.29
  107.1 5.1 collective-permute-start.1
  114.3 42.6 %collective-permute-done.1 = bf16[256,4096]{1,0:T(8,128)(2,1)S(1)} collective-permute-done((bf16[256,4096]{1,0:T(8,128)(2,1)}, bf16[256,4096]{1,0:T(8,128)(2,1)S(1)}, u32[]{:S(2)}, u32[]{:S(2)}) %collective-permute-start.1) | collective-permute-done | bytes 2097184 | tf_op jit(solution)/shard_map/ppermute | solution.py:100
  156.9 6.0 fusion.28
  162.9 10.1 %collective-permute-start.2 = (bf16[256,4096]{1,0:T(8,128)(2,1)}, bf16[256,4096]{1,0:T(8,128)(2,1)S(1)}, u32[]{:S(2)}, u32[]{:S(2)}) collective-permute-start(bf16[256,4096]{1,0:T(8,128)(2,1)} %get-tuple-element.14), channel_id=1, source_target_pairs={{0,4},{4,8},{8,12},{1,5},{5,9},{9,13},{2,6},{6,10},{10,14},{3,7},{... | collective-permute-start | bytes 6291464 | tf_op jit(solution)/shard_map/ppermute | solution.py:100
  174.3 42.1 %collective-permute-done.2 = bf16[256,4096]{1,0:T(8,128)(2,1)S(1)} collective-permute-done((bf16[256,4096]{1,0:T(8,128)(2,1)}, bf16[256,4096]{1,0:T(8,128)(2,1)S(1)}, u32[]{:S(2)}, u32[]{:S(2)}) %collective-permute-start.2) | collective-permute-done | bytes 2097184 | tf_op jit(solution)/shard_map/ppermute | solution.py:100
  217.8 2.9 collective-permute-done.5
  220.7 3.3 multiply_convert_fusion
  225.3 6.1 collective-permute-start.6
  231.4 12.8 %fusion.11 = bf16[1024,4096]{1,0:T(8,128)(2,1)S(1)} fusion(bf16[1024,1024]{1,0:T(8,128)(2,1)} %all-gather.5.cloned.1.call-done, bf16[1,4096,1024]{2,1,0:T(8,128)(2,1)} %param.6), kind=kOutput, calls=%fused_computation.13 | convolution fusion | flops 8594128896 | bytes 18874368 | tf_op jit(solution)/shard_map/dot_general | solution.py:121
  244.3 26.2 %collective-permute-done.9 = bf16[256,4096]{1,0:T(8,128)(2,1)} collective-permute-done((bf16[256,4096]{1,0:T(8,128)(2,1)S(1)}, bf16[256,4096]{1,0:T(8,128)(2,1)}, u32[]{:S(2)}, u32[]{:S(2)}) %collective-permute-start.9) | collective-permute-done | bytes 2097184 | tf_op jit(solution)/shard_map/ppermute | solution.py:100
  271.6 4.2 bitcast_select_fusion.1
  275.8 6.4 collective-permute-start.7
  283.5 38.6 %collective-permute-done.7 = bf16[256,4096]{1,0:T(8,128)(2,1)} collective-permute-done((bf16[256,4096]{1,0:T(8,128)(2,1)}, bf16[256,4096]{1,0:T(8,128)(2,1)}, u32[]{:S(2)}, u32[]{:S(2)}) %collective-permute-start.7) | collective-permute-done | bytes 2097184 | tf_op jit(solution)/shard_map/ppermute | solution.py:100
  322.1 5.4 collective-permute-done.10
  327.5 4.5 fusion.30
  335.3 38.5 %collective-permute-done.8 = bf16[256,4096]{1,0:T(8,128)(2,1)S(1)} collective-permute-done((bf16[256,4096]{1,0:T(8,128)(2,1)S(1)}, bf16[256,4096]{1,0:T(8,128)(2,1)S(1)}, u32[]{:S(2)}, u32[]{:S(2)}) %collective-permute-start.8) | collective-permute-done | bytes 2097184 | tf_op jit(solution)/shard_map/ppermute | solution.py:100
  373.8 4.2 collective-permute-done.11
  378.1 3.9 fusion.22
  382.0 4.6 collective-permute-start.12
  388.0 3.4 select_select_fusion.6
  391.4 33.2 %collective-permute-done.12 = bf16[256,4096]{1,0:T(8,128)(2,1)} collective-permute-done((bf16[256,4096]{1,0:T(8,128)(2,1)}, bf16[256,4096]{1,0:T(8,128)(2,1)}, u32[]{:S(2)}, u32[]{:S(2)}) %collective-permute-start.12) | collective-permute-done | bytes 2097184 | tf_op jit(solution)/shard_map/ppermute | solution.py:100
  424.7 5.4 collective-permute-done.13
  430.1 5.8 fusion.19
  437.2 2.6 select_select_fusion.5
  439.9 5.8 collective-permute-start.14
  445.7 2.6 select_select_fusion.4
  448.4 31.9 %collective-permute-done.17 = bf16[256,4096]{1,0:T(8,128)(2,1)S(1)} collective-permute-done((bf16[256,4096]{1,0:T(8,128)(2,1)S(1)}, bf16[256,4096]{1,0:T(8,128)(2,1)S(1)}, u32[]{:S(2)}, u32[]{:S(2)}) %collective-permute-start.17) | collective-permute-done | bytes 2097184 | tf_op jit(solution)/shard_map/ppermute | solution.py:100
  485.2 2.6 select_select_fusion.7
  487.8 37.5 %collective-permute-done.18 = bf16[256,4096]{1,0:T(8,128)(2,1)S(1)} collective-permute-done((bf16[256,4096]{1,0:T(8,128)(2,1)S(1)}, bf16[256,4096]{1,0:T(8,128)(2,1)S(1)}, u32[]{:S(2)}, u32[]{:S(2)}) %collective-permute-start.18) | collective-permute-done | bytes 2097184 | tf_op jit(solution)/shard_map/ppermute | solution.py:100
  532.6 14.2 %fusion = f32[1024,1024]{1,0:T(8,128)} fusion(bf16[1,4096,1024]{2,1,0:T(8,128)(2,1)} %param.6, bf16[256,4096]{1,0:T(8,128)(2,1)S(1)} %select_select_fusion.4, bf16[256,4096]{1,0:T(8,128)(2,1)S(1)} %select_select_fusion.5, bf16[256,4096]{1,0:T(8,128)(2,1)S(1)} %select_select_fusion.6, bf16[256,4096]{1,0:T(8,128)(2,1)S(1)} %select_select_fusion.7), kind=kOutput, calls=%fused_computation.2 | convolution fusion | flops 8623489024 | bytes 20971520 | tf_op jit(solution)/shard_map/dot_general | solution.py:144
  547.1 21.0 %collective-permute-done.19 = bf16[256,4096]{1,0:T(8,128)(2,1)} collective-permute-done((bf16[256,4096]{1,0:T(8,128)(2,1)}, bf16[256,4096]{1,0:T(8,128)(2,1)}, u32[]{:S(2)}, u32[]{:S(2)}) %collective-permute-start.19) | collective-permute-done | bytes 2097184 | tf_op jit(solution)/shard_map/ppermute | solution.py:100
  568.1 3.7 select_select_fusion.2
  571.9 3.1 select_select_fusion.1
  574.9 3.0 select_select_fusion
  578.0 3.1 select_select_fusion.3
  581.0 17.1 %fusion.4 = f32[1024,1024]{1,0:T(8,128)} fusion(bf16[1,1024,4096]{2,1,0:T(8,128)(2,1)} %param.5, bf16[256,4096]{1,0:T(8,128)(2,1)} %select_select_fusion, bf16[256,4096]{1,0:T(8,128)(2,1)} %select_select_fusion.1, bf16[256,4096]{1,0:T(8,128)(2,1)} %select_select_fusion.2, bf16[256,4096]{1,0:T(8,128)(2,1)} %select_select_fusion.3), kind=kOutput, calls=%fused_computation.6 | convolution fusion | flops 8623489024 | bytes 20971520 | tf_op jit(solution)/shard_map/dot_general | solution.py:155
  599.7 13.9 %convert_bitcast_fusion = bf16[1,4096,1024]{2,1,0:T(8,128)(2,1)} fusion(bf16[1024,1024]{1,0:T(8,128)(2,1)} %all-gather.5.cloned.1.call-done, bf16[256,4096]{1,0:T(8,128)(2,1)} %copy-done.22, bf16[256,4096]{1,0:T(8,128)(2,1)} %copy-done.21, bf16[256,4096]{1,0:T(8,128)(2,1)S(1)} %copy-done.20, bf16[256,4096]{1,0:T(8,128)(2,1)} %copy-done.23), kind=kOutput, calls=%fused_computation.10 | convolution fusion | flops 8627683328 | bytes 18874368 | tf_op jit(solution)/shard_map/dot_general | solution.py:149
  613.6 13.5 %convert_bitcast_fusion.1 = bf16[1,1024,4096]{1,2,0:T(8,128)(2,1)} fusion(bf16[1024,1024]{1,0:T(8,128)(2,1)} %all-gather.3.cloned.1.call-done, bf16[256,4096]{1,0:T(8,128)(2,1)S(1)} %copy-done.26, bf16[256,4096]{1,0:T(8,128)(2,1)S(1)} %copy-done.25, bf16[256,4096]{1,0:T(8,128)(2,1)S(1)} %copy-done.24, bf16[256,4096]{1,0:T(8,128)(2,1)} %select_select_fusion.3), kind=kOutput, calls=%fused_computation.11 | convolution fusion | flops 8627683328 | bytes 18874368 | tf_op jit(solution)/shard_map/dot_general | solution.py:152
  627.1 12.0 %copy.8 = bf16[1,1024,4096]{2,1,0:T(8,128)(2,1)} copy(bf16[1,1024,4096]{1,2,0:T(8,128)(2,1)} %convert_bitcast_fusion.1) | data formatting | bytes 16777216
  639.1 2.2 add_convert_fusion.1
  641.3 5.0 reduce-scatter.5.cloned.1.call-done
  646.3 2.1 add_convert_fusion
  (91 shorter events, 33.0 us)
Async XLA Ops:
  7.2 28.0 %all-gather.3.cloned.1.call-start = ((), (), s32[]{:S(2)}) async-start(), calls=%async_computation.2 | async-start | bytes 2621440 | tf_op jit(solution)/shard_map/all_gather | solution.py:118
  7.9 223.5 %all-gather.5.cloned.1.call-start = ((), (), s32[]{:S(2)}) async-start(), calls=%async_computation.3 | async-start | bytes 2621440 | tf_op jit(solution)/shard_map/all_gather | solution.py:120
  47.9 4.0 copy-start.14
  51.9 49.0 %collective-permute-start = (bf16[256,4096]{1,0:T(8,128)(2,1)}, bf16[256,4096]{1,0:T(8,128)(2,1)}, u32[]{:S(2)}, u32[]{:S(2)}) collective-permute-start(bf16[256,4096]{1,0:T(8,128)(2,1)} %get-tuple-element.18), channel_id=1, source_target_pairs={{0,4},{1,5},{2,6},{3,7},{16,20},{17,21},{18,22},{19,23}} | collective-permute-start | bytes 6291464 | tf_op jit(solution)/shard_map/ppermute | solution.py:100
  56.7 44.3 %collective-permute-start.3 = (bf16[256,4096]{1,0:T(8,128)(2,1)S(1)}, bf16[256,4096]{1,0:T(8,128)(2,1)}, u32[]{:S(2)}, u32[]{:S(2)}) collective-permute-start(bf16[256,4096]{1,0:T(8,128)(2,1)S(1)} %get-tuple-element.19), channel_id=1, source_target_pairs={{12,8},{13,9},{14,10},{15,11},{28,24},{29,25},{30,26},{31,27}} | collective-permute-start | bytes 6291464 | tf_op jit(solution)/shard_map/ppermute | solution.py:100
  107.1 49.8 %collective-permute-start.1 = (bf16[256,4096]{1,0:T(8,128)(2,1)}, bf16[256,4096]{1,0:T(8,128)(2,1)S(1)}, u32[]{:S(2)}, u32[]{:S(2)}) collective-permute-start(bf16[256,4096]{1,0:T(8,128)(2,1)} %get-tuple-element.16), channel_id=1, source_target_pairs={{0,4},{4,8},{1,5},{5,9},{2,6},{6,10},{3,7},{7,11},{16,20},{20,24},... | collective-permute-start | bytes 6291464 | tf_op jit(solution)/shard_map/ppermute | solution.py:100
  112.2 44.7 %collective-permute-start.4 = (bf16[256,4096]{1,0:T(8,128)(2,1)}, bf16[256,4096]{1,0:T(8,128)(2,1)}, u32[]{:S(2)}, u32[]{:S(2)}) collective-permute-start(bf16[256,4096]{1,0:T(8,128)(2,1)} %get-tuple-element.17), channel_id=1, source_target_pairs={{8,4},{12,8},{9,5},{13,9},{10,6},{14,10},{11,7},{15,11},{24,20},{2... | collective-permute-start | bytes 6291464 | tf_op jit(solution)/shard_map/ppermute | solution.py:100
  162.9 53.5 %collective-permute-start.2 = (bf16[256,4096]{1,0:T(8,128)(2,1)}, bf16[256,4096]{1,0:T(8,128)(2,1)S(1)}, u32[]{:S(2)}, u32[]{:S(2)}) collective-permute-start(bf16[256,4096]{1,0:T(8,128)(2,1)} %get-tuple-element.14), channel_id=1, source_target_pairs={{0,4},{4,8},{8,12},{1,5},{5,9},{9,13},{2,6},{6,10},{10,14},{3,7},{... | collective-permute-start | bytes 6291464 | tf_op jit(solution)/shard_map/ppermute | solution.py:100
  173.0 47.7 %collective-permute-start.5 = (bf16[256,4096]{1,0:T(8,128)(2,1)}, bf16[256,4096]{1,0:T(8,128)(2,1)}, u32[]{:S(2)}, u32[]{:S(2)}) collective-permute-start(bf16[256,4096]{1,0:T(8,128)(2,1)} %get-tuple-element.15), channel_id=1, source_target_pairs={{4,0},{8,4},{12,8},{5,1},{9,5},{13,9},{6,2},{10,6},{14,10},{7,3},{... | collective-permute-start | bytes 6291464 | tf_op jit(solution)/shard_map/ppermute | solution.py:100
  174.3 464.8 %reduce-scatter.3.cloned.1.call-start = ((), (), s32[]{:S(2)}) async-start(), calls=%async_computation.4 | async-start | bytes 5242880 | tf_op jit(solution)/shard_map/reduce_scatter | solution.py:147
  224.0 46.6 %collective-permute-start.9 = (bf16[256,4096]{1,0:T(8,128)(2,1)S(1)}, bf16[256,4096]{1,0:T(8,128)(2,1)}, u32[]{:S(2)}, u32[]{:S(2)}) collective-permute-start(bf16[256,4096]{1,0:T(8,128)(2,1)S(1)} %multiply_convert_fusion), channel_id=1, source_target_pairs={{4,0},{8,4},{12,8},{5,1},{9,5},{13,9},{6,2},{10,6},{14,10},{7,3},{... | collective-permute-start | bytes 6291464 | tf_op jit(solution)/shard_map/ppermute | solution.py:100
  225.3 46.4 %collective-permute-start.6 = (bf16[256,4096]{1,0:T(8,128)(2,1)S(1)}, bf16[256,4096]{1,0:T(8,128)(2,1)}, u32[]{:S(2)}, u32[]{:S(2)}) collective-permute-start(bf16[256,4096]{1,0:T(8,128)(2,1)S(1)} %multiply_convert_fusion), channel_id=1, source_target_pairs={{0,4},{4,8},{8,12},{1,5},{5,9},{9,13},{2,6},{6,10},{10,14},{3,7},{... | collective-permute-start | bytes 6291464 | tf_op jit(solution)/shard_map/ppermute | solution.py:100
  244.3 31.5 %copy-start.15 = (bf16[1024,4096]{1,0:T(8,128)(2,1)}, bf16[1024,4096]{1,0:T(8,128)(2,1)S(1)}, u32[]{:S(2)}) copy-start(bf16[1024,4096]{1,0:T(8,128)(2,1)S(1)} %fusion.11) | copy-start | bytes 25165828
  275.8 46.3 %collective-permute-start.7 = (bf16[256,4096]{1,0:T(8,128)(2,1)}, bf16[256,4096]{1,0:T(8,128)(2,1)}, u32[]{:S(2)}, u32[]{:S(2)}) collective-permute-start(bf16[256,4096]{1,0:T(8,128)(2,1)} %get-tuple-element.12), channel_id=1, source_target_pairs={{4,8},{8,12},{0,4},{5,9},{9,13},{1,5},{6,10},{10,14},{2,6},{7,11},... | collective-permute-start | bytes 6291464 | tf_op jit(solution)/shard_map/ppermute | solution.py:100
  282.2 45.3 %collective-permute-start.10 = (bf16[256,4096]{1,0:T(8,128)(2,1)}, bf16[256,4096]{1,0:T(8,128)(2,1)}, u32[]{:S(2)}, u32[]{:S(2)}) collective-permute-start(bf16[256,4096]{1,0:T(8,128)(2,1)} %get-tuple-element.13), channel_id=1, source_target_pairs={{4,0},{8,4},{12,8},{5,1},{9,5},{13,9},{6,2},{10,6},{14,10},{7,3},{... | collective-permute-start | bytes 6291464 | tf_op jit(solution)/shard_map/ppermute | solution.py:100
  327.5 50.6 %copy-start.16 = (bf16[1024,4096]{1,0:T(8,128)(2,1)S(1)}, bf16[1024,4096]{1,0:T(8,128)(2,1)}, u32[]{:S(2)}) copy-start(bf16[1024,4096]{1,0:T(8,128)(2,1)} %copy-done.15) | copy-start | bytes 25165828
  332.0 41.8 %collective-permute-start.8 = (bf16[256,4096]{1,0:T(8,128)(2,1)S(1)}, bf16[256,4096]{1,0:T(8,128)(2,1)S(1)}, u32[]{:S(2)}, u32[]{:S(2)}) collective-permute-start(bf16[256,4096]{1,0:T(8,128)(2,1)S(1)} %get-tuple-element.10), channel_id=1, source_target_pairs={{8,12},{0,4},{4,8},{9,13},{1,5},{5,9},{10,14},{2,6},{6,10},{11,15}... | collective-permute-start | bytes 6291464 | tf_op jit(solution)/shard_map/ppermute | solution.py:100
  334.0 44.1 %collective-permute-start.11 = (bf16[256,4096]{1,0:T(8,128)(2,1)S(1)}, bf16[256,4096]{1,0:T(8,128)(2,1)S(1)}, u32[]{:S(2)}, u32[]{:S(2)}) collective-permute-start(bf16[256,4096]{1,0:T(8,128)(2,1)S(1)} %get-tuple-element.11), channel_id=1, source_target_pairs={{4,0},{8,4},{12,8},{5,1},{9,5},{13,9},{6,2},{10,6},{14,10},{7,3},{... | collective-permute-start | bytes 6291464 | tf_op jit(solution)/shard_map/ppermute | solution.py:100
  373.8 8.2 %copy-start = (bf16[256,4096]{1,0:T(8,128)(2,1)}, bf16[256,4096]{1,0:T(8,128)(2,1)S(1)}, u32[]{:S(2)}) copy-start(bf16[256,4096]{1,0:T(8,128)(2,1)S(1)} %collective-permute-done.8) | copy-start | bytes 6291460
  378.1 3.9 copy-start.2
  382.0 42.7 %collective-permute-start.12 = (bf16[256,4096]{1,0:T(8,128)(2,1)}, bf16[256,4096]{1,0:T(8,128)(2,1)}, u32[]{:S(2)}, u32[]{:S(2)}) collective-permute-start(bf16[256,4096]{1,0:T(8,128)(2,1)} %get-tuple-element.8), channel_id=1, source_target_pairs={{0,4},{4,8},{8,12},{1,5},{5,9},{9,13},{2,6},{6,10},{10,14},{3,7},{... | collective-permute-start | bytes 6291464 | tf_op jit(solution)/shard_map/ppermute | solution.py:100
  386.6 43.5 %collective-permute-start.13 = (bf16[256,4096]{1,0:T(8,128)(2,1)}, bf16[256,4096]{1,0:T(8,128)(2,1)}, u32[]{:S(2)}, u32[]{:S(2)}) collective-permute-start(bf16[256,4096]{1,0:T(8,128)(2,1)} %get-tuple-element.9), channel_id=1, source_target_pairs={{4,0},{8,4},{12,8},{5,1},{9,5},{13,9},{6,2},{10,6},{14,10},{7,3},{... | collective-permute-start | bytes 6291464 | tf_op jit(solution)/shard_map/ppermute | solution.py:100
  388.0 42.1 %copy-start.18 = (bf16[256,4096]{1,0:T(8,128)(2,1)S(1)}, bf16[256,4096]{1,0:T(8,128)(2,1)}, u32[]{:S(2)}) copy-start(bf16[256,4096]{1,0:T(8,128)(2,1)} %copy-done.17) | copy-start | bytes 6291460
  391.4 141.2 %copy-start.19 = (bf16[256,4096]{1,0:T(8,128)(2,1)}, bf16[256,4096]{1,0:T(8,128)(2,1)S(1)}, u32[]{:S(2)}) copy-start(bf16[256,4096]{1,0:T(8,128)(2,1)S(1)} %select_select_fusion.6) | copy-start | bytes 6291460
  391.4 45.8 %copy-start.1 = (bf16[256,4096]{1,0:T(8,128)(2,1)S(1)}, bf16[256,4096]{1,0:T(8,128)(2,1)}, u32[]{:S(2)}) copy-start(bf16[256,4096]{1,0:T(8,128)(2,1)} %copy-done) | copy-start | bytes 6291460
  391.4 45.8 %copy-start.3 = (bf16[256,4096]{1,0:T(8,128)(2,1)S(1)}, bf16[256,4096]{1,0:T(8,128)(2,1)}, u32[]{:S(2)}) copy-start(bf16[256,4096]{1,0:T(8,128)(2,1)} %copy-done.2) | copy-start | bytes 6291460
  435.9 4.0 copy-start.12
  435.9 44.4 %collective-permute-start.17 = (bf16[256,4096]{1,0:T(8,128)(2,1)S(1)}, bf16[256,4096]{1,0:T(8,128)(2,1)S(1)}, u32[]{:S(2)}, u32[]{:S(2)}) collective-permute-start(bf16[256,4096]{1,0:T(8,128)(2,1)S(1)} %fusion.19), channel_id=1, source_target_pairs={{4,0},{8,4},{12,8},{5,1},{9,5},{13,9},{6,2},{10,6},{14,10},{7,3},{... | collective-permute-start | bytes 6291464 | tf_op jit(solution)/shard_map/ppermute | solution.py:100
  439.9 92.7 %copy-start.21 = (bf16[256,4096]{1,0:T(8,128)(2,1)}, bf16[256,4096]{1,0:T(8,128)(2,1)S(1)}, u32[]{:S(2)}) copy-start(bf16[256,4096]{1,0:T(8,128)(2,1)S(1)} %select_select_fusion.5) | copy-start | bytes 6291460
  439.9 43.1 %collective-permute-start.14 = (bf16[256,4096]{1,0:T(8,128)(2,1)S(1)}, bf16[256,4096]{1,0:T(8,128)(2,1)S(1)}, u32[]{:S(2)}, u32[]{:S(2)}) collective-permute-start(bf16[256,4096]{1,0:T(8,128)(2,1)S(1)} %fusion.19), channel_id=1, source_target_pairs={{0,4},{4,8},{8,12},{1,5},{5,9},{9,13},{2,6},{6,10},{10,14},{3,7},{... | collective-permute-start | bytes 6291464 | tf_op jit(solution)/shard_map/ppermute | solution.py:100
  448.4 84.2 %copy-start.22 = (bf16[256,4096]{1,0:T(8,128)(2,1)}, bf16[256,4096]{1,0:T(8,128)(2,1)S(1)}, u32[]{:S(2)}) copy-start(bf16[256,4096]{1,0:T(8,128)(2,1)S(1)} %select_select_fusion.4) | copy-start | bytes 6291460
  481.7 43.6 %collective-permute-start.18 = (bf16[256,4096]{1,0:T(8,128)(2,1)S(1)}, bf16[256,4096]{1,0:T(8,128)(2,1)S(1)}, u32[]{:S(2)}, u32[]{:S(2)}) collective-permute-start(bf16[256,4096]{1,0:T(8,128)(2,1)S(1)} %broadcast_select_fusion.8), channel_id=1, source_target_pairs={{4,0},{8,4},{5,1},{9,5},{6,2},{10,6},{7,3},{11,7},{20,16},{24,20},... | collective-permute-start | bytes 6291464 | tf_op jit(solution)/shard_map/ppermute | solution.py:100
  484.4 44.2 %collective-permute-start.15 = (bf16[256,4096]{1,0:T(8,128)(2,1)S(1)}, bf16[256,4096]{1,0:T(8,128)(2,1)S(1)}, u32[]{:S(2)}, u32[]{:S(2)}) collective-permute-start(bf16[256,4096]{1,0:T(8,128)(2,1)S(1)} %broadcast_select_fusion.10), channel_id=1, source_target_pairs={{4,8},{8,12},{5,9},{9,13},{6,10},{10,14},{7,11},{11,15},{20,24},{2... | collective-permute-start | bytes 6291464 | tf_op jit(solution)/shard_map/ppermute | solution.py:100
  487.8 44.8 %copy-start.23 = (bf16[256,4096]{1,0:T(8,128)(2,1)}, bf16[256,4096]{1,0:T(8,128)(2,1)S(1)}, u32[]{:S(2)}) copy-start(bf16[256,4096]{1,0:T(8,128)(2,1)S(1)} %select_select_fusion.7) | copy-start | bytes 6291460
  527.3 40.8 %collective-permute-start.19 = (bf16[256,4096]{1,0:T(8,128)(2,1)}, bf16[256,4096]{1,0:T(8,128)(2,1)}, u32[]{:S(2)}, u32[]{:S(2)}) collective-permute-start(bf16[256,4096]{1,0:T(8,128)(2,1)} %broadcast_select_fusion), channel_id=1, source_target_pairs={{4,0},{5,1},{6,2},{7,3},{20,16},{21,17},{22,18},{23,19}} | collective-permute-start | bytes 6291464 | tf_op jit(solution)/shard_map/ppermute | solution.py:100
  528.6 2.0 copy-start.10
  530.6 37.5 %collective-permute-start.16 = (bf16[256,4096]{1,0:T(8,128)(2,1)}, bf16[256,4096]{1,0:T(8,128)(2,1)}, u32[]{:S(2)}, u32[]{:S(2)}) collective-permute-start(bf16[256,4096]{1,0:T(8,128)(2,1)} %broadcast_select_fusion.6), channel_id=1, source_target_pairs={{8,12},{9,13},{10,14},{11,15},{24,28},{25,29},{26,30},{27,31}} | collective-permute-start | bytes 6291464 | tf_op jit(solution)/shard_map/ppermute | solution.py:100
  546.8 21.3 %copy-start.5 = (bf16[256,4096]{1,0:T(8,128)(2,1)S(1)}, bf16[256,4096]{1,0:T(8,128)(2,1)}, u32[]{:S(2)}) copy-start(bf16[256,4096]{1,0:T(8,128)(2,1)} %copy-done.4) | copy-start | bytes 6291460
  546.9 99.4 %reduce-scatter.5.cloned.1.call-start = ((), (), s32[]{:S(2)}) async-start(), calls=%async_computation.5 | async-start | bytes 5242880 | tf_op jit(solution)/shard_map/reduce_scatter | solution.py:160
  547.1 24.7 %copy-start.7 = (bf16[256,4096]{1,0:T(8,128)(2,1)S(1)}, bf16[256,4096]{1,0:T(8,128)(2,1)}, u32[]{:S(2)}) copy-start(bf16[256,4096]{1,0:T(8,128)(2,1)} %copy-done.6) | copy-start | bytes 6291460
  547.1 24.7 %copy-start.9 = (bf16[256,4096]{1,0:T(8,128)(2,1)S(1)}, bf16[256,4096]{1,0:T(8,128)(2,1)}, u32[]{:S(2)}) copy-start(bf16[256,4096]{1,0:T(8,128)(2,1)} %copy-done.8) | copy-start | bytes 6291460
  547.1 24.7 %copy-start.11 = (bf16[256,4096]{1,0:T(8,128)(2,1)S(1)}, bf16[256,4096]{1,0:T(8,128)(2,1)}, u32[]{:S(2)}) copy-start(bf16[256,4096]{1,0:T(8,128)(2,1)} %copy-done.10) | copy-start | bytes 6291460
  547.1 24.7 %copy-start.13 = (bf16[256,4096]{1,0:T(8,128)(2,1)S(1)}, bf16[256,4096]{1,0:T(8,128)(2,1)}, u32[]{:S(2)}) copy-start(bf16[256,4096]{1,0:T(8,128)(2,1)} %copy-done.12) | copy-start | bytes 6291460
  599.7 13.9 %copy-start.24 = (bf16[256,4096]{1,0:T(8,128)(2,1)S(1)}, bf16[256,4096]{1,0:T(8,128)(2,1)}, u32[]{:S(2)}) copy-start(bf16[256,4096]{1,0:T(8,128)(2,1)} %select_select_fusion.2) | copy-start | bytes 6291460
  599.7 13.9 %copy-start.25 = (bf16[256,4096]{1,0:T(8,128)(2,1)S(1)}, bf16[256,4096]{1,0:T(8,128)(2,1)}, u32[]{:S(2)}) copy-start(bf16[256,4096]{1,0:T(8,128)(2,1)} %select_select_fusion.1) | copy-start | bytes 6291460
  599.7 13.9 %copy-start.26 = (bf16[256,4096]{1,0:T(8,128)(2,1)S(1)}, bf16[256,4096]{1,0:T(8,128)(2,1)}, u32[]{:S(2)}) copy-start(bf16[256,4096]{1,0:T(8,128)(2,1)} %select_select_fusion) | copy-start | bytes 6291460
  627.1 12.0 %copy-start.27 = (bf16[1024,256]{1,0:T(8,128)(2,1)S(1)}, bf16[1024,256]{1,0:T(8,128)(2,1)}, u32[]{:S(2)}) copy-start(bf16[1024,256]{1,0:T(8,128)(2,1)} %param.4) | copy-start | bytes 1572868
  639.1 7.2 %copy-start.28 = (bf16[1024,256]{1,0:T(8,128)(2,1)S(1)}, bf16[1024,256]{1,0:T(8,128)(2,1)}, u32[]{:S(2)}) copy-start(bf16[1024,256]{1,0:T(8,128)(2,1)} %param.7) | copy-start | bytes 1572868
  (5 other events, 7.7 us)
Sparse Core Ops, SparseCore 0:
  9.6 25.5 all-gather.2
  174.4 22.1 all-gather.4
  547.0 45.8 reduce-scatter.2
  598.3 47.9 reduce-scatter.4

commit v4 on v3

--- a/solution.py
+++ b/solution.py
@@ -123,8 +123,13 @@
     ).astype(jnp.bfloat16)
 
     up_sum = LineReduce(up_terms)
+    if count > 1:
+        run_slot([(up_sum, 0)])
+        up_sum.up_in, up_sum.down_in, grad_terms = lax.optimization_barrier(
+            (up_sum.up_in, up_sum.down_in, grad_terms)
+        )
     grad_sum = LineReduce(grad_terms)
-    for step in range(count - 1):
+    for step in range(1, count - 1):
         run_slot([(up_sum, step)])
     preact = up_sum.result()
     act_gather = LineGather(gelu_value(preact).astype(jnp.bfloat16))
@@ -132,23 +137,25 @@
         run_slot([(act_gather, 0)])
     for step in range(1, count - 1):
         run_slot([(act_gather, step), (grad_sum, step - 1)])
+    activation = act_gather.result()
+    out_part = jnp.dot(activation, down_tile, preferred_element_type=jnp.float32)
+    out_sum = lax.psum_scatter(out_part, "p", scatter_dimension=1, tiled=True)
+    grad_down = lax.dot_general(
+        activation, grad_rows, (((0,), (0,)), ((), ())), preferred_element_type=jnp.float32
+    ).astype(jnp.bfloat16)
     if count > 1:
         run_slot([(grad_sum, count - 2)])
     act_grad = grad_sum.result()
     pre_gather = LineGather((act_grad * gelu_slope(preact)).astype(jnp.bfloat16))
     for step in range(count - 1):
         run_slot([(pre_gather, step)])
-    activation = act_gather.result()
+        if step == min(1, count - 2):
+            pre_gather.up_cur, pre_gather.down_cur, out_sum, grad_down = lax.optimization_barrier(
+                (pre_gather.up_cur, pre_gather.down_cur, out_sum, grad_down)
+            )
+            pre_gather.ups[-1], pre_gather.downs[-1] = pre_gather.up_cur, pre_gather.down_cur
     pre_grad = pre_gather.result()
-
-    out_part = jnp.dot(activation, down_tile, preferred_element_type=jnp.float32)
-    block_out = (
-        hidden_in.astype(jnp.float32)
-        + lax.psum_scatter(out_part, "p", scatter_dimension=1, tiled=True)
-    ).astype(jnp.bfloat16)
-    grad_down = lax.dot_general(
-        activation, grad_rows, (((0,), (0,)), ((), ())), preferred_element_type=jnp.float32
-    ).astype(jnp.bfloat16)
+    block_out = (hidden_in.astype(jnp.float32) + out_sum).astype(jnp.bfloat16)
     grad_up = lax.dot_general(
         x_rows, pre_grad, (((0,), (0,)), ((), ())), preferred_element_type=jnp.float32
     ).astype(jnp.bfloat16)

time: 663 us -> 660 us (level)
  waiting for transfers between devices: 406 us -> 383 us
  starting transfers between devices: 62.4 us -> 73.3 us
    ppermute x20, waiting for transfers between devices: 373 us -> 340 us  [run_slot(): received.append(lax.ppermute(combined, 'r', pairs))]
    ppermute x20, starting transfers between devices: 62 us -> 73.1 us  [run_slot(): received.append(lax.ppermute(combined, 'r', pairs))]
    reduce_scatter x1, waiting for transfers between devices: 4.97 us -> 13.7 us  [on_device(): lax.psum_scatter(back_part, 'p', scatter_dimension=1, tiled=True)]
    unnamed x59 -> x43, local copies, waits for them, and re-layouts: 20.5 us -> 21.1 us
  transfers between devices with their start and end apart: 24 -> 24, of which waited for: 17 -> 18; matrix products, arithmetic and copies ran while one was open for 18% -> 17% of each run, Pallas kernels for 0% -> 0%
where the time goes in v4:
time: 660 us; the launch traced here: 651 us
  waiting for transfers between devices  383 us (58%)
  matrix products  85.8 us (13%)
  starting transfers between devices  73.3 us (11%)
  other arithmetic  72 us (11%)
  local copies, waits for them, and re-layouts  23.1 us (4%)
  between operations  14.4 us (2%)
    ppermute x20, waiting for transfers between devices, run_slot(): received.append(lax.ppermute(combined, 'r', pairs))  340 us
    ppermute x20, starting transfers between devices, run_slot(): received.append(lax.ppermute(combined, 'r', pairs))  73.1 us
    all_gather x1, waiting for transfers between devices, on_device(): x_rows = lax.all_gather(hidden_in, 'p', axis=1, tiled=True)  26.4 us
    select_n x8, other arithmetic, result(): pieces.append(lax.select_n(which.astype(jnp.int32), *cases))  23.8 us
    unnamed x43, local copies, waits for them, and re-layouts  21.1 us
    dot_general x1, matrix products, on_device(): lax.dot_general(pre_grad, up_tile, (((1,), (1,)), ((), ())), preferred_el...  17.1 us
    convert_element_type x3, other arithmetic, payload(): return (up.astype(jnp.bfloat16), down.astype(jnp.bfloat16))  15.7 us
    dot_general x1, matrix products, on_device(): lax.dot_general(grad_rows, down_tile, (((1,), (1,)), ((), ())), preferred...  14.8 us
  transfers between devices with their start and end apart: 24, of which 18 were waited for; matrix products, arithmetic and copies ran while one was open for 17% of the time, Pallas kernels for 0%

profile of v4, /device:TPU:0, one launch (start us, length us, event | category | flops | bytes accessed | tf_op | source)
XLA Modules:
  0.0 651.0 jit_solution(15060408806701086762)
XLA Ops:
  8.7 26.4 %all-gather.3.cloned.1.call-done = bf16[1024,1024]{1,0:T(8,128)(2,1)} async-done(((bf16[1024,256]{1,0:T(8,128)(2,1)}), bf16[1024,1024]{1,0:T(8,128)(2,1)}) %all-gather.3.cloned.1.call-update) | async-done | bytes 2097168 | tf_op jit(solution)/shard_map/all_gather | solution.py:118
  35.1 12.8 %fusion.8 = bf16[1024,4096]{1,0:T(8,128)(2,1)S(1)} fusion(bf16[1024,1024]{1,0:T(8,128)(2,1)} %all-gather.3.cloned.1.call-done, bf16[1,1024,4096]{2,1,0:T(8,128)(2,1)} %param.5), kind=kOutput, calls=%fused_computation.11 | convolution fusion | flops 8594128896 | bytes 18874368 | tf_op jit(solution)/shard_map/dot_general | solution.py:119
  51.9 4.7 collective-permute-start
  59.6 14.8 %fusion.11 = bf16[1024,4096]{1,0:T(8,128)(2,1)} fusion(bf16[1024,1024]{1,0:T(8,128)(2,1)} %all-gather.5.cloned.1.call-done, bf16[1,4096,1024]{2,1,0:T(8,128)(2,1)} %param.6), kind=kOutput, calls=%fused_computation.12 | convolution fusion | flops 8594128896 | bytes 18874368 | tf_op jit(solution)/shard_map/dot_general | solution.py:121
  74.4 26.5 %collective-permute-done = bf16[256,4096]{1,0:T(8,128)(2,1)} collective-permute-done((bf16[256,4096]{1,0:T(8,128)(2,1)}, bf16[256,4096]{1,0:T(8,128)(2,1)}, u32[]{:S(2)}, u32[]{:S(2)}) %collective-permute-start) | collective-permute-done | bytes 2097184 | tf_op jit(solution)/shard_map/ppermute | solution.py:100
  101.5 2.8 copy-done.7
  104.3 3.5 fusion.29
  107.8 5.1 collective-permute-start.2
  114.9 42.7 %collective-permute-done.2 = bf16[256,4096]{1,0:T(8,128)(2,1)S(1)} collective-permute-done((bf16[256,4096]{1,0:T(8,128)(2,1)}, bf16[256,4096]{1,0:T(8,128)(2,1)S(1)}, u32[]{:S(2)}, u32[]{:S(2)}) %collective-permute-start.2) | collective-permute-done | bytes 2097184 | tf_op jit(solution)/shard_map/ppermute | solution.py:100
  157.6 6.0 fusion.28
  165.2 9.8 %collective-permute-start.3 = (bf16[256,4096]{1,0:T(8,128)(2,1)}, bf16[256,4096]{1,0:T(8,128)(2,1)}, u32[]{:S(2)}, u32[]{:S(2)}) collective-permute-start(bf16[256,4096]{1,0:T(8,128)(2,1)} %get-tuple-element.28), channel_id=1, source_target_pairs={{0,4},{4,8},{8,12},{1,5},{5,9},{9,13},{2,6},{6,10},{10,14},{3,7},{... | collective-permute-start | bytes 6291464 | tf_op jit(solution)/shard_map/ppermute | solution.py:100
  175.0 40.9 %collective-permute-done.5 = bf16[256,4096]{1,0:T(8,128)(2,1)S(1)} collective-permute-done((bf16[256,4096]{1,0:T(8,128)(2,1)}, bf16[256,4096]{1,0:T(8,128)(2,1)S(1)}, u32[]{:S(2)}, u32[]{:S(2)}) %collective-permute-start.5) | collective-permute-done | bytes 2097184 | tf_op jit(solution)/shard_map/ppermute | solution.py:100
  217.3 3.3 multiply_convert_fusion
  220.5 6.1 collective-permute-start.6
  227.9 39.7 %collective-permute-done.6 = bf16[256,4096]{1,0:T(8,128)(2,1)} collective-permute-done((bf16[256,4096]{1,0:T(8,128)(2,1)S(1)}, bf16[256,4096]{1,0:T(8,128)(2,1)}, u32[]{:S(2)}, u32[]{:S(2)}) %collective-permute-start.6) | collective-permute-done | bytes 2097184 | tf_op jit(solution)/shard_map/ppermute | solution.py:100
  267.6 5.5 collective-permute-done.10
  273.2 5.3 bitcast_select_fusion.1
  278.5 4.0 collective-permute-start.7
  283.8 38.5 %collective-permute-done.7 = bf16[256,4096]{1,0:T(8,128)(2,1)} collective-permute-done((bf16[256,4096]{1,0:T(8,128)(2,1)}, bf16[256,4096]{1,0:T(8,128)(2,1)}, u32[]{:S(2)}, u32[]{:S(2)}) %collective-permute-start.7) | collective-permute-done | bytes 2097184 | tf_op jit(solution)/shard_map/ppermute | solution.py:100
  322.3 5.5 collective-permute-done.11
  327.8 5.7 fusion.30
  333.5 2.8 collective-permute-start.8
  337.6 37.4 %collective-permute-done.8 = bf16[256,4096]{1,0:T(8,128)(2,1)} collective-permute-done((bf16[256,4096]{1,0:T(8,128)(2,1)}, bf16[256,4096]{1,0:T(8,128)(2,1)}, u32[]{:S(2)}, u32[]{:S(2)}) %collective-permute-start.8) | collective-permute-done | bytes 2097184 | tf_op jit(solution)/shard_map/ppermute | solution.py:100
  375.1 5.4 collective-permute-done.12
  380.5 6.2 fusion.23
  388.0 5.9 collective-permute-start.9
  393.8 3.3 select_select_fusion.4
  397.1 4.0 select_select_fusion.5
  401.1 4.0 select_select_fusion.6
  405.1 4.0 select_select_fusion.7
  410.5 14.2 %fusion = f32[1024,1024]{1,0:T(8,128)} fusion(bf16[1,4096,1024]{2,1,0:T(8,128)(2,1)} %param.6, bf16[256,4096]{1,0:T(8,128)(2,1)S(1)} %select_select_fusion.4, bf16[256,4096]{1,0:T(8,128)(2,1)S(1)} %select_select_fusion.5, bf16[256,4096]{1,0:T(8,128)(2,1)S(1)} %select_select_fusion.6, bf16[256,4096]{1,0:T(8,128)(2,1)S(1)} %select_select_fusion.7), kind=kOutput, calls=%fused_computation.2 | convolution fusion | flops 8623489024 | bytes 20971520 | tf_op jit(solution)/shard_map/dot_general | solution.py:141
  424.7 5.2 collective-permute-done.13
  431.1 5.7 fusion.19
  436.8 5.2 collective-permute-start.14
  443.3 36.0 %collective-permute-done.14 = bf16[256,4096]{1,0:T(8,128)(2,1)S(1)} collective-permute-done((bf16[256,4096]{1,0:T(8,128)(2,1)S(1)}, bf16[256,4096]{1,0:T(8,128)(2,1)S(1)}, u32[]{:S(2)}, u32[]{:S(2)}) %collective-permute-start.14) | collective-permute-done | bytes 2097184 | tf_op jit(solution)/shard_map/ppermute | solution.py:100
  480.8 2.1 collective-permute-start.15
  485.6 12.8 %collective-permute-start.17 = (bf16[256,4096]{1,0:T(8,128)(2,1)}, bf16[256,4096]{1,0:T(8,128)(2,1)}, u32[]{:S(2)}, u32[]{:S(2)}) collective-permute-start(bf16[256,4096]{1,0:T(8,128)(2,1)} %broadcast_select_fusion.2), channel_id=1, source_target_pairs={{4,0},{8,4},{5,1},{9,5},{6,2},{10,6},{7,3},{11,7},{20,16},{24,20},... | collective-permute-start | bytes 6291464 | tf_op jit(solution)/shard_map/ppermute | solution.py:100
  498.4 13.3 %convolution_convert_fusion = bf16[4096,1024]{1,0:T(8,128)(2,1)} fusion(bf16[1024,1024]{1,0:T(8,128)(2,1)} %all-gather.5.cloned.1.call-done, bf16[256,4096]{1,0:T(8,128)(2,1)S(1)} %copy-done.11, bf16[256,4096]{1,0:T(8,128)(2,1)S(1)} %copy-done.13, bf16[256,4096]{1,0:T(8,128)(2,1)S(1)} %copy-done.15, bf16[256,4096]{1,0:T(8,128)(2,1)} %copy-done.16), kind=kOutput, calls=%fused_computation.13 | convolution fusion | flops 8627683328 | bytes 18874368 | tf_op jit(solution)/shard_map/dot_general | solution.py:143
  513.2 18.5 %collective-permute-done.17 = bf16[256,4096]{1,0:T(8,128)(2,1)} collective-permute-done((bf16[256,4096]{1,0:T(8,128)(2,1)}, bf16[256,4096]{1,0:T(8,128)(2,1)}, u32[]{:S(2)}, u32[]{:S(2)}) %collective-permute-start.17) | collective-permute-done | bytes 2097184 | tf_op jit(solution)/shard_map/ppermute | solution.py:100
  531.7 3.0 broadcast_select_fusion.6
  537.3 36.4 %collective-permute-done.19 = bf16[256,4096]{1,0:T(8,128)(2,1)S(1)} collective-permute-done((bf16[256,4096]{1,0:T(8,128)(2,1)}, bf16[256,4096]{1,0:T(8,128)(2,1)S(1)}, u32[]{:S(2)}, u32[]{:S(2)}) %collective-permute-start.19) | collective-permute-done | bytes 2097184 | tf_op jit(solution)/shard_map/ppermute | solution.py:100
  573.7 3.5 select_select_fusion
  582.3 17.1 %fusion.4 = f32[1024,1024]{1,0:T(8,128)} fusion(bf16[1,1024,4096]{2,1,0:T(8,128)(2,1)} %param.5, bf16[256,4096]{1,0:T(8,128)(2,1)} %select_select_fusion, bf16[256,4096]{1,0:T(8,128)(2,1)} %select_select_fusion.1, bf16[256,4096]{1,0:T(8,128)(2,1)} %select_select_fusion.2, bf16[256,4096]{1,0:T(8,128)(2,1)} %select_select_fusion.3), kind=kOutput, calls=%fused_computation.6 | convolution fusion | flops 8623489024 | bytes 20971520 | tf_op jit(solution)/shard_map/dot_general | solution.py:162
  600.4 2.3 add_convert_fusion.1
  602.7 13.7 %convert_bitcast_fusion = bf16[1,1024,4096]{1,2,0:T(8,128)(2,1)} fusion(bf16[1024,1024]{1,0:T(8,128)(2,1)} %all-gather.3.cloned.1.call-done, bf16[256,4096]{1,0:T(8,128)(2,1)S(1)} %copy-done.17, bf16[256,4096]{1,0:T(8,128)(2,1)S(1)} %copy-done.18, bf16[256,4096]{1,0:T(8,128)(2,1)} %select_select_fusion.2, bf16[256,4096]{1,0:T(8,128)(2,1)} %select_select_fusion.3), kind=kOutput, calls=%fused_computation.10 | convolution fusion | flops 8627683328 | bytes 18874368 | tf_op jit(solution)/shard_map/dot_general | solution.py:159
  616.4 12.1 %copy.8 = bf16[1,1024,4096]{2,1,0:T(8,128)(2,1)} copy(bf16[1,1024,4096]{1,2,0:T(8,128)(2,1)} %convert_bitcast_fusion) | data formatting | bytes 16777216
  628.5 13.7 %reduce-scatter.5.cloned.1.call-done = f32[1024,256]{1,0:T(8,128)} async-done(((f32[1024,1024]{1,0:T(8,128)}), f32[1024,256]{1,0:T(8,128)}) %reduce-scatter.5.cloned.1.call-update) | async-done | bytes 1048592 | tf_op jit(solution)/shard_map/reduce_scatter | solution.py:167
  642.2 2.1 add_convert_fusion
  (77 shorter events, 37.1 us)
Async XLA Ops:
  7.2 28.0 %all-gather.3.cloned.1.call-start = ((), (), s32[]{:S(2)}) async-start(), calls=%async_computation.2 | async-start | bytes 2621440 | tf_op jit(solution)/shard_map/all_gather | solution.py:118
  7.9 51.7 %all-gather.5.cloned.1.call-start = ((), (), s32[]{:S(2)}) async-start(), calls=%async_computation.3 | async-start | bytes 2621440 | tf_op jit(solution)/shard_map/all_gather | solution.py:120
  8.6 526.2 %reduce-scatter.3.cloned.1.call-start = ((), (), s32[]{:S(2)}) async-start(), calls=%async_computation.4 | async-start | bytes 5242880 | tf_op jit(solution)/shard_map/reduce_scatter | solution.py:142
  47.9 4.0 copy-start.6
  51.9 49.0 %collective-permute-start = (bf16[256,4096]{1,0:T(8,128)(2,1)}, bf16[256,4096]{1,0:T(8,128)(2,1)}, u32[]{:S(2)}, u32[]{:S(2)}) collective-permute-start(bf16[256,4096]{1,0:T(8,128)(2,1)} %get-tuple-element.33), channel_id=1, source_target_pairs={{0,4},{1,5},{2,6},{3,7},{16,20},{17,21},{18,22},{19,23}} | collective-permute-start | bytes 6291464 | tf_op jit(solution)/shard_map/ppermute | solution.py:100
  56.7 44.5 %collective-permute-start.1 = (bf16[256,4096]{1,0:T(8,128)(2,1)S(1)}, bf16[256,4096]{1,0:T(8,128)(2,1)}, u32[]{:S(2)}, u32[]{:S(2)}) collective-permute-start(bf16[256,4096]{1,0:T(8,128)(2,1)S(1)} %get-tuple-element.32), channel_id=1, source_target_pairs={{12,8},{13,9},{14,10},{15,11},{28,24},{29,25},{30,26},{31,27}} | collective-permute-start | bytes 6291464 | tf_op jit(solution)/shard_map/ppermute | solution.py:100
  100.9 3.4 copy-start.7
  107.8 49.8 %collective-permute-start.2 = (bf16[256,4096]{1,0:T(8,128)(2,1)}, bf16[256,4096]{1,0:T(8,128)(2,1)S(1)}, u32[]{:S(2)}, u32[]{:S(2)}) collective-permute-start(bf16[256,4096]{1,0:T(8,128)(2,1)} %get-tuple-element.30), channel_id=1, source_target_pairs={{0,4},{4,8},{1,5},{5,9},{2,6},{6,10},{3,7},{7,11},{16,20},{20,24},... | collective-permute-start | bytes 6291464 | tf_op jit(solution)/shard_map/ppermute | solution.py:100
  112.9 44.7 %collective-permute-start.4 = (bf16[256,4096]{1,0:T(8,128)(2,1)}, bf16[256,4096]{1,0:T(8,128)(2,1)}, u32[]{:S(2)}, u32[]{:S(2)}) collective-permute-start(bf16[256,4096]{1,0:T(8,128)(2,1)} %get-tuple-element.31), channel_id=1, source_target_pairs={{8,4},{12,8},{9,5},{13,9},{10,6},{14,10},{11,7},{15,11},{24,20},{2... | collective-permute-start | bytes 6291464 | tf_op jit(solution)/shard_map/ppermute | solution.py:100
  163.6 52.3 %collective-permute-start.5 = (bf16[256,4096]{1,0:T(8,128)(2,1)}, bf16[256,4096]{1,0:T(8,128)(2,1)S(1)}, u32[]{:S(2)}, u32[]{:S(2)}) collective-permute-start(bf16[256,4096]{1,0:T(8,128)(2,1)} %get-tuple-element.29), channel_id=1, source_target_pairs={{4,0},{8,4},{12,8},{5,1},{9,5},{13,9},{6,2},{10,6},{14,10},{7,3},{... | collective-permute-start | bytes 6291464 | tf_op jit(solution)/shard_map/ppermute | solution.py:100
  165.2 52.1 %collective-permute-start.3 = (bf16[256,4096]{1,0:T(8,128)(2,1)}, bf16[256,4096]{1,0:T(8,128)(2,1)}, u32[]{:S(2)}, u32[]{:S(2)}) collective-permute-start(bf16[256,4096]{1,0:T(8,128)(2,1)} %get-tuple-element.28), channel_id=1, source_target_pairs={{0,4},{4,8},{8,12},{1,5},{5,9},{9,13},{2,6},{6,10},{10,14},{3,7},{... | collective-permute-start | bytes 6291464 | tf_op jit(solution)/shard_map/ppermute | solution.py:100
  215.9 1.3 copy-start.8
  220.5 47.1 %collective-permute-start.6 = (bf16[256,4096]{1,0:T(8,128)(2,1)S(1)}, bf16[256,4096]{1,0:T(8,128)(2,1)}, u32[]{:S(2)}, u32[]{:S(2)}) collective-permute-start(bf16[256,4096]{1,0:T(8,128)(2,1)S(1)} %multiply_convert_fusion), channel_id=1, source_target_pairs={{0,4},{4,8},{8,12},{1,5},{5,9},{9,13},{2,6},{6,10},{10,14},{3,7},{... | collective-permute-start | bytes 6291464 | tf_op jit(solution)/shard_map/ppermute | solution.py:100
  226.6 46.6 %collective-permute-start.10 = (bf16[256,4096]{1,0:T(8,128)(2,1)S(1)}, bf16[256,4096]{1,0:T(8,128)(2,1)}, u32[]{:S(2)}, u32[]{:S(2)}) collective-permute-start(bf16[256,4096]{1,0:T(8,128)(2,1)S(1)} %multiply_convert_fusion), channel_id=1, source_target_pairs={{4,0},{8,4},{12,8},{5,1},{9,5},{13,9},{6,2},{10,6},{14,10},{7,3},{... | collective-permute-start | bytes 6291464 | tf_op jit(solution)/shard_map/ppermute | solution.py:100
  278.5 43.8 %collective-permute-start.7 = (bf16[256,4096]{1,0:T(8,128)(2,1)}, bf16[256,4096]{1,0:T(8,128)(2,1)}, u32[]{:S(2)}, u32[]{:S(2)}) collective-permute-start(bf16[256,4096]{1,0:T(8,128)(2,1)} %get-tuple-element.26), channel_id=1, source_target_pairs={{4,8},{8,12},{0,4},{5,9},{9,13},{1,5},{6,10},{10,14},{2,6},{7,11},... | collective-permute-start | bytes 6291464 | tf_op jit(solution)/shard_map/ppermute | solution.py:100
  282.5 45.3 %collective-permute-start.11 = (bf16[256,4096]{1,0:T(8,128)(2,1)}, bf16[256,4096]{1,0:T(8,128)(2,1)}, u32[]{:S(2)}, u32[]{:S(2)}) collective-permute-start(bf16[256,4096]{1,0:T(8,128)(2,1)} %get-tuple-element.27), channel_id=1, source_target_pairs={{4,0},{8,4},{12,8},{5,1},{9,5},{13,9},{6,2},{10,6},{14,10},{7,3},{... | collective-permute-start | bytes 6291464 | tf_op jit(solution)/shard_map/ppermute | solution.py:100
  333.5 41.6 %collective-permute-start.8 = (bf16[256,4096]{1,0:T(8,128)(2,1)}, bf16[256,4096]{1,0:T(8,128)(2,1)}, u32[]{:S(2)}, u32[]{:S(2)}) collective-permute-start(bf16[256,4096]{1,0:T(8,128)(2,1)} %get-tuple-element.24), channel_id=1, source_target_pairs={{8,12},{0,4},{4,8},{9,13},{1,5},{5,9},{10,14},{2,6},{6,10},{11,15}... | collective-permute-start | bytes 6291464 | tf_op jit(solution)/shard_map/ppermute | solution.py:100
  336.3 44.2 %collective-permute-start.12 = (bf16[256,4096]{1,0:T(8,128)(2,1)}, bf16[256,4096]{1,0:T(8,128)(2,1)}, u32[]{:S(2)}, u32[]{:S(2)}) collective-permute-start(bf16[256,4096]{1,0:T(8,128)(2,1)} %get-tuple-element.25), channel_id=1, source_target_pairs={{4,0},{8,4},{12,8},{5,1},{9,5},{13,9},{6,2},{10,6},{14,10},{7,3},{... | collective-permute-start | bytes 6291464 | tf_op jit(solution)/shard_map/ppermute | solution.py:100
  386.7 43.3 %collective-permute-start.13 = (bf16[256,4096]{1,0:T(8,128)(2,1)}, bf16[256,4096]{1,0:T(8,128)(2,1)}, u32[]{:S(2)}, u32[]{:S(2)}) collective-permute-start(bf16[256,4096]{1,0:T(8,128)(2,1)} %get-tuple-element.23), channel_id=1, source_target_pairs={{4,0},{8,4},{12,8},{5,1},{9,5},{13,9},{6,2},{10,6},{14,10},{7,3},{... | collective-permute-start | bytes 6291464 | tf_op jit(solution)/shard_map/ppermute | solution.py:100
  388.0 43.2 %collective-permute-start.9 = (bf16[256,4096]{1,0:T(8,128)(2,1)}, bf16[256,4096]{1,0:T(8,128)(2,1)}, u32[]{:S(2)}, u32[]{:S(2)}) collective-permute-start(bf16[256,4096]{1,0:T(8,128)(2,1)} %get-tuple-element.22), channel_id=1, source_target_pairs={{0,4},{4,8},{8,12},{1,5},{5,9},{9,13},{2,6},{6,10},{10,14},{3,7},{... | collective-permute-start | bytes 6291464 | tf_op jit(solution)/shard_map/ppermute | solution.py:100
  397.1 12.0 %copy-start.10 = (bf16[256,4096]{1,0:T(8,128)(2,1)}, bf16[256,4096]{1,0:T(8,128)(2,1)S(1)}, u32[]{:S(2)}) copy-start(bf16[256,4096]{1,0:T(8,128)(2,1)S(1)} %select_select_fusion.4) | copy-start | bytes 6291460
  401.1 8.0 %copy-start.12 = (bf16[256,4096]{1,0:T(8,128)(2,1)}, bf16[256,4096]{1,0:T(8,128)(2,1)S(1)}, u32[]{:S(2)}) copy-start(bf16[256,4096]{1,0:T(8,128)(2,1)S(1)} %select_select_fusion.5) | copy-start | bytes 6291460
  405.1 4.0 copy-start.14
  409.2 1.3 copy-start.16
  424.7 6.5 copy-start.9
  424.7 217.5 %reduce-scatter.5.cloned.1.call-start = ((), (), s32[]{:S(2)}) async-start(), calls=%async_computation.5 | async-start | bytes 5242880 | tf_op jit(solution)/shard_map/reduce_scatter | solution.py:167
  436.8 44.0 %copy-start.4 = (bf16[256,4096]{1,0:T(8,128)(2,1)}, bf16[256,4096]{1,0:T(8,128)(2,1)S(1)}, u32[]{:S(2)}) copy-start(bf16[256,4096]{1,0:T(8,128)(2,1)S(1)} %fusion.19) | copy-start | bytes 6291460
  436.8 42.5 %collective-permute-start.14 = (bf16[256,4096]{1,0:T(8,128)(2,1)S(1)}, bf16[256,4096]{1,0:T(8,128)(2,1)S(1)}, u32[]{:S(2)}, u32[]{:S(2)}) collective-permute-start(bf16[256,4096]{1,0:T(8,128)(2,1)S(1)} %fusion.19), channel_id=1, source_target_pairs={{0,4},{4,8},{8,12},{1,5},{5,9},{9,13},{2,6},{6,10},{10,14},{3,7},{... | collective-permute-start | bytes 6291464 | tf_op jit(solution)/shard_map/ppermute | solution.py:100
  442.0 41.5 %collective-permute-start.16 = (bf16[256,4096]{1,0:T(8,128)(2,1)S(1)}, bf16[256,4096]{1,0:T(8,128)(2,1)S(1)}, u32[]{:S(2)}, u32[]{:S(2)}) collective-permute-start(bf16[256,4096]{1,0:T(8,128)(2,1)S(1)} %fusion.19), channel_id=1, source_target_pairs={{4,0},{8,4},{12,8},{5,1},{9,5},{13,9},{6,2},{10,6},{14,10},{7,3},{... | collective-permute-start | bytes 6291464 | tf_op jit(solution)/shard_map/ppermute | solution.py:100
  479.3 19.1 %copy-start.15 = (bf16[256,4096]{1,0:T(8,128)(2,1)S(1)}, bf16[256,4096]{1,0:T(8,128)(2,1)}, u32[]{:S(2)}) copy-start(bf16[256,4096]{1,0:T(8,128)(2,1)} %copy-done.14) | copy-start | bytes 6291460
  480.8 17.6 %copy-start.11 = (bf16[256,4096]{1,0:T(8,128)(2,1)S(1)}, bf16[256,4096]{1,0:T(8,128)(2,1)}, u32[]{:S(2)}) copy-start(bf16[256,4096]{1,0:T(8,128)(2,1)} %copy-done.10) | copy-start | bytes 6291460
  480.8 17.6 %copy-start.13 = (bf16[256,4096]{1,0:T(8,128)(2,1)S(1)}, bf16[256,4096]{1,0:T(8,128)(2,1)}, u32[]{:S(2)}) copy-start(bf16[256,4096]{1,0:T(8,128)(2,1)} %copy-done.12) | copy-start | bytes 6291460
  480.8 30.9 %collective-permute-start.15 = (bf16[256,4096]{1,0:T(8,128)(2,1)}, bf16[256,4096]{1,0:T(8,128)(2,1)}, u32[]{:S(2)}, u32[]{:S(2)}) collective-permute-start(bf16[256,4096]{1,0:T(8,128)(2,1)} %broadcast_select_fusion.8), channel_id=1, source_target_pairs={{4,8},{8,12},{5,9},{9,13},{6,10},{10,14},{7,11},{11,15},{20,24},{2... | collective-permute-start | bytes 6291464 | tf_op jit(solution)/shard_map/ppermute | solution.py:100
  483.6 2.0 copy-start
  485.6 46.2 %collective-permute-start.17 = (bf16[256,4096]{1,0:T(8,128)(2,1)}, bf16[256,4096]{1,0:T(8,128)(2,1)}, u32[]{:S(2)}, u32[]{:S(2)}) collective-permute-start(bf16[256,4096]{1,0:T(8,128)(2,1)} %broadcast_select_fusion.2), channel_id=1, source_target_pairs={{4,0},{8,4},{5,1},{9,5},{6,2},{10,6},{7,3},{11,7},{20,16},{24,20},... | collective-permute-start | bytes 6291464 | tf_op jit(solution)/shard_map/ppermute | solution.py:100
  534.8 42.4 %copy-start.1 = (bf16[256,4096]{1,0:T(8,128)(2,1)S(1)}, bf16[256,4096]{1,0:T(8,128)(2,1)}, u32[]{:S(2)}) copy-start(bf16[256,4096]{1,0:T(8,128)(2,1)} %copy-done) | copy-start | bytes 6291460
  534.8 42.4 %copy-start.2 = (bf16[256,4096]{1,0:T(8,128)(2,1)S(1)}, bf16[256,4096]{1,0:T(8,128)(2,1)}, u32[]{:S(2)}) copy-start(bf16[256,4096]{1,0:T(8,128)(2,1)} %broadcast_select_fusion.10) | copy-start | bytes 6291460
  534.8 42.4 %copy-start.3 = (bf16[256,4096]{1,0:T(8,128)(2,1)S(1)}, bf16[256,4096]{1,0:T(8,128)(2,1)}, u32[]{:S(2)}) copy-start(bf16[256,4096]{1,0:T(8,128)(2,1)} %broadcast_select_fusion.6) | copy-start | bytes 6291460
  534.8 42.4 %copy-start.5 = (bf16[256,4096]{1,0:T(8,128)(2,1)S(1)}, bf16[256,4096]{1,0:T(8,128)(2,1)}, u32[]{:S(2)}) copy-start(bf16[256,4096]{1,0:T(8,128)(2,1)} %copy-done.4) | copy-start | bytes 6291460
  534.8 38.9 %collective-permute-start.19 = (bf16[256,4096]{1,0:T(8,128)(2,1)}, bf16[256,4096]{1,0:T(8,128)(2,1)S(1)}, u32[]{:S(2)}, u32[]{:S(2)}) collective-permute-start(bf16[256,4096]{1,0:T(8,128)(2,1)} %broadcast_select_fusion.6), channel_id=1, source_target_pairs={{4,0},{5,1},{6,2},{7,3},{20,16},{21,17},{22,18},{23,19}} | collective-permute-start | bytes 6291464 | tf_op jit(solution)/shard_map/ppermute | solution.py:100
  536.4 37.3 %collective-permute-start.18 = (bf16[256,4096]{1,0:T(8,128)(2,1)}, bf16[256,4096]{1,0:T(8,128)(2,1)S(1)}, u32[]{:S(2)}, u32[]{:S(2)}) collective-permute-start(bf16[256,4096]{1,0:T(8,128)(2,1)} %broadcast_select_fusion.10), channel_id=1, source_target_pairs={{8,12},{9,13},{10,14},{11,15},{24,28},{25,29},{26,30},{27,31}} | collective-permute-start | bytes 6291464 | tf_op jit(solution)/shard_map/ppermute | solution.py:100
  599.4 1.0 copy-start.19
  599.4 3.3 copy-start.18
  600.4 2.3 copy-start.17
  616.4 25.8 %copy-start.20 = (bf16[1024,256]{1,0:T(8,128)(2,1)S(1)}, bf16[1024,256]{1,0:T(8,128)(2,1)}, u32[]{:S(2)}) copy-start(bf16[1024,256]{1,0:T(8,128)(2,1)} %param.7) | copy-start | bytes 1572868
Sparse Core Ops, SparseCore 0:
  9.6 25.5 all-gather.2
  36.7 22.8 all-gather.4
  424.8 41.7 reduce-scatter.2
  599.5 42.6 reduce-scatter.4

commit v5 on v4

--- a/solution.py
+++ b/solution.py
@@ -139,21 +139,32 @@
         run_slot([(act_gather, step), (grad_sum, step - 1)])
     activation = act_gather.result()
     out_part = jnp.dot(activation, down_tile, preferred_element_type=jnp.float32)
-    out_sum = lax.psum_scatter(out_part, "p", scatter_dimension=1, tiled=True)
     grad_down = lax.dot_general(
         activation, grad_rows, (((0,), (0,)), ((), ())), preferred_element_type=jnp.float32
     ).astype(jnp.bfloat16)
     if count > 1:
         run_slot([(grad_sum, count - 2)])
+        grad_sum.up_in, grad_sum.down_in, out_part = lax.optimization_barrier(
+            (grad_sum.up_in, grad_sum.down_in, out_part)
+        )
+    out_sum = lax.psum_scatter(out_part, "p", scatter_dimension=1, tiled=True)
     act_grad = grad_sum.result()
     pre_gather = LineGather((act_grad * gelu_slope(preact)).astype(jnp.bfloat16))
+    tied = {0: "grad_down", min(1, count - 2): "out_sum"}
     for step in range(count - 1):
         run_slot([(pre_gather, step)])
-        if step == min(1, count - 2):
-            pre_gather.up_cur, pre_gather.down_cur, out_sum, grad_down = lax.optimization_barrier(
-                (pre_gather.up_cur, pre_gather.down_cur, out_sum, grad_down)
+        for name in [tied.get(0), tied.get(1)] if step == 0 and count == 2 else [tied.get(step)]:
+            if name is None:
+                continue
+            value = grad_down if name == "grad_down" else out_sum
+            pre_gather.up_cur, pre_gather.down_cur, value = lax.optimization_barrier(
+                (pre_gather.up_cur, pre_gather.down_cur, value)
             )
             pre_gather.ups[-1], pre_gather.downs[-1] = pre_gather.up_cur, pre_gather.down_cur
+            if name == "grad_down":
+                grad_down = value
+            else:
+                out_sum = value
     pre_grad = pre_gather.result()
     block_out = (hidden_in.astype(jnp.float32) + out_sum).astype(jnp.bfloat16)
     grad_up = lax.dot_general(

time: 660 us -> 673 us (1.020)
  waiting for transfers between devices: 383 us -> 391 us
  other arithmetic: 72 us -> 79.5 us
    unnamed x43 -> x41, local copies, waits for them, and re-layouts: 21.1 us -> 18.8 us
  transfers between devices with their start and end apart: 24 -> 24, of which waited for: 18 -> 17; matrix products, arithmetic and copies ran while one was open for 17% -> 17% of each run, Pallas kernels for 0% -> 0%
where the time goes in v5:
time: 673 us; the launch traced here: 663 us
  waiting for transfers between devices  391 us (58%)
  matrix products  86 us (13%)
  other arithmetic  79.5 us (12%)
  starting transfers between devices  72 us (11%)
  local copies, waits for them, and re-layouts  20.8 us (3%)
  between operations  14.4 us (2%)
    ppermute x20, waiting for transfers between devices, run_slot(): received.append(lax.ppermute(combined, 'r', pairs))  342 us
    ppermute x20, starting transfers between devices, run_slot(): received.append(lax.ppermute(combined, 'r', pairs))  71.9 us
    select_n x8, other arithmetic, result(): pieces.append(lax.select_n(which.astype(jnp.int32), *cases))  26.6 us
    all_gather x1, waiting for transfers between devices, on_device(): x_rows = lax.all_gather(hidden_in, 'p', axis=1, tiled=True)  26.4 us
    reduce_scatter x1, waiting for transfers between devices, on_device(): lax.psum_scatter(back_part, 'p', scatter_dimension=1, tiled=True)  19.5 us
    unnamed x41, local copies, waits for them, and re-layouts  18.8 us
    dot_general x1, matrix products, on_device(): lax.dot_general(pre_grad, up_tile, (((1,), (1,)), ((), ())), preferred_el...  17.3 us
    convert_element_type x3, other arithmetic, payload(): return (up.astype(jnp.bfloat16), down.astype(jnp.bfloat16))  15.6 us
  transfers between devices with their start and end apart: 24, of which 17 were waited for; matrix products, arithmetic and copies ran while one was open for 17% of the time, Pallas kernels for 0%

profile of v5, /device:TPU:0, one launch (start us, length us, event | category | flops | bytes accessed | tf_op | source)
XLA Modules:
  0.0 663.4 jit_solution(2562078575683099211)
XLA Ops:
  8.7 26.4 %all-gather.3.cloned.1.call-done = bf16[1024,1024]{1,0:T(8,128)(2,1)} async-done(((bf16[1024,256]{1,0:T(8,128)(2,1)}), bf16[1024,1024]{1,0:T(8,128)(2,1)}) %all-gather.3.cloned.1.call-update) | async-done | bytes 2097168 | tf_op jit(solution)/shard_map/all_gather | solution.py:118
  35.1 12.8 %fusion.8 = bf16[1024,4096]{1,0:T(8,128)(2,1)S(1)} fusion(bf16[1024,1024]{1,0:T(8,128)(2,1)} %all-gather.3.cloned.1.call-done, bf16[1,1024,4096]{2,1,0:T(8,128)(2,1)} %param.5), kind=kOutput, calls=%fused_computation.11 | convolution fusion | flops 8594128896 | bytes 18874368 | tf_op jit(solution)/shard_map/dot_general | solution.py:119
  49.9 2.0 copy-done.6
  53.9 4.7 collective-permute-start
  59.6 14.8 %fusion.11 = bf16[1024,4096]{1,0:T(8,128)(2,1)} fusion(bf16[1024,1024]{1,0:T(8,128)(2,1)} %all-gather.5.cloned.1.call-done, bf16[1,4096,1024]{2,1,0:T(8,128)(2,1)} %param.6), kind=kOutput, calls=%fused_computation.12 | convolution fusion | flops 8594128896 | bytes 18874368 | tf_op jit(solution)/shard_map/dot_general | solution.py:121
  74.7 28.0 %collective-permute-done = bf16[256,4096]{1,0:T(8,128)(2,1)} collective-permute-done((bf16[256,4096]{1,0:T(8,128)(2,1)S(1)}, bf16[256,4096]{1,0:T(8,128)(2,1)}, u32[]{:S(2)}, u32[]{:S(2)}) %collective-permute-start) | collective-permute-done | bytes 2097184 | tf_op jit(solution)/shard_map/ppermute | solution.py:100
  102.9 3.5 fusion.29
  106.4 6.2 collective-permute-start.2
  114.6 42.7 %collective-permute-done.2 = bf16[256,4096]{1,0:T(8,128)(2,1)S(1)} collective-permute-done((bf16[256,4096]{1,0:T(8,128)(2,1)}, bf16[256,4096]{1,0:T(8,128)(2,1)S(1)}, u32[]{:S(2)}, u32[]{:S(2)}) %collective-permute-start.2) | collective-permute-done | bytes 2097184 | tf_op jit(solution)/shard_map/ppermute | solution.py:100
  157.3 6.0 fusion.28
  163.3 8.9 %collective-permute-start.3 = (bf16[256,4096]{1,0:T(8,128)(2,1)}, bf16[256,4096]{1,0:T(8,128)(2,1)S(1)}, u32[]{:S(2)}, u32[]{:S(2)}) collective-permute-start(bf16[256,4096]{1,0:T(8,128)(2,1)} %get-tuple-element.38), channel_id=1, source_target_pairs={{0,4},{4,8},{8,12},{1,5},{5,9},{9,13},{2,6},{6,10},{10,14},{3,7},{... | collective-permute-start | bytes 6291464 | tf_op jit(solution)/shard_map/ppermute | solution.py:100
  173.5 42.2 %collective-permute-done.3 = bf16[256,4096]{1,0:T(8,128)(2,1)S(1)} collective-permute-done((bf16[256,4096]{1,0:T(8,128)(2,1)}, bf16[256,4096]{1,0:T(8,128)(2,1)S(1)}, u32[]{:S(2)}, u32[]{:S(2)}) %collective-permute-start.3) | collective-permute-done | bytes 2097184 | tf_op jit(solution)/shard_map/ppermute | solution.py:100
  217.0 2.9 collective-permute-done.5
  219.9 3.3 multiply_convert_fusion
  224.5 5.9 collective-permute-start.6
  230.4 39.4 %collective-permute-done.10 = bf16[256,4096]{1,0:T(8,128)(2,1)} collective-permute-done((bf16[256,4096]{1,0:T(8,128)(2,1)S(1)}, bf16[256,4096]{1,0:T(8,128)(2,1)}, u32[]{:S(2)}, u32[]{:S(2)}) %collective-permute-start.10) | collective-permute-done | bytes 2097184 | tf_op jit(solution)/shard_map/ppermute | solution.py:100
  270.8 5.4 bitcast_select_fusion
  277.5 7.1 %collective-permute-start.7 = (bf16[256,4096]{1,0:T(8,128)(2,1)}, bf16[256,4096]{1,0:T(8,128)(2,1)}, u32[]{:S(2)}, u32[]{:S(2)}) collective-permute-start(bf16[256,4096]{1,0:T(8,128)(2,1)} %get-tuple-element.37), channel_id=1, source_target_pairs={{4,8},{8,12},{0,4},{5,9},{9,13},{1,5},{6,10},{10,14},{2,6},{7,11},... | collective-permute-start | bytes 6291464 | tf_op jit(solution)/shard_map/ppermute | solution.py:100
  284.6 38.6 %collective-permute-done.11 = bf16[256,4096]{1,0:T(8,128)(2,1)} collective-permute-done((bf16[256,4096]{1,0:T(8,128)(2,1)}, bf16[256,4096]{1,0:T(8,128)(2,1)}, u32[]{:S(2)}, u32[]{:S(2)}) %collective-permute-start.11) | collective-permute-done | bytes 2097184 | tf_op jit(solution)/shard_map/ppermute | solution.py:100
  324.4 5.7 fusion.31
  331.4 6.4 collective-permute-start.8
  337.8 37.7 %collective-permute-done.12 = bf16[256,4096]{1,0:T(8,128)(2,1)} collective-permute-done((bf16[256,4096]{1,0:T(8,128)(2,1)}, bf16[256,4096]{1,0:T(8,128)(2,1)}, u32[]{:S(2)}, u32[]{:S(2)}) %collective-permute-start.12) | collective-permute-done | bytes 2097184 | tf_op jit(solution)/shard_map/ppermute | solution.py:100
  376.7 6.1 fusion.21
  384.1 7.6 %collective-permute-start.9 = (bf16[256,4096]{1,0:T(8,128)(2,1)}, bf16[256,4096]{1,0:T(8,128)(2,1)}, u32[]{:S(2)}, u32[]{:S(2)}) collective-permute-start(bf16[256,4096]{1,0:T(8,128)(2,1)} %get-tuple-element.33), channel_id=1, source_target_pairs={{0,4},{4,8},{8,12},{1,5},{5,9},{9,13},{2,6},{6,10},{10,14},{3,7},{... | collective-permute-start | bytes 6291464 | tf_op jit(solution)/shard_map/ppermute | solution.py:100
  391.7 3.3 select_select_fusion.7
  395.0 4.0 select_select_fusion.6
  399.0 4.0 select_select_fusion.5
  403.0 4.0 select_select_fusion.4
  408.5 14.1 %fusion = f32[1024,1024]{1,0:T(8,128)} fusion(bf16[1,4096,1024]{2,1,0:T(8,128)(2,1)} %param.6, bf16[256,4096]{1,0:T(8,128)(2,1)S(1)} %select_select_fusion.4, bf16[256,4096]{1,0:T(8,128)(2,1)S(1)} %select_select_fusion.5, bf16[256,4096]{1,0:T(8,128)(2,1)S(1)} %select_select_fusion.6, bf16[256,4096]{1,0:T(8,128)(2,1)S(1)} %select_select_fusion.7), kind=kOutput, calls=%fused_computation.2 | convolution fusion | flops 8623489024 | bytes 20971520 | tf_op jit(solution)/shard_map/dot_general | solution.py:141
  422.6 6.0 collective-permute-done.13
  428.6 3.9 select_convert_fusion
  432.5 2.3 select_convert_fusion.1
  436.4 6.9 %fusion.19 = bf16[256,4096]{1,0:T(8,128)(2,1)S(1)} fusion(f32[256,4096]{1,0:T(8,128)} %select_convert_fusion, f32[256,4096]{1,0:T(8,128)} %select_convert_fusion.1, bf16[4,256,4096]{2,1,0:T(8,128)(2,1)} %bitcast.81, s32[]{:T(128)S(6)} %select_n.530, bf16[256,4096]{1,0:T(8,128)(2,1)} %collective-permute-done.5, pred[]{:T(512)S(6)} %and.26, ...), kind=kLoop, calls=%fused_computation.20 | loop fusion | flops 20971520 | bytes 18874374 | tf_op jit(solution)/shard_map/convert_element_type | solution.py:152
  444.6 8.6 %collective-permute-start.14 = (bf16[256,4096]{1,0:T(8,128)(2,1)S(1)}, bf16[256,4096]{1,0:T(8,128)(2,1)}, u32[]{:S(2)}, u32[]{:S(2)}) collective-permute-start(bf16[256,4096]{1,0:T(8,128)(2,1)S(1)} %fusion.19), channel_id=1, source_target_pairs={{0,4},{4,8},{8,12},{1,5},{5,9},{9,13},{2,6},{6,10},{10,14},{3,7},{... | collective-permute-start | bytes 6291464 | tf_op jit(solution)/shard_map/ppermute | solution.py:100
  453.3 13.5 %convolution_convert_fusion = bf16[4096,1024]{1,0:T(8,128)(2,1)} fusion(bf16[1024,1024]{1,0:T(8,128)(2,1)} %all-gather.5.cloned.1.call-done, bf16[256,4096]{1,0:T(8,128)(2,1)} %copy-done.15, bf16[256,4096]{1,0:T(8,128)(2,1)} %copy-done.14, bf16[256,4096]{1,0:T(8,128)(2,1)S(1)} %copy-done.13, bf16[256,4096]{1,0:T(8,128)(2,1)S(1)} %copy-done.11), kind=kOutput, calls=%fused_computation.13 | convolution fusion | flops 8627683328 | bytes 18874368 | tf_op jit(solution)/shard_map/dot_general | solution.py:142
  466.8 21.5 %collective-permute-done.15 = bf16[256,4096]{1,0:T(8,128)(2,1)} collective-permute-done((bf16[256,4096]{1,0:T(8,128)(2,1)S(1)}, bf16[256,4096]{1,0:T(8,128)(2,1)}, u32[]{:S(2)}, u32[]{:S(2)}) %collective-permute-start.15) | collective-permute-done | bytes 2097184 | tf_op jit(solution)/shard_map/ppermute | solution.py:100
  492.3 40.7 %collective-permute-done.17 = bf16[256,4096]{1,0:T(8,128)(2,1)S(1)} collective-permute-done((bf16[256,4096]{1,0:T(8,128)(2,1)S(1)}, bf16[256,4096]{1,0:T(8,128)(2,1)S(1)}, u32[]{:S(2)}, u32[]{:S(2)}) %collective-permute-start.17) | collective-permute-done | bytes 2097184 | tf_op jit(solution)/shard_map/ppermute | solution.py:100
  538.5 39.4 %collective-permute-done.19 = bf16[256,4096]{1,0:T(8,128)(2,1)S(1)} collective-permute-done((bf16[256,4096]{1,0:T(8,128)(2,1)}, bf16[256,4096]{1,0:T(8,128)(2,1)S(1)}, u32[]{:S(2)}, u32[]{:S(2)}) %collective-permute-start.19) | collective-permute-done | bytes 2097184 | tf_op jit(solution)/shard_map/ppermute | solution.py:100
  578.0 5.0 select_select_fusion.3
  583.0 2.2 select_select_fusion.2
  585.1 2.1 select_select_fusion.1
  587.3 2.1 select_select_fusion
  589.4 17.3 %fusion.4 = f32[1024,1024]{1,0:T(8,128)} fusion(bf16[1,1024,4096]{2,1,0:T(8,128)(2,1)} %param.5, bf16[256,4096]{1,0:T(8,128)(2,1)} %select_select_fusion, bf16[256,4096]{1,0:T(8,128)(2,1)} %select_select_fusion.1, bf16[256,4096]{1,0:T(8,128)(2,1)} %select_select_fusion.2, bf16[256,4096]{1,0:T(8,128)(2,1)} %select_select_fusion.3), kind=kOutput, calls=%fused_computation.6 | convolution fusion | flops 8623489024 | bytes 20971520 | tf_op jit(solution)/shard_map/dot_general | solution.py:173
  607.8 2.3 add_convert_fusion.1
  610.1 13.5 %convert_bitcast_fusion = bf16[1,1024,4096]{1,2,0:T(8,128)(2,1)} fusion(bf16[1024,1024]{1,0:T(8,128)(2,1)} %all-gather.3.cloned.1.call-done, bf16[256,4096]{1,0:T(8,128)(2,1)} %select_select_fusion, bf16[256,4096]{1,0:T(8,128)(2,1)} %select_select_fusion.1, bf16[256,4096]{1,0:T(8,128)(2,1)S(1)} %copy-done.17, bf16[256,4096]{1,0:T(8,128)(2,1)S(1)} %copy-done.16), kind=kOutput, calls=%fused_computation.10 | convolution fusion | flops 8627683328 | bytes 18874368 | tf_op jit(solution)/shard_map/dot_general | solution.py:170
  623.5 11.5 %copy.8 = bf16[1,1024,4096]{2,1,0:T(8,128)(2,1)} copy(bf16[1,1024,4096]{1,2,0:T(8,128)(2,1)} %convert_bitcast_fusion) | data formatting | bytes 16777216
  635.0 19.5 %reduce-scatter.5.cloned.1.call-done = f32[1024,256]{1,0:T(8,128)} async-done(((f32[1024,1024]{1,0:T(8,128)}), f32[1024,256]{1,0:T(8,128)}) %reduce-scatter.5.cloned.1.call-update) | async-done | bytes 1048592 | tf_op jit(solution)/shard_map/reduce_scatter | solution.py:178
  654.5 2.1 add_convert_fusion
  (77 shorter events, 34.9 us)
Async XLA Ops:
  7.2 28.0 %all-gather.3.cloned.1.call-start = ((), (), s32[]{:S(2)}) async-start(), calls=%async_computation.2 | async-start | bytes 2621440 | tf_op jit(solution)/shard_map/all_gather | solution.py:118
  7.9 51.7 %all-gather.5.cloned.1.call-start = ((), (), s32[]{:S(2)}) async-start(), calls=%async_computation.3 | async-start | bytes 2621440 | tf_op jit(solution)/shard_map/all_gather | solution.py:120
  8.6 527.4 %reduce-scatter.3.cloned.1.call-start = ((), (), s32[]{:S(2)}) async-start(), calls=%async_computation.4 | async-start | bytes 5242880 | tf_op jit(solution)/shard_map/reduce_scatter | solution.py:150
  47.9 4.0 copy-start.6
  51.9 22.5 %collective-permute-start.1 = (bf16[256,4096]{1,0:T(8,128)(2,1)}, bf16[256,4096]{1,0:T(8,128)(2,1)}, u32[]{:S(2)}, u32[]{:S(2)}) collective-permute-start(bf16[256,4096]{1,0:T(8,128)(2,1)} %get-tuple-element.42), channel_id=1, source_target_pairs={{12,8},{13,9},{14,10},{15,11},{28,24},{29,25},{30,26},{31,27}} | collective-permute-start | bytes 6291464 | tf_op jit(solution)/shard_map/ppermute | solution.py:100
  53.9 48.7 %collective-permute-start = (bf16[256,4096]{1,0:T(8,128)(2,1)S(1)}, bf16[256,4096]{1,0:T(8,128)(2,1)}, u32[]{:S(2)}, u32[]{:S(2)}) collective-permute-start(bf16[256,4096]{1,0:T(8,128)(2,1)S(1)} %get-tuple-element.43), channel_id=1, source_target_pairs={{0,4},{1,5},{2,6},{3,7},{16,20},{17,21},{18,22},{19,23}} | collective-permute-start | bytes 6291464 | tf_op jit(solution)/shard_map/ppermute | solution.py:100
  74.4 28.5 %copy-start.7 = (bf16[1024,4096]{1,0:T(8,128)(2,1)S(1)}, bf16[1024,4096]{1,0:T(8,128)(2,1)}, u32[]{:S(2)}) copy-start(bf16[1024,4096]{1,0:T(8,128)(2,1)} %copy-done.6) | copy-start | bytes 25165828
  106.4 50.9 %collective-permute-start.2 = (bf16[256,4096]{1,0:T(8,128)(2,1)}, bf16[256,4096]{1,0:T(8,128)(2,1)S(1)}, u32[]{:S(2)}, u32[]{:S(2)}) collective-permute-start(bf16[256,4096]{1,0:T(8,128)(2,1)} %get-tuple-element.40), channel_id=1, source_target_pairs={{0,4},{4,8},{1,5},{5,9},{2,6},{6,10},{3,7},{7,11},{16,20},{20,24},... | collective-permute-start | bytes 6291464 | tf_op jit(solution)/shard_map/ppermute | solution.py:100
  112.6 44.7 %collective-permute-start.4 = (bf16[256,4096]{1,0:T(8,128)(2,1)}, bf16[256,4096]{1,0:T(8,128)(2,1)}, u32[]{:S(2)}, u32[]{:S(2)}) collective-permute-start(bf16[256,4096]{1,0:T(8,128)(2,1)} %get-tuple-element.41), channel_id=1, source_target_pairs={{8,4},{12,8},{9,5},{13,9},{10,6},{14,10},{11,7},{15,11},{24,20},{2... | collective-permute-start | bytes 6291464 | tf_op jit(solution)/shard_map/ppermute | solution.py:100
  163.3 52.4 %collective-permute-start.3 = (bf16[256,4096]{1,0:T(8,128)(2,1)}, bf16[256,4096]{1,0:T(8,128)(2,1)S(1)}, u32[]{:S(2)}, u32[]{:S(2)}) collective-permute-start(bf16[256,4096]{1,0:T(8,128)(2,1)} %get-tuple-element.38), channel_id=1, source_target_pairs={{0,4},{4,8},{8,12},{1,5},{5,9},{9,13},{2,6},{6,10},{10,14},{3,7},{... | collective-permute-start | bytes 6291464 | tf_op jit(solution)/shard_map/ppermute | solution.py:100
  172.2 47.7 %collective-permute-start.5 = (bf16[256,4096]{1,0:T(8,128)(2,1)}, bf16[256,4096]{1,0:T(8,128)(2,1)}, u32[]{:S(2)}, u32[]{:S(2)}) collective-permute-start(bf16[256,4096]{1,0:T(8,128)(2,1)} %get-tuple-element.39), channel_id=1, source_target_pairs={{4,0},{8,4},{12,8},{5,1},{9,5},{13,9},{6,2},{10,6},{14,10},{7,3},{... | collective-permute-start | bytes 6291464 | tf_op jit(solution)/shard_map/ppermute | solution.py:100
  215.7 1.3 copy-start.8
  223.2 46.6 %collective-permute-start.10 = (bf16[256,4096]{1,0:T(8,128)(2,1)S(1)}, bf16[256,4096]{1,0:T(8,128)(2,1)}, u32[]{:S(2)}, u32[]{:S(2)}) collective-permute-start(bf16[256,4096]{1,0:T(8,128)(2,1)S(1)} %multiply_convert_fusion), channel_id=1, source_target_pairs={{4,0},{8,4},{12,8},{5,1},{9,5},{13,9},{6,2},{10,6},{14,10},{7,3},{... | collective-permute-start | bytes 6291464 | tf_op jit(solution)/shard_map/ppermute | solution.py:100
  224.5 46.4 %collective-permute-start.6 = (bf16[256,4096]{1,0:T(8,128)(2,1)S(1)}, bf16[256,4096]{1,0:T(8,128)(2,1)}, u32[]{:S(2)}, u32[]{:S(2)}) collective-permute-start(bf16[256,4096]{1,0:T(8,128)(2,1)S(1)} %multiply_convert_fusion), channel_id=1, source_target_pairs={{0,4},{4,8},{8,12},{1,5},{5,9},{9,13},{2,6},{6,10},{10,14},{3,7},{... | collective-permute-start | bytes 6291464 | tf_op jit(solution)/shard_map/ppermute | solution.py:100
  276.2 47.0 %collective-permute-start.11 = (bf16[256,4096]{1,0:T(8,128)(2,1)}, bf16[256,4096]{1,0:T(8,128)(2,1)}, u32[]{:S(2)}, u32[]{:S(2)}) collective-permute-start(bf16[256,4096]{1,0:T(8,128)(2,1)} %get-tuple-element.36), channel_id=1, source_target_pairs={{4,0},{8,4},{12,8},{5,1},{9,5},{13,9},{6,2},{10,6},{14,10},{7,3},{... | collective-permute-start | bytes 6291464 | tf_op jit(solution)/shard_map/ppermute | solution.py:100
  277.5 46.9 %collective-permute-start.7 = (bf16[256,4096]{1,0:T(8,128)(2,1)}, bf16[256,4096]{1,0:T(8,128)(2,1)}, u32[]{:S(2)}, u32[]{:S(2)}) collective-permute-start(bf16[256,4096]{1,0:T(8,128)(2,1)} %get-tuple-element.37), channel_id=1, source_target_pairs={{4,8},{8,12},{0,4},{5,9},{9,13},{1,5},{6,10},{10,14},{2,6},{7,11},... | collective-permute-start | bytes 6291464 | tf_op jit(solution)/shard_map/ppermute | solution.py:100
  330.1 45.4 %collective-permute-start.12 = (bf16[256,4096]{1,0:T(8,128)(2,1)}, bf16[256,4096]{1,0:T(8,128)(2,1)}, u32[]{:S(2)}, u32[]{:S(2)}) collective-permute-start(bf16[256,4096]{1,0:T(8,128)(2,1)} %get-tuple-element.34), channel_id=1, source_target_pairs={{4,0},{8,4},{12,8},{5,1},{9,5},{13,9},{6,2},{10,6},{14,10},{7,3},{... | collective-permute-start | bytes 6291464 | tf_op jit(solution)/shard_map/ppermute | solution.py:100
  331.4 45.3 %collective-permute-start.8 = (bf16[256,4096]{1,0:T(8,128)(2,1)}, bf16[256,4096]{1,0:T(8,128)(2,1)}, u32[]{:S(2)}, u32[]{:S(2)}) collective-permute-start(bf16[256,4096]{1,0:T(8,128)(2,1)} %get-tuple-element.35), channel_id=1, source_target_pairs={{8,12},{0,4},{4,8},{9,13},{1,5},{5,9},{10,14},{2,6},{6,10},{11,15}... | collective-permute-start | bytes 6291464 | tf_op jit(solution)/shard_map/ppermute | solution.py:100
  382.8 45.8 %collective-permute-start.13 = (bf16[256,4096]{1,0:T(8,128)(2,1)}, bf16[256,4096]{1,0:T(8,128)(2,1)}, u32[]{:S(2)}, u32[]{:S(2)}) collective-permute-start(bf16[256,4096]{1,0:T(8,128)(2,1)} %get-tuple-element.32), channel_id=1, source_target_pairs={{4,0},{8,4},{12,8},{5,1},{9,5},{13,9},{6,2},{10,6},{14,10},{7,3},{... | collective-permute-start | bytes 6291464 | tf_op jit(solution)/shard_map/ppermute | solution.py:100
  384.1 48.4 %collective-permute-start.9 = (bf16[256,4096]{1,0:T(8,128)(2,1)}, bf16[256,4096]{1,0:T(8,128)(2,1)}, u32[]{:S(2)}, u32[]{:S(2)}) collective-permute-start(bf16[256,4096]{1,0:T(8,128)(2,1)} %get-tuple-element.33), channel_id=1, source_target_pairs={{0,4},{4,8},{8,12},{1,5},{5,9},{9,13},{2,6},{6,10},{10,14},{3,7},{... | collective-permute-start | bytes 6291464 | tf_op jit(solution)/shard_map/ppermute | solution.py:100
  395.0 12.0 %copy-start.10 = (bf16[256,4096]{1,0:T(8,128)(2,1)}, bf16[256,4096]{1,0:T(8,128)(2,1)S(1)}, u32[]{:S(2)}) copy-start(bf16[256,4096]{1,0:T(8,128)(2,1)S(1)} %select_select_fusion.7) | copy-start | bytes 6291460
  399.0 8.0 %copy-start.12 = (bf16[256,4096]{1,0:T(8,128)(2,1)}, bf16[256,4096]{1,0:T(8,128)(2,1)S(1)}, u32[]{:S(2)}) copy-start(bf16[256,4096]{1,0:T(8,128)(2,1)S(1)} %select_select_fusion.6) | copy-start | bytes 6291460
  403.0 4.0 copy-start.14
  407.1 1.4 copy-start.15
  434.8 1.6 copy-start.9
  434.8 219.7 %reduce-scatter.5.cloned.1.call-start = ((), (), s32[]{:S(2)}) async-start(), calls=%async_computation.5 | async-start | bytes 5242880 | tf_op jit(solution)/shard_map/reduce_scatter | solution.py:178
  436.4 16.9 %copy-start.11 = (bf16[256,4096]{1,0:T(8,128)(2,1)S(1)}, bf16[256,4096]{1,0:T(8,128)(2,1)}, u32[]{:S(2)}) copy-start(bf16[256,4096]{1,0:T(8,128)(2,1)} %copy-done.10) | copy-start | bytes 6291460
  436.4 16.9 %copy-start.13 = (bf16[256,4096]{1,0:T(8,128)(2,1)S(1)}, bf16[256,4096]{1,0:T(8,128)(2,1)}, u32[]{:S(2)}) copy-start(bf16[256,4096]{1,0:T(8,128)(2,1)} %copy-done.12) | copy-start | bytes 6291460
  443.3 23.5 %copy-start.4 = (bf16[256,4096]{1,0:T(8,128)(2,1)}, bf16[256,4096]{1,0:T(8,128)(2,1)S(1)}, u32[]{:S(2)}) copy-start(bf16[256,4096]{1,0:T(8,128)(2,1)S(1)} %fusion.19) | copy-start | bytes 6291460
  443.3 45.0 %collective-permute-start.15 = (bf16[256,4096]{1,0:T(8,128)(2,1)S(1)}, bf16[256,4096]{1,0:T(8,128)(2,1)}, u32[]{:S(2)}, u32[]{:S(2)}) collective-permute-start(bf16[256,4096]{1,0:T(8,128)(2,1)S(1)} %fusion.19), channel_id=1, source_target_pairs={{4,0},{8,4},{12,8},{5,1},{9,5},{13,9},{6,2},{10,6},{14,10},{7,3},{... | collective-permute-start | bytes 6291464 | tf_op jit(solution)/shard_map/ppermute | solution.py:100
  444.6 45.4 %collective-permute-start.14 = (bf16[256,4096]{1,0:T(8,128)(2,1)S(1)}, bf16[256,4096]{1,0:T(8,128)(2,1)}, u32[]{:S(2)}, u32[]{:S(2)}) collective-permute-start(bf16[256,4096]{1,0:T(8,128)(2,1)S(1)} %fusion.19), channel_id=1, source_target_pairs={{0,4},{4,8},{8,12},{1,5},{5,9},{9,13},{2,6},{6,10},{10,14},{3,7},{... | collective-permute-start | bytes 6291464 | tf_op jit(solution)/shard_map/ppermute | solution.py:100
  490.2 44.3 %copy-start = (bf16[256,4096]{1,0:T(8,128)(2,1)}, bf16[256,4096]{1,0:T(8,128)(2,1)S(1)}, u32[]{:S(2)}) copy-start(bf16[256,4096]{1,0:T(8,128)(2,1)S(1)} %broadcast_select_fusion.8) | copy-start | bytes 6291460
  490.2 42.8 %collective-permute-start.17 = (bf16[256,4096]{1,0:T(8,128)(2,1)S(1)}, bf16[256,4096]{1,0:T(8,128)(2,1)S(1)}, u32[]{:S(2)}, u32[]{:S(2)}) collective-permute-start(bf16[256,4096]{1,0:T(8,128)(2,1)S(1)} %broadcast_select_fusion.2), channel_id=1, source_target_pairs={{4,0},{8,4},{5,1},{9,5},{6,2},{10,6},{7,3},{11,7},{20,16},{24,20},... | collective-permute-start | bytes 6291464 | tf_op jit(solution)/shard_map/ppermute | solution.py:100
  491.5 43.0 %collective-permute-start.16 = (bf16[256,4096]{1,0:T(8,128)(2,1)S(1)}, bf16[256,4096]{1,0:T(8,128)(2,1)S(1)}, u32[]{:S(2)}, u32[]{:S(2)}) collective-permute-start(bf16[256,4096]{1,0:T(8,128)(2,1)S(1)} %broadcast_select_fusion.8), channel_id=1, source_target_pairs={{4,8},{8,12},{5,9},{9,13},{6,10},{10,14},{7,11},{11,15},{20,24},{2... | collective-permute-start | bytes 6291464 | tf_op jit(solution)/shard_map/ppermute | solution.py:100
  536.0 46.9 %copy-start.1 = (bf16[256,4096]{1,0:T(8,128)(2,1)S(1)}, bf16[256,4096]{1,0:T(8,128)(2,1)}, u32[]{:S(2)}) copy-start(bf16[256,4096]{1,0:T(8,128)(2,1)} %copy-done) | copy-start | bytes 6291460
  536.0 46.9 %copy-start.2 = (bf16[256,4096]{1,0:T(8,128)(2,1)S(1)}, bf16[256,4096]{1,0:T(8,128)(2,1)}, u32[]{:S(2)}) copy-start(bf16[256,4096]{1,0:T(8,128)(2,1)} %broadcast_select_fusion.6) | copy-start | bytes 6291460
  536.0 46.9 %copy-start.3 = (bf16[256,4096]{1,0:T(8,128)(2,1)S(1)}, bf16[256,4096]{1,0:T(8,128)(2,1)}, u32[]{:S(2)}) copy-start(bf16[256,4096]{1,0:T(8,128)(2,1)} %broadcast_select_fusion.10) | copy-start | bytes 6291460
  536.0 46.9 %copy-start.5 = (bf16[256,4096]{1,0:T(8,128)(2,1)S(1)}, bf16[256,4096]{1,0:T(8,128)(2,1)}, u32[]{:S(2)}) copy-start(bf16[256,4096]{1,0:T(8,128)(2,1)} %copy-done.4) | copy-start | bytes 6291460
  536.0 2.5 collective-permute-start.18
  537.0 41.0 %collective-permute-start.19 = (bf16[256,4096]{1,0:T(8,128)(2,1)}, bf16[256,4096]{1,0:T(8,128)(2,1)S(1)}, u32[]{:S(2)}, u32[]{:S(2)}) collective-permute-start(bf16[256,4096]{1,0:T(8,128)(2,1)} %broadcast_select_fusion.6), channel_id=1, source_target_pairs={{4,0},{5,1},{6,2},{7,3},{20,16},{21,17},{22,18},{23,19}} | collective-permute-start | bytes 6291464 | tf_op jit(solution)/shard_map/ppermute | solution.py:100
  606.7 1.0 copy-start.18
  606.7 3.3 copy-start.17
  607.8 2.3 copy-start.16
  623.5 31.0 %copy-start.19 = (bf16[1024,256]{1,0:T(8,128)(2,1)S(1)}, bf16[1024,256]{1,0:T(8,128)(2,1)}, u32[]{:S(2)}) copy-start(bf16[1024,256]{1,0:T(8,128)(2,1)} %param.7) | copy-start | bytes 1572868
Sparse Core Ops, SparseCore 0:
  9.6 25.5 all-gather.2
  36.7 22.8 all-gather.4
  435.0 46.7 reduce-scatter.2
  606.9 47.5 reduce-scatter.4

commit v6 on v4

--- a/solution.py
+++ b/solution.py
@@ -154,18 +154,40 @@
                 (pre_gather.up_cur, pre_gather.down_cur, out_sum, grad_down)
             )
             pre_gather.ups[-1], pre_gather.downs[-1] = pre_gather.up_cur, pre_gather.down_cur
-    pre_grad = pre_gather.result()
     block_out = (hidden_in.astype(jnp.float32) + out_sum).astype(jnp.bfloat16)
-    grad_up = lax.dot_general(
-        x_rows, pre_grad, (((0,), (0,)), ((), ())), preferred_element_type=jnp.float32
-    ).astype(jnp.bfloat16)
-    back_part = lax.dot_general(
-        pre_grad, up_tile, (((1,), (1,)), ((), ())), preferred_element_type=jnp.float32
-    )
-    input_grad = (
-        out_grad.astype(jnp.float32)
-        + lax.psum_scatter(back_part, "p", scatter_dimension=1, tiled=True)
-    ).astype(jnp.bfloat16)
+
+    pos = lax.axis_index("r")
+    rows = pre_gather.block.shape[0]
+    x_blocks = x_rows.reshape(count, rows, x_rows.shape[1])
+    pieces = [(pre_gather.block, pos)]
+    for step in range(count - 1):
+        up_piece, down_piece = pre_gather.ups[step], pre_gather.downs[step]
+        up_at, down_at = pos - 1 - step, pos + 1 + step
+        if 2 * step + 3 <= count:
+            pieces += [(up_piece, up_at), (down_piece, down_at)]
+        else:
+            pieces.append((up_piece + down_piece, jnp.where(up_at >= 0, up_at, down_at)))
+    grad_up = None
+    sums = []
+    for piece, at in pieces:
+        x_block = lax.dynamic_index_in_dim(x_blocks, jnp.clip(at, 0, count - 1), 0, keepdims=False)
+        term = lax.dot_general(
+            x_block, piece, (((0,), (0,)), ((), ())), preferred_element_type=jnp.float32
+        )
+        grad_up = term if grad_up is None else grad_up + term
+        back_rows = lax.dot_general(
+            piece, up_tile, (((1,), (1,)), ((), ())), preferred_element_type=jnp.float32
+        )
+        sums.append((lax.psum_scatter(back_rows, "p", scatter_dimension=1, tiled=True), at))
+    grad_up = grad_up.astype(jnp.bfloat16)
+    grad_blocks = out_grad.reshape(count, rows, out_grad.shape[1]).astype(jnp.float32)
+    input_rows = []
+    for k in range(count):
+        total = grad_blocks[k]
+        for value, at in sums:
+            total = total + jnp.where(at == k, value, jnp.zeros_like(value))
+        input_rows.append(total)
+    input_grad = jnp.concatenate(input_rows, axis=0).astype(jnp.bfloat16)
     return (block_out, input_grad, grad_up[None], grad_down[None])
 
 

time: 660 us -> 678 us (1.027)
  matrix products: 85.8 us -> 154 us
  waiting for transfers between devices: 383 us -> 361 us
  local copies, waits for them, and re-layouts: 23.1 us -> 7.59 us
  starting transfers between devices: 73.3 us -> 65.3 us
    dot_general x2 -> x10, matrix products: 30.7 us -> 98.1 us  [the longest x5 65.7 us: on_device(): lax.dot_general(x_block, piece, (((0,), (0,)), ((), ())), preferred_eleme...]
    unnamed x43 -> x44, local copies, waits for them, and re-layouts: 21.1 us -> 5.61 us
    reduce_scatter x1 -> x5, waiting for transfers between devices: 13.7 us -> 1.71 us  [on_device(): lax.psum_scatter(back_rows, 'p', scatter_dimension=1, tiled=True)]
    ppermute x20, waiting for transfers between devices: 340 us -> 331 us  [run_slot(): received.append(lax.ppermute(combined, 'r', pairs))]
    select_n x8 -> x4, other arithmetic: 23.8 us -> 15.2 us  [result(): pieces.append(lax.select_n(which.astype(jnp.int32), *cases))]
    ppermute x20, starting transfers between devices: 73.1 us -> 64.8 us  [run_slot(): received.append(lax.ppermute(combined, 'r', pairs))]
  transfers between devices with their start and end apart: 24 -> 28, of which waited for: 18 -> 19; matrix products, arithmetic and copies ran while one was open for 17% -> 25% of each run, Pallas kernels for 0% -> 0%
where the time goes in v6:
time: 678 us; the launch traced here: 668 us
  waiting for transfers between devices  361 us (53%)
  matrix products  154 us (23%)
  starting transfers between devices  65.3 us (10%)
  other arithmetic  65.3 us (10%)
  between operations  15.2 us (2%)
  local copies, waits for them, and re-layouts  7.59 us (1%)
    ppermute x20, waiting for transfers between devices, run_slot(): received.append(lax.ppermute(combined, 'r', pairs))  331 us
    dot_general x5, matrix products, on_device(): lax.dot_general(x_block, piece, (((0,), (0,)), ((), ())), preferred_eleme...  65.7 us
    ppermute x20, starting transfers between devices, run_slot(): received.append(lax.ppermute(combined, 'r', pairs))  64.8 us
    dot_general x5, matrix products, on_device(): lax.dot_general(piece, up_tile, (((1,), (1,)), ((), ())), preferred_eleme...  32.4 us
    all_gather x1, waiting for transfers between devices, on_device(): x_rows = lax.all_gather(hidden_in, 'p', axis=1, tiled=True)  26.4 us
    convert_element_type x3, other arithmetic, payload(): return (up.astype(jnp.bfloat16), down.astype(jnp.bfloat16))  16.1 us
    select_n x4, other arithmetic, result(): pieces.append(lax.select_n(which.astype(jnp.int32), *cases))  15.2 us
    dot_general x1, matrix products, on_device(): lax.dot_general(grad_rows, down_tile, (((1,), (1,)), ((), ())), preferred...  14.8 us
  transfers between devices with their start and end apart: 28, of which 19 were waited for; matrix products, arithmetic and copies ran while one was open for 25% of the time, Pallas kernels for 0%

profile of v6, /device:TPU:0, one launch (start us, length us, event | category | flops | bytes accessed | tf_op | source)
XLA Modules:
  0.0 668.4 jit_solution(14889077099267929167)
XLA Ops:
  8.7 26.4 %all-gather.3.cloned.1.call-done = bf16[1024,1024]{1,0:T(8,128)(2,1)} async-done(((bf16[1024,256]{1,0:T(8,128)(2,1)}), bf16[1024,1024]{1,0:T(8,128)(2,1)}) %all-gather.3.cloned.1.call-update) | async-done | bytes 2097168 | tf_op jit(solution)/shard_map/all_gather | solution.py:118
  35.1 12.8 %fusion.16 = bf16[1024,4096]{1,0:T(8,128)(2,1)S(1)} fusion(bf16[1024,1024]{1,0:T(8,128)(2,1)} %all-gather.3.cloned.1.call-done, bf16[1,1024,4096]{2,1,0:T(8,128)(2,1)} %param.5), kind=kOutput, calls=%fused_computation.18 | convolution fusion | flops 8594128896 | bytes 18874368 | tf_op jit(solution)/shard_map/dot_general | solution.py:119
  54.0 4.7 collective-permute-start
  59.6 14.8 %fusion.19 = bf16[1024,4096]{1,0:T(8,128)(2,1)} fusion(bf16[1024,1024]{1,0:T(8,128)(2,1)} %all-gather.5.cloned.1.call-done, bf16[1,4096,1024]{2,1,0:T(8,128)(2,1)} %param.6), kind=kOutput, calls=%fused_computation.19 | convolution fusion | flops 8594128896 | bytes 18874368 | tf_op jit(solution)/shard_map/dot_general | solution.py:121
  74.7 28.0 %collective-permute-done = bf16[256,4096]{1,0:T(8,128)(2,1)} collective-permute-done((bf16[256,4096]{1,0:T(8,128)(2,1)S(1)}, bf16[256,4096]{1,0:T(8,128)(2,1)}, u32[]{:S(2)}, u32[]{:S(2)}) %collective-permute-start) | collective-permute-done | bytes 2097184 | tf_op jit(solution)/shard_map/ppermute | solution.py:100
  102.9 3.5 fusion.38
  106.4 6.2 collective-permute-start.2
  114.7 42.6 %collective-permute-done.2 = bf16[256,4096]{1,0:T(8,128)(2,1)S(1)} collective-permute-done((bf16[256,4096]{1,0:T(8,128)(2,1)}, bf16[256,4096]{1,0:T(8,128)(2,1)S(1)}, u32[]{:S(2)}, u32[]{:S(2)}) %collective-permute-start.2) | collective-permute-done | bytes 2097184 | tf_op jit(solution)/shard_map/ppermute | solution.py:100
  157.3 6.0 fusion.37
  163.3 9.0 %collective-permute-start.3 = (bf16[256,4096]{1,0:T(8,128)(2,1)}, bf16[256,4096]{1,0:T(8,128)(2,1)S(1)}, u32[]{:S(2)}, u32[]{:S(2)}) collective-permute-start(bf16[256,4096]{1,0:T(8,128)(2,1)} %get-tuple-element.24), channel_id=1, source_target_pairs={{0,4},{4,8},{8,12},{1,5},{5,9},{9,13},{2,6},{6,10},{10,14},{3,7},{... | collective-permute-start | bytes 6291464 | tf_op jit(solution)/shard_map/ppermute | solution.py:100
  173.6 42.2 %collective-permute-done.3 = bf16[256,4096]{1,0:T(8,128)(2,1)S(1)} collective-permute-done((bf16[256,4096]{1,0:T(8,128)(2,1)}, bf16[256,4096]{1,0:T(8,128)(2,1)S(1)}, u32[]{:S(2)}, u32[]{:S(2)}) %collective-permute-start.3) | collective-permute-done | bytes 2097184 | tf_op jit(solution)/shard_map/ppermute | solution.py:100
  220.0 3.3 multiply_convert_fusion
  224.6 5.9 collective-permute-start.6
  230.5 39.4 %collective-permute-done.10 = bf16[256,4096]{1,0:T(8,128)(2,1)} collective-permute-done((bf16[256,4096]{1,0:T(8,128)(2,1)S(1)}, bf16[256,4096]{1,0:T(8,128)(2,1)}, u32[]{:S(2)}, u32[]{:S(2)}) %collective-permute-start.10) | collective-permute-done | bytes 2097184 | tf_op jit(solution)/shard_map/ppermute | solution.py:100
  271.0 5.3 bitcast_select_fusion.1
  276.3 6.5 collective-permute-start.7
  284.0 38.5 %collective-permute-done.7 = bf16[256,4096]{1,0:T(8,128)(2,1)} collective-permute-done((bf16[256,4096]{1,0:T(8,128)(2,1)}, bf16[256,4096]{1,0:T(8,128)(2,1)}, u32[]{:S(2)}, u32[]{:S(2)}) %collective-permute-start.7) | collective-permute-done | bytes 2097184 | tf_op jit(solution)/shard_map/ppermute | solution.py:100
  322.5 5.5 collective-permute-done.11
  328.0 5.6 fusion.39
  333.7 3.0 collective-permute-start.8
  338.0 37.5 %collective-permute-done.8 = bf16[256,4096]{1,0:T(8,128)(2,1)} collective-permute-done((bf16[256,4096]{1,0:T(8,128)(2,1)}, bf16[256,4096]{1,0:T(8,128)(2,1)}, u32[]{:S(2)}, u32[]{:S(2)}) %collective-permute-start.8) | collective-permute-done | bytes 2097184 | tf_op jit(solution)/shard_map/ppermute | solution.py:100
  375.6 5.5 collective-permute-done.12
  381.0 3.3 select_select_fusion.2
  384.3 4.0 select_select_fusion.1
  388.3 4.0 select_select_fusion
  392.3 4.0 select_select_fusion.3
  397.7 14.3 %fusion = f32[1024,1024]{1,0:T(8,128)} fusion(bf16[1,4096,1024]{2,1,0:T(8,128)(2,1)} %param.6, bf16[256,4096]{1,0:T(8,128)(2,1)S(1)} %select_select_fusion, bf16[256,4096]{1,0:T(8,128)(2,1)S(1)} %select_select_fusion.1, bf16[256,4096]{1,0:T(8,128)(2,1)S(1)} %select_select_fusion.2, bf16[256,4096]{1,0:T(8,128)(2,1)S(1)} %select_select_fusion.3), kind=kOutput, calls=%fused_computation.2 | convolution fusion | flops 8623489024 | bytes 20971520 | tf_op jit(solution)/shard_map/dot_general | solution.py:141
  412.2 6.7 fusion.32
  418.9 4.7 collective-permute-start.9
  426.0 35.1 %collective-permute-done.9 = bf16[256,4096]{1,0:T(8,128)(2,1)} collective-permute-done((bf16[256,4096]{1,0:T(8,128)(2,1)}, bf16[256,4096]{1,0:T(8,128)(2,1)}, u32[]{:S(2)}, u32[]{:S(2)}) %collective-permute-start.9) | collective-permute-done | bytes 2097184 | tf_op jit(solution)/shard_map/ppermute | solution.py:100
  461.2 5.4 collective-permute-done.13
  466.6 6.8 %fusion.28 = bf16[256,4096]{1,0:T(8,128)(2,1)} fusion(bf16[256,4096]{1,0:T(8,128)(2,1)} %collective-permute-done.13, bf16[4,256,4096]{2,1,0:T(8,128)(2,1)} %bitcast.108, s32[]{:T(128)S(6)} %select_n.536, bf16[256,4096]{1,0:T(8,128)(2,1)} %collective-permute-done.9, pred[]{:T(512)S(6)} %and.26, pred[]{:T(512)S(6)} %and.20, ...), kind=kLoop, calls=%fused_computation.28 | loop fusion | flops 25165824 | bytes 14680070 | tf_op jit(solution)/shard_map/convert_element_type | solution.py:149
  474.8 7.4 %fusion.12 = f32[256,1024]{1,0:T(8,128)} fusion(bf16[256,4096]{1,0:T(8,128)(2,1)} %fusion.28, bf16[1,1024,4096]{2,1,0:T(8,128)(2,1)} %param.5), kind=kOutput, calls=%fused_computation.14 | convolution fusion | flops 2147483648 | bytes 11534336 | tf_op jit(solution)/shard_map/dot_general | solution.py:178
  482.2 13.8 %convolution_convert_fusion = bf16[4096,1024]{1,0:T(8,128)(2,1)} fusion(bf16[1024,1024]{1,0:T(8,128)(2,1)} %all-gather.5.cloned.1.call-done, bf16[256,4096]{1,0:T(8,128)(2,1)} %copy-done.9, bf16[256,4096]{1,0:T(8,128)(2,1)} %copy-done.8, bf16[256,4096]{1,0:T(8,128)(2,1)S(1)} %copy-done.7, bf16[256,4096]{1,0:T(8,128)(2,1)} %copy-done.10), kind=kOutput, calls=%fused_computation.20 | convolution fusion | flops 8627683328 | bytes 18874368 | tf_op jit(solution)/shard_map/dot_general | solution.py:143
  496.0 6.1 collective-permute-start.14
  502.1 13.5 %collective-permute-done.16 = bf16[256,4096]{1,0:T(8,128)(2,1)} collective-permute-done((bf16[256,4096]{1,0:T(8,128)(2,1)}, bf16[256,4096]{1,0:T(8,128)(2,1)}, u32[]{:S(2)}, u32[]{:S(2)}) %collective-permute-start.16) | collective-permute-done | bytes 2097184 | tf_op jit(solution)/shard_map/ppermute | solution.py:100
  517.4 6.7 %fusion.8 = f32[256,1024]{1,0:T(8,128)} fusion(bf16[256,4096]{1,0:T(8,128)(2,1)S(1)} %broadcast_select_fusion.1, bf16[1,1024,4096]{2,1,0:T(8,128)(2,1)} %param.5), kind=kOutput, calls=%fused_computation.10 | convolution fusion | flops 2147483648 | bytes 11534336 | tf_op jit(solution)/shard_map/dot_general | solution.py:178
  524.2 10.1 %fusion.50 = f32[1024,4096]{1,0:T(8,128)} fusion(bf16[256,4096]{1,0:T(8,128)(2,1)} %fusion.28, bf16[4,256,1024]{2,1,0:T(8,128)(2,1)} %bitcast.109, s32[]{:T(128)S(6)} %min.42), kind=kOutput, calls=%fused_computation.85 | convolution fusion | flops 2147483648 | bytes 19398660 | tf_op jit(solution)/shard_map/dot_general | solution.py:174
  541.5 5.0 fusion.10
  546.6 10.1 %fusion.48 = f32[1024,4096]{1,0:T(8,128)} fusion(bf16[256,4096]{1,0:T(8,128)(2,1)} %broadcast_select_fusion.6, bf16[4,256,1024]{2,1,0:T(8,128)(2,1)} %bitcast.110, s32[]{:T(128)S(6)} %min.41), kind=kOutput, calls=%fused_computation.83 | convolution fusion | flops 2147483648 | bytes 19398660 | tf_op jit(solution)/shard_map/dot_general | solution.py:174
  556.7 18.6 %collective-permute-done.17 = bf16[256,4096]{1,0:T(8,128)(2,1)} collective-permute-done((bf16[256,4096]{1,0:T(8,128)(2,1)S(1)}, bf16[256,4096]{1,0:T(8,128)(2,1)}, u32[]{:S(2)}, u32[]{:S(2)}) %collective-permute-start.17) | collective-permute-done | bytes 2097184 | tf_op jit(solution)/shard_map/ppermute | solution.py:100
  575.3 3.0 broadcast_select_fusion.4
  583.4 8.1 %fusion.6 = f32[256,1024]{1,0:T(8,128)} fusion(bf16[1,1024,4096]{2,1,0:T(8,128)(2,1)} %param.5, bf16[256,4096]{1,0:T(8,128)(2,1)} %broadcast_select_fusion.8, bf16[256,4096]{1,0:T(8,128)(2,1)} %broadcast_select_fusion.4), kind=kOutput, calls=%fused_computation.8 | convolution fusion | flops 2148532224 | bytes 13631488 | tf_op jit(solution)/shard_map/dot_general | solution.py:178
  591.6 9.4 %fusion.46 = f32[1024,4096]{1,0:T(8,128)} fusion(bf16[256,4096]{1,0:T(8,128)(2,1)S(1)} %broadcast_select_fusion.1, bf16[4,256,1024]{2,1,0:T(8,128)(2,1)} %bitcast.111, s32[]{:T(128)S(6)} %min.39), kind=kOutput, calls=%fused_computation.81 | convolution fusion | flops 2147483648 | bytes 19398660 | tf_op jit(solution)/shard_map/dot_general | solution.py:174
  602.7 9.6 %fusion.41 = f32[1024,4096]{1,0:T(8,128)} fusion(bf16[256,4096]{1,0:T(8,128)(2,1)S(1)} %copy-done.3, bf16[256,4096]{1,0:T(8,128)(2,1)S(1)} %copy-done.2, bf16[4,256,1024]{2,1,0:T(8,128)(2,1)} %bitcast.112, s32[]{:T(128)S(6)} %min.43), kind=kOutput, calls=%fused_computation.75 | convolution fusion | flops 2148532224 | bytes 21495812 | tf_op jit(solution)/shard_map/dot_general | solution.py:174
  612.3 12.6 %collective-permute-done.19 = bf16[256,4096]{1,0:T(8,128)(2,1)} collective-permute-done((bf16[256,4096]{1,0:T(8,128)(2,1)}, bf16[256,4096]{1,0:T(8,128)(2,1)}, u32[]{:S(2)}, u32[]{:S(2)}) %collective-permute-start.19) | collective-permute-done | bytes 2097184 | tf_op jit(solution)/shard_map/ppermute | solution.py:100
  624.9 5.3 fusion.4
  630.2 26.6 %fusion.22 = bf16[1,1024,4096]{2,1,0:T(8,128)(2,1)} fusion(f32[1024,4096]{1,0:T(8,128)} %fusion.41, f32[1024,4096]{1,0:T(8,128)} %fusion.46, f32[1024,4096]{1,0:T(8,128)} %fusion.50, f32[1024,4096]{1,0:T(8,128)} %fusion.48, bf16[4,256,1024]{2,1,0:T(8,128)(2,1)} %bitcast.113, s32[]{:T(128)S(6)} %min.44, bf16[256,4096]{1,0:T(8,128)(2,1)} %collective-permute-done.19, ...), kind=kOutput, calls=%fused_computation.21 | convolution fusion | flops 2171600896 | bytes 80216072 | tf_op jit(solution)/shard_map/dot_general | solution.py:174
  (99 shorter events, 47.2 us)
Async XLA Ops:
  7.2 28.0 %all-gather.3.cloned.1.call-start = ((), (), s32[]{:S(2)}) async-start(), calls=%async_computation.6 | async-start | bytes 2621440 | tf_op jit(solution)/shard_map/all_gather | solution.py:118
  7.9 51.7 %all-gather.5.cloned.1.call-start = ((), (), s32[]{:S(2)}) async-start(), calls=%async_computation.7 | async-start | bytes 2621440 | tf_op jit(solution)/shard_map/all_gather | solution.py:120
  8.6 571.2 %reduce-scatter.7.cloned.1.call-start = ((), (), s32[]{:S(2)}) async-start(), calls=%async_computation.8 | async-start | bytes 5242880 | tf_op jit(solution)/shard_map/reduce_scatter | solution.py:142
  47.9 4.0 copy-start
  51.9 22.5 %collective-permute-start.1 = (bf16[256,4096]{1,0:T(8,128)(2,1)}, bf16[256,4096]{1,0:T(8,128)(2,1)}, u32[]{:S(2)}, u32[]{:S(2)}) collective-permute-start(bf16[256,4096]{1,0:T(8,128)(2,1)} %get-tuple-element.28), channel_id=1, source_target_pairs={{12,8},{13,9},{14,10},{15,11},{28,24},{29,25},{30,26},{31,27}} | collective-permute-start | bytes 6291464 | tf_op jit(solution)/shard_map/ppermute | solution.py:100
  54.0 48.7 %collective-permute-start = (bf16[256,4096]{1,0:T(8,128)(2,1)S(1)}, bf16[256,4096]{1,0:T(8,128)(2,1)}, u32[]{:S(2)}, u32[]{:S(2)}) collective-permute-start(bf16[256,4096]{1,0:T(8,128)(2,1)S(1)} %get-tuple-element.29), channel_id=1, source_target_pairs={{0,4},{1,5},{2,6},{3,7},{16,20},{17,21},{18,22},{19,23}} | collective-permute-start | bytes 6291464 | tf_op jit(solution)/shard_map/ppermute | solution.py:100
  74.4 28.6 %copy-start.1 = (bf16[1024,4096]{1,0:T(8,128)(2,1)S(1)}, bf16[1024,4096]{1,0:T(8,128)(2,1)}, u32[]{:S(2)}) copy-start(bf16[1024,4096]{1,0:T(8,128)(2,1)} %copy-done) | copy-start | bytes 25165828
  106.4 50.9 %collective-permute-start.2 = (bf16[256,4096]{1,0:T(8,128)(2,1)}, bf16[256,4096]{1,0:T(8,128)(2,1)S(1)}, u32[]{:S(2)}, u32[]{:S(2)}) collective-permute-start(bf16[256,4096]{1,0:T(8,128)(2,1)} %get-tuple-element.26), channel_id=1, source_target_pairs={{0,4},{4,8},{1,5},{5,9},{2,6},{6,10},{3,7},{7,11},{16,20},{20,24},... | collective-permute-start | bytes 6291464 | tf_op jit(solution)/shard_map/ppermute | solution.py:100
  112.6 44.7 %collective-permute-start.4 = (bf16[256,4096]{1,0:T(8,128)(2,1)}, bf16[256,4096]{1,0:T(8,128)(2,1)}, u32[]{:S(2)}, u32[]{:S(2)}) collective-permute-start(bf16[256,4096]{1,0:T(8,128)(2,1)} %get-tuple-element.27), channel_id=1, source_target_pairs={{8,4},{12,8},{9,5},{13,9},{10,6},{14,10},{11,7},{15,11},{24,20},{2... | collective-permute-start | bytes 6291464 | tf_op jit(solution)/shard_map/ppermute | solution.py:100
  163.3 52.5 %collective-permute-start.3 = (bf16[256,4096]{1,0:T(8,128)(2,1)}, bf16[256,4096]{1,0:T(8,128)(2,1)S(1)}, u32[]{:S(2)}, u32[]{:S(2)}) collective-permute-start(bf16[256,4096]{1,0:T(8,128)(2,1)} %get-tuple-element.24), channel_id=1, source_target_pairs={{0,4},{4,8},{8,12},{1,5},{5,9},{9,13},{2,6},{6,10},{10,14},{3,7},{... | collective-permute-start | bytes 6291464 | tf_op jit(solution)/shard_map/ppermute | solution.py:100
  172.3 47.7 %collective-permute-start.5 = (bf16[256,4096]{1,0:T(8,128)(2,1)}, bf16[256,4096]{1,0:T(8,128)(2,1)}, u32[]{:S(2)}, u32[]{:S(2)}) collective-permute-start(bf16[256,4096]{1,0:T(8,128)(2,1)} %get-tuple-element.25), channel_id=1, source_target_pairs={{4,0},{8,4},{12,8},{5,1},{9,5},{13,9},{6,2},{10,6},{14,10},{7,3},{... | collective-permute-start | bytes 6291464 | tf_op jit(solution)/shard_map/ppermute | solution.py:100
  223.3 46.6 %collective-permute-start.10 = (bf16[256,4096]{1,0:T(8,128)(2,1)S(1)}, bf16[256,4096]{1,0:T(8,128)(2,1)}, u32[]{:S(2)}, u32[]{:S(2)}) collective-permute-start(bf16[256,4096]{1,0:T(8,128)(2,1)S(1)} %multiply_convert_fusion), channel_id=1, source_target_pairs={{4,0},{8,4},{12,8},{5,1},{9,5},{13,9},{6,2},{10,6},{14,10},{7,3},{... | collective-permute-start | bytes 6291464 | tf_op jit(solution)/shard_map/ppermute | solution.py:100
  224.6 46.4 %collective-permute-start.6 = (bf16[256,4096]{1,0:T(8,128)(2,1)S(1)}, bf16[256,4096]{1,0:T(8,128)(2,1)}, u32[]{:S(2)}, u32[]{:S(2)}) collective-permute-start(bf16[256,4096]{1,0:T(8,128)(2,1)S(1)} %multiply_convert_fusion), channel_id=1, source_target_pairs={{0,4},{4,8},{8,12},{1,5},{5,9},{9,13},{2,6},{6,10},{10,14},{3,7},{... | collective-permute-start | bytes 6291464 | tf_op jit(solution)/shard_map/ppermute | solution.py:100
  276.3 46.3 %collective-permute-start.7 = (bf16[256,4096]{1,0:T(8,128)(2,1)}, bf16[256,4096]{1,0:T(8,128)(2,1)}, u32[]{:S(2)}, u32[]{:S(2)}) collective-permute-start(bf16[256,4096]{1,0:T(8,128)(2,1)} %get-tuple-element.22), channel_id=1, source_target_pairs={{4,8},{8,12},{0,4},{5,9},{9,13},{1,5},{6,10},{10,14},{2,6},{7,11},... | collective-permute-start | bytes 6291464 | tf_op jit(solution)/shard_map/ppermute | solution.py:100
  282.7 45.3 %collective-permute-start.11 = (bf16[256,4096]{1,0:T(8,128)(2,1)}, bf16[256,4096]{1,0:T(8,128)(2,1)}, u32[]{:S(2)}, u32[]{:S(2)}) collective-permute-start(bf16[256,4096]{1,0:T(8,128)(2,1)} %get-tuple-element.23), channel_id=1, source_target_pairs={{4,0},{8,4},{12,8},{5,1},{9,5},{13,9},{6,2},{10,6},{14,10},{7,3},{... | collective-permute-start | bytes 6291464 | tf_op jit(solution)/shard_map/ppermute | solution.py:100
  333.7 41.9 %collective-permute-start.8 = (bf16[256,4096]{1,0:T(8,128)(2,1)}, bf16[256,4096]{1,0:T(8,128)(2,1)}, u32[]{:S(2)}, u32[]{:S(2)}) collective-permute-start(bf16[256,4096]{1,0:T(8,128)(2,1)} %get-tuple-element.20), channel_id=1, source_target_pairs={{8,12},{0,4},{4,8},{9,13},{1,5},{5,9},{10,14},{2,6},{6,10},{11,15}... | collective-permute-start | bytes 6291464 | tf_op jit(solution)/shard_map/ppermute | solution.py:100
  336.7 44.4 %collective-permute-start.12 = (bf16[256,4096]{1,0:T(8,128)(2,1)}, bf16[256,4096]{1,0:T(8,128)(2,1)}, u32[]{:S(2)}, u32[]{:S(2)}) collective-permute-start(bf16[256,4096]{1,0:T(8,128)(2,1)} %get-tuple-element.21), channel_id=1, source_target_pairs={{4,0},{8,4},{12,8},{5,1},{9,5},{13,9},{6,2},{10,6},{14,10},{7,3},{... | collective-permute-start | bytes 6291464 | tf_op jit(solution)/shard_map/ppermute | solution.py:100
  384.3 12.0 %copy-start.6 = (bf16[256,4096]{1,0:T(8,128)(2,1)}, bf16[256,4096]{1,0:T(8,128)(2,1)S(1)}, u32[]{:S(2)}) copy-start(bf16[256,4096]{1,0:T(8,128)(2,1)S(1)} %select_select_fusion.2) | copy-start | bytes 6291460
  388.3 8.0 %copy-start.8 = (bf16[256,4096]{1,0:T(8,128)(2,1)}, bf16[256,4096]{1,0:T(8,128)(2,1)S(1)}, u32[]{:S(2)}) copy-start(bf16[256,4096]{1,0:T(8,128)(2,1)S(1)} %select_select_fusion.1) | copy-start | bytes 6291460
  392.3 4.0 copy-start.9
  412.0 244.8 %reduce-scatter.9.cloned.1.call-start = ((), (), s32[]{:S(2)}) async-start(), calls=%async_computation.9 | async-start | bytes 1310720 | tf_op jit(solution)/shard_map/reduce_scatter | solution.py:181
  412.2 54.4 %copy-start.5 = (bf16[256,4096]{1,0:T(8,128)(2,1)S(1)}, bf16[256,4096]{1,0:T(8,128)(2,1)}, u32[]{:S(2)}) copy-start(bf16[256,4096]{1,0:T(8,128)(2,1)} %copy-done.4) | copy-start | bytes 6291460
  418.9 42.3 %collective-permute-start.9 = (bf16[256,4096]{1,0:T(8,128)(2,1)}, bf16[256,4096]{1,0:T(8,128)(2,1)}, u32[]{:S(2)}, u32[]{:S(2)}) collective-permute-start(bf16[256,4096]{1,0:T(8,128)(2,1)} %get-tuple-element.18), channel_id=1, source_target_pairs={{0,4},{4,8},{8,12},{1,5},{5,9},{9,13},{2,6},{6,10},{10,14},{3,7},{... | collective-permute-start | bytes 6291464 | tf_op jit(solution)/shard_map/ppermute | solution.py:100
  423.6 43.0 %collective-permute-start.13 = (bf16[256,4096]{1,0:T(8,128)(2,1)}, bf16[256,4096]{1,0:T(8,128)(2,1)}, u32[]{:S(2)}, u32[]{:S(2)}) collective-permute-start(bf16[256,4096]{1,0:T(8,128)(2,1)} %get-tuple-element.19), channel_id=1, source_target_pairs={{4,0},{8,4},{12,8},{5,1},{9,5},{13,9},{6,2},{10,6},{14,10},{7,3},{... | collective-permute-start | bytes 6291464 | tf_op jit(solution)/shard_map/ppermute | solution.py:100
  473.4 8.9 %copy-start.7 = (bf16[256,4096]{1,0:T(8,128)(2,1)S(1)}, bf16[256,4096]{1,0:T(8,128)(2,1)}, u32[]{:S(2)}) copy-start(bf16[256,4096]{1,0:T(8,128)(2,1)} %copy-done.6) | copy-start | bytes 6291460
  473.4 42.3 %collective-permute-start.16 = (bf16[256,4096]{1,0:T(8,128)(2,1)}, bf16[256,4096]{1,0:T(8,128)(2,1)}, u32[]{:S(2)}, u32[]{:S(2)}) collective-permute-start(bf16[256,4096]{1,0:T(8,128)(2,1)} %fusion.28), channel_id=1, source_target_pairs={{4,0},{8,4},{12,8},{5,1},{9,5},{13,9},{6,2},{10,6},{14,10},{7,3},{... | collective-permute-start | bytes 6291464 | tf_op jit(solution)/shard_map/ppermute | solution.py:100
  482.2 174.6 %reduce-scatter.13.cloned.1.call-start = ((), (), s32[]{:S(2)}) async-start(), calls=%async_computation.11 | async-start | bytes 1310720 | tf_op jit(solution)/shard_map/reduce_scatter | solution.py:181
  496.0 42.0 %collective-permute-start.14 = (bf16[256,4096]{1,0:T(8,128)(2,1)}, bf16[256,4096]{1,0:T(8,128)(2,1)}, u32[]{:S(2)}, u32[]{:S(2)}) collective-permute-start(bf16[256,4096]{1,0:T(8,128)(2,1)} %fusion.28), channel_id=1, source_target_pairs={{0,4},{4,8},{8,12},{1,5},{5,9},{9,13},{2,6},{6,10},{10,14},{3,7},{... | collective-permute-start | bytes 6291464 | tf_op jit(solution)/shard_map/ppermute | solution.py:100
  524.1 132.7 %reduce-scatter.11.cloned.1.call-start = ((), (), s32[]{:S(2)}) async-start(), calls=%async_computation.10 | async-start | bytes 1310720 | tf_op jit(solution)/shard_map/reduce_scatter | solution.py:181
  524.2 17.4 %slice-start = ((s8[8388608]{0:T(1024)(128)(4,1)}), s8[4194304]{0:T(1024)(128)(4,1)S(1)}, s32[]{:S(2)}) async-start(s8[8388608]{0:T(1024)(128)(4,1)} %bitcast.114), calls=%async_computation.14 | async-start | bytes 8388608
  524.2 17.4 %slice-start.1 = ((s8[8388608]{0:T(1024)(128)(4,1)}), s8[4194304]{0:T(1024)(128)(4,1)S(1)}, s32[]{:S(2)}) async-start(s8[8388608]{0:T(1024)(128)(4,1)} %bitcast.114), calls=%async_computation.15 | async-start | bytes 8388608
  534.3 41.0 %collective-permute-start.17 = (bf16[256,4096]{1,0:T(8,128)(2,1)S(1)}, bf16[256,4096]{1,0:T(8,128)(2,1)}, u32[]{:S(2)}, u32[]{:S(2)}) collective-permute-start(bf16[256,4096]{1,0:T(8,128)(2,1)S(1)} %broadcast_select_fusion.1), channel_id=1, source_target_pairs={{4,0},{8,4},{5,1},{9,5},{6,2},{10,6},{7,3},{11,7},{20,16},{24,20},... | collective-permute-start | bytes 6291464 | tf_op jit(solution)/shard_map/ppermute | solution.py:100
  539.5 38.8 %collective-permute-start.15 = (bf16[256,4096]{1,0:T(8,128)(2,1)}, bf16[256,4096]{1,0:T(8,128)(2,1)}, u32[]{:S(2)}, u32[]{:S(2)}) collective-permute-start(bf16[256,4096]{1,0:T(8,128)(2,1)} %broadcast_select_fusion.6), channel_id=1, source_target_pairs={{4,8},{8,12},{5,9},{9,13},{6,10},{10,14},{7,11},{11,15},{20,24},{2... | collective-permute-start | bytes 6291464 | tf_op jit(solution)/shard_map/ppermute | solution.py:100
  546.5 110.4 %reduce-scatter.15.cloned.1.call-start = ((), (), s32[]{:S(2)}) async-start(), calls=%async_computation.12 | async-start | bytes 1310720 | tf_op jit(solution)/shard_map/reduce_scatter | solution.py:181
  579.8 32.5 %collective-permute-start.18 = (bf16[256,4096]{1,0:T(8,128)(2,1)}, bf16[256,4096]{1,0:T(8,128)(2,1)}, u32[]{:S(2)}, u32[]{:S(2)}) collective-permute-start(bf16[256,4096]{1,0:T(8,128)(2,1)} %broadcast_select_fusion.8), channel_id=1, source_target_pairs={{8,12},{9,13},{10,14},{11,15},{24,28},{25,29},{26,30},{27,31}} | collective-permute-start | bytes 6291464 | tf_op jit(solution)/shard_map/ppermute | solution.py:100
  581.8 43.1 %collective-permute-start.19 = (bf16[256,4096]{1,0:T(8,128)(2,1)}, bf16[256,4096]{1,0:T(8,128)(2,1)}, u32[]{:S(2)}, u32[]{:S(2)}) collective-permute-start(bf16[256,4096]{1,0:T(8,128)(2,1)} %broadcast_select_fusion.4), channel_id=1, source_target_pairs={{4,0},{5,1},{6,2},{7,3},{20,16},{21,17},{22,18},{23,19}} | collective-permute-start | bytes 6291464 | tf_op jit(solution)/shard_map/ppermute | solution.py:100
  591.5 67.1 %reduce-scatter.17.cloned.1.call-start = ((), (), s32[]{:S(2)}) async-start(), calls=%async_computation.13 | async-start | bytes 1310720 | tf_op jit(solution)/shard_map/reduce_scatter | solution.py:181
  591.5 9.4 %copy-start.11 = (bf16[1024,256]{1,0:T(8,128)(2,1)S(1)}, bf16[1024,256]{1,0:T(8,128)(2,1)}, u32[]{:S(2)}) copy-start(bf16[1024,256]{1,0:T(8,128)(2,1)} %param.4) | copy-start | bytes 1572868
  591.5 9.4 %copy-start.12 = (f32[1024,256]{1,0:T(8,128)S(1)}, f32[1024,256]{1,0:T(8,128)}, u32[]{:S(2)}) copy-start(f32[1024,256]{1,0:T(8,128)} %reduce-scatter.7.cloned.1.call-done) | copy-start | bytes 3145732
  591.6 10.3 %copy-start.3 = (bf16[256,4096]{1,0:T(8,128)(2,1)S(1)}, bf16[256,4096]{1,0:T(8,128)(2,1)}, u32[]{:S(2)}) copy-start(bf16[256,4096]{1,0:T(8,128)(2,1)} %broadcast_select_fusion.8) | copy-start | bytes 6291460
  591.6 33.3 %slice-start.2 = ((s8[8388608]{0:T(1024)(128)(4,1)}), s8[4194304]{0:T(1024)(128)(4,1)S(1)}, s32[]{:S(2)}) async-start(s8[8388608]{0:T(1024)(128)(4,1)} %bitcast.116), calls=%async_computation.16 | async-start | bytes 8388608
  601.0 1.8 copy-start.2
  602.7 22.2 %slice-start.3 = ((s8[8388608]{0:T(1024)(128)(4,1)}), s8[4194304]{0:T(1024)(128)(4,1)S(1)}, s32[]{:S(2)}) async-start(s8[8388608]{0:T(1024)(128)(4,1)} %bitcast.116), calls=%async_computation.17 | async-start | bytes 8388608
  656.8 3.3 copy-start.13
  656.8 3.2 copy-start.14
  656.9 3.2 copy-start.15
  656.9 3.2 copy-start.16
  658.6 1.5 copy-start.17
  (2 other events, 2.7 us)
Sparse Core Ops, SparseCore 0:
  9.6 25.5 all-gather.2
  36.7 22.8 all-gather.4
  412.1 41.7 reduce-scatter.6
  482.3 24.2 reduce-scatter.8
  524.2 22.4 reduce-scatter.12
  549.3 25.0 reduce-scatter.10
  591.6 34.7 reduce-scatter.14
  630.4 28.1 reduce-scatter.16

commit v7 on v6

--- a/solution.py
+++ b/solution.py
@@ -158,7 +158,6 @@
 
     pos = lax.axis_index("r")
     rows = pre_gather.block.shape[0]
-    x_blocks = x_rows.reshape(count, rows, x_rows.shape[1])
     pieces = [(pre_gather.block, pos)]
     for step in range(count - 1):
         up_piece, down_piece = pre_gather.ups[step], pre_gather.downs[step]
@@ -167,19 +166,16 @@
             pieces += [(up_piece, up_at), (down_piece, down_at)]
         else:
             pieces.append((up_piece + down_piece, jnp.where(up_at >= 0, up_at, down_at)))
-    grad_up = None
     sums = []
     for piece, at in pieces:
-        x_block = lax.dynamic_index_in_dim(x_blocks, jnp.clip(at, 0, count - 1), 0, keepdims=False)
-        term = lax.dot_general(
-            x_block, piece, (((0,), (0,)), ((), ())), preferred_element_type=jnp.float32
-        )
-        grad_up = term if grad_up is None else grad_up + term
         back_rows = lax.dot_general(
             piece, up_tile, (((1,), (1,)), ((), ())), preferred_element_type=jnp.float32
         )
         sums.append((lax.psum_scatter(back_rows, "p", scatter_dimension=1, tiled=True), at))
-    grad_up = grad_up.astype(jnp.bfloat16)
+    pre_grad = pre_gather.result()
+    grad_up = lax.dot_general(
+        x_rows, pre_grad, (((0,), (0,)), ((), ())), preferred_element_type=jnp.float32
+    ).astype(jnp.bfloat16)
     grad_blocks = out_grad.reshape(count, rows, out_grad.shape[1]).astype(jnp.float32)
     input_rows = []
     for k in range(count):

time: 678 us -> 669 us (0.987)
  matrix products: 154 us -> 104 us
  waiting for transfers between devices: 361 us -> 379 us
  local copies, waits for them, and re-layouts: 7.59 us -> 22.3 us
  other arithmetic: 65.3 us -> 77.7 us
    dot_general x5 -> x1, matrix products: 65.7 us -> 13.3 us  [on_device(): lax.dot_general(x_rows, pre_grad, (((0,), (0,)), ((), ())), preferred_ele...]
    ppermute x20, waiting for transfers between devices: 331 us -> 350 us  [run_slot(): received.append(lax.ppermute(combined, 'r', pairs))]
    unnamed x44 -> x35, local copies, waits for them, and re-layouts: 5.61 us -> 20.2 us
    select_n x4 -> x8, other arithmetic: 15.2 us -> 28 us  [result(): pieces.append(lax.select_n(which.astype(jnp.int32), *cases))]
  transfers between devices with their start and end apart: 28 -> 28, of which waited for: 19 -> 17; matrix products, arithmetic and copies ran while one was open for 25% -> 21% of each run, Pallas kernels for 0% -> 0%
where the time goes in v7:
time: 669 us; the launch traced here: 660 us
  waiting for transfers between devices  379 us (57%)
  matrix products  104 us (16%)
  other arithmetic  77.7 us (12%)
  starting transfers between devices  62 us (9%)
  local copies, waits for them, and re-layouts  22.3 us (3%)
  between operations  15.2 us (2%)
    ppermute x20, waiting for transfers between devices, run_slot(): received.append(lax.ppermute(combined, 'r', pairs))  350 us
    ppermute x20, starting transfers between devices, run_slot(): received.append(lax.ppermute(combined, 'r', pairs))  61.1 us
    dot_general x5, matrix products, on_device(): lax.dot_general(piece, up_tile, (((1,), (1,)), ((), ())), preferred_eleme...  35.1 us
    select_n x8, other arithmetic, result(): pieces.append(lax.select_n(which.astype(jnp.int32), *cases))  28 us
    all_gather x1, waiting for transfers between devices, on_device(): x_rows = lax.all_gather(hidden_in, 'p', axis=1, tiled=True)  26.4 us
    unnamed x35, local copies, waits for them, and re-layouts  20.2 us
    dot_general x1, matrix products, on_device(): lax.dot_general(grad_rows, down_tile, (((1,), (1,)), ((), ())), preferred...  14.8 us
    dot_general x1, matrix products, on_device(): jnp.dot(activation, down_tile, preferred_element_type=jnp.float32)  14.2 us
  transfers between devices with their start and end apart: 28, of which 17 were waited for; matrix products, arithmetic and copies ran while one was open for 21% of the time, Pallas kernels for 0%

profile of v7, /device:TPU:0, one launch (start us, length us, event | category | flops | bytes accessed | tf_op | source)
XLA Modules:
  0.0 660.2 jit_solution(15566850632707875871)
XLA Ops:
  8.7 26.4 %all-gather.3.cloned.1.call-done = bf16[1024,1024]{1,0:T(8,128)(2,1)} async-done(((bf16[1024,256]{1,0:T(8,128)(2,1)}), bf16[1024,1024]{1,0:T(8,128)(2,1)}) %all-gather.3.cloned.1.call-update) | async-done | bytes 2097168 | tf_op jit(solution)/shard_map/all_gather | solution.py:118
  35.1 12.8 %fusion.24 = bf16[1024,4096]{1,0:T(8,128)(2,1)S(1)} fusion(bf16[1024,1024]{1,0:T(8,128)(2,1)} %all-gather.3.cloned.1.call-done, bf16[1,1024,4096]{2,1,0:T(8,128)(2,1)} %param.5), kind=kOutput, calls=%fused_computation.26 | convolution fusion | flops 8594128896 | bytes 18874368 | tf_op jit(solution)/shard_map/dot_general | solution.py:119
  51.9 4.7 collective-permute-start
  59.6 14.8 %fusion.27 = bf16[1024,4096]{1,0:T(8,128)(2,1)} fusion(bf16[1024,1024]{1,0:T(8,128)(2,1)} %all-gather.5.cloned.1.call-done, bf16[1,4096,1024]{2,1,0:T(8,128)(2,1)} %param.6), kind=kOutput, calls=%fused_computation.27 | convolution fusion | flops 8594128896 | bytes 18874368 | tf_op jit(solution)/shard_map/dot_general | solution.py:121
  74.4 26.5 %collective-permute-done = bf16[256,4096]{1,0:T(8,128)(2,1)} collective-permute-done((bf16[256,4096]{1,0:T(8,128)(2,1)}, bf16[256,4096]{1,0:T(8,128)(2,1)}, u32[]{:S(2)}, u32[]{:S(2)}) %collective-permute-start) | collective-permute-done | bytes 2097184 | tf_op jit(solution)/shard_map/ppermute | solution.py:100
  101.5 2.8 copy-done.3
  104.3 3.4 fusion.47
  107.7 5.1 collective-permute-start.2
  114.9 42.6 %collective-permute-done.2 = bf16[256,4096]{1,0:T(8,128)(2,1)S(1)} collective-permute-done((bf16[256,4096]{1,0:T(8,128)(2,1)}, bf16[256,4096]{1,0:T(8,128)(2,1)S(1)}, u32[]{:S(2)}, u32[]{:S(2)}) %collective-permute-start.2) | collective-permute-done | bytes 2097184 | tf_op jit(solution)/shard_map/ppermute | solution.py:100
  157.5 5.9 fusion.46
  165.2 9.8 %collective-permute-start.3 = (bf16[256,4096]{1,0:T(8,128)(2,1)}, bf16[256,4096]{1,0:T(8,128)(2,1)}, u32[]{:S(2)}, u32[]{:S(2)}) collective-permute-start(bf16[256,4096]{1,0:T(8,128)(2,1)} %get-tuple-element.28), channel_id=1, source_target_pairs={{0,4},{4,8},{8,12},{1,5},{5,9},{9,13},{2,6},{6,10},{10,14},{3,7},{... | collective-permute-start | bytes 6291464 | tf_op jit(solution)/shard_map/ppermute | solution.py:100
  175.0 40.9 %collective-permute-done.5 = bf16[256,4096]{1,0:T(8,128)(2,1)S(1)} collective-permute-done((bf16[256,4096]{1,0:T(8,128)(2,1)}, bf16[256,4096]{1,0:T(8,128)(2,1)S(1)}, u32[]{:S(2)}, u32[]{:S(2)}) %collective-permute-start.5) | collective-permute-done | bytes 2097184 | tf_op jit(solution)/shard_map/ppermute | solution.py:100
  217.4 3.3 multiply_convert_fusion
  220.7 6.0 collective-permute-start.6
  227.9 39.7 %collective-permute-done.6 = bf16[256,4096]{1,0:T(8,128)(2,1)} collective-permute-done((bf16[256,4096]{1,0:T(8,128)(2,1)S(1)}, bf16[256,4096]{1,0:T(8,128)(2,1)}, u32[]{:S(2)}, u32[]{:S(2)}) %collective-permute-start.6) | collective-permute-done | bytes 2097184 | tf_op jit(solution)/shard_map/ppermute | solution.py:100
  267.7 5.5 collective-permute-done.10
  273.2 5.2 bitcast_select_fusion.1
  278.4 4.0 collective-permute-start.7
  283.7 38.5 %collective-permute-done.7 = bf16[256,4096]{1,0:T(8,128)(2,1)} collective-permute-done((bf16[256,4096]{1,0:T(8,128)(2,1)}, bf16[256,4096]{1,0:T(8,128)(2,1)}, u32[]{:S(2)}, u32[]{:S(2)}) %collective-permute-start.7) | collective-permute-done | bytes 2097184 | tf_op jit(solution)/shard_map/ppermute | solution.py:100
  322.3 5.5 collective-permute-done.11
  327.7 5.6 fusion.48
  337.5 37.4 %collective-permute-done.8 = bf16[256,4096]{1,0:T(8,128)(2,1)} collective-permute-done((bf16[256,4096]{1,0:T(8,128)(2,1)}, bf16[256,4096]{1,0:T(8,128)(2,1)}, u32[]{:S(2)}, u32[]{:S(2)}) %collective-permute-start.8) | collective-permute-done | bytes 2097184 | tf_op jit(solution)/shard_map/ppermute | solution.py:100
  374.9 5.4 collective-permute-done.12
  380.4 3.3 select_select_fusion.4
  383.6 4.0 select_select_fusion.5
  387.7 4.0 select_select_fusion.6
  391.7 4.0 select_select_fusion.7
  397.0 14.2 %fusion.8 = f32[1024,1024]{1,0:T(8,128)} fusion(bf16[1,4096,1024]{2,1,0:T(8,128)(2,1)} %param.6, bf16[256,4096]{1,0:T(8,128)(2,1)S(1)} %select_select_fusion.4, bf16[256,4096]{1,0:T(8,128)(2,1)S(1)} %select_select_fusion.5, bf16[256,4096]{1,0:T(8,128)(2,1)S(1)} %select_select_fusion.6, bf16[256,4096]{1,0:T(8,128)(2,1)S(1)} %select_select_fusion.7), kind=kOutput, calls=%fused_computation.9 | convolution fusion | flops 8623489024 | bytes 20971520 | tf_op jit(solution)/shard_map/dot_general | solution.py:141
  411.5 4.3 fusion.41
  417.0 4.9 collective-permute-start.9
  422.0 36.7 %collective-permute-done.13 = bf16[256,4096]{1,0:T(8,128)(2,1)S(1)} collective-permute-done((bf16[256,4096]{1,0:T(8,128)(2,1)S(1)}, bf16[256,4096]{1,0:T(8,128)(2,1)S(1)}, u32[]{:S(2)}, u32[]{:S(2)}) %collective-permute-start.13) | collective-permute-done | bytes 2097184 | tf_op jit(solution)/shard_map/ppermute | solution.py:100
  460.2 6.2 fusion.37
  466.4 4.8 collective-permute-start.14
  472.5 4.9 fusion.20
  477.5 31.3 %collective-permute-done.14 = bf16[256,4096]{1,0:T(8,128)(2,1)S(1)} collective-permute-done((bf16[256,4096]{1,0:T(8,128)(2,1)}, bf16[256,4096]{1,0:T(8,128)(2,1)S(1)}, u32[]{:S(2)}, u32[]{:S(2)}) %collective-permute-start.14) | collective-permute-done | bytes 2097184 | tf_op jit(solution)/shard_map/ppermute | solution.py:100
  513.0 3.0 broadcast_select_fusion.2
  517.4 7.4 %fusion.16 = f32[256,1024]{1,0:T(8,128)} fusion(bf16[256,4096]{1,0:T(8,128)(2,1)} %broadcast_select_fusion.2, bf16[1,1024,4096]{2,1,0:T(8,128)(2,1)} %param.5), kind=kOutput, calls=%fused_computation.17 | convolution fusion | flops 2147483648 | bytes 11534336 | tf_op jit(solution)/shard_map/dot_general | solution.py:171
  525.0 14.1 %convolution_convert_fusion = bf16[4096,1024]{1,0:T(8,128)(2,1)} fusion(bf16[1024,1024]{1,0:T(8,128)(2,1)} %all-gather.5.cloned.1.call-done, bf16[256,4096]{1,0:T(8,128)(2,1)} %copy-done.6, bf16[256,4096]{1,0:T(8,128)(2,1)} %copy-done.7, bf16[256,4096]{1,0:T(8,128)(2,1)} %copy-done.8, bf16[256,4096]{1,0:T(8,128)(2,1)} %copy-done.9), kind=kOutput, calls=%fused_computation.28 | convolution fusion | flops 8627683328 | bytes 18874368 | tf_op jit(solution)/shard_map/dot_general | solution.py:143
  539.1 7.4 %fusion.18 = f32[256,1024]{1,0:T(8,128)} fusion(bf16[256,4096]{1,0:T(8,128)(2,1)} %broadcast_select_fusion.8, bf16[1,1024,4096]{2,1,0:T(8,128)(2,1)} %param.5), kind=kOutput, calls=%fused_computation.19 | convolution fusion | flops 2147483648 | bytes 11534336 | tf_op jit(solution)/shard_map/dot_general | solution.py:171
  548.1 14.6 %collective-permute-done.17 = bf16[256,4096]{1,0:T(8,128)(2,1)} collective-permute-done((bf16[256,4096]{1,0:T(8,128)(2,1)}, bf16[256,4096]{1,0:T(8,128)(2,1)}, u32[]{:S(2)}, u32[]{:S(2)}) %collective-permute-start.17) | collective-permute-done | bytes 2097184 | tf_op jit(solution)/shard_map/ppermute | solution.py:100
  562.7 3.2 broadcast_select_fusion.6
  569.2 8.0 %fusion.14 = f32[256,1024]{1,0:T(8,128)} fusion(bf16[1,1024,4096]{2,1,0:T(8,128)(2,1)} %param.5, bf16[256,4096]{1,0:T(8,128)(2,1)} %broadcast_select_fusion.10, bf16[256,4096]{1,0:T(8,128)(2,1)} %broadcast_select_fusion.6), kind=kOutput, calls=%fused_computation.15 | convolution fusion | flops 2148532224 | bytes 13631488 | tf_op jit(solution)/shard_map/dot_general | solution.py:171
  581.0 22.9 %collective-permute-done.19 = bf16[256,4096]{1,0:T(8,128)(2,1)} collective-permute-done((bf16[256,4096]{1,0:T(8,128)(2,1)}, bf16[256,4096]{1,0:T(8,128)(2,1)}, u32[]{:S(2)}, u32[]{:S(2)}) %collective-permute-start.19) | collective-permute-done | bytes 2097184 | tf_op jit(solution)/shard_map/ppermute | solution.py:100
  604.0 7.5 %fusion.12 = f32[256,1024]{1,0:T(8,128)} fusion(bf16[1,1024,4096]{2,1,0:T(8,128)(2,1)} %param.5, bf16[256,4096]{1,0:T(8,128)(2,1)} %collective-permute-done.19, pred[]{:T(512)S(6)} %and.24, bf16[256,4096]{1,0:T(8,128)(2,1)} %collective-permute-done.18, pred[]{:T(512)S(6)} %and.27), kind=kOutput, calls=%fused_computation.13 | convolution fusion | flops 2150629376 | bytes 13631490 | tf_op jit(solution)/shard_map/dot_general | solution.py:171
  611.5 3.3 select_select_fusion
  620.7 4.3 select_select_fusion.3
  625.0 13.3 %convert_bitcast_fusion = bf16[1,1024,4096]{1,2,0:T(8,128)(2,1)} fusion(bf16[1024,1024]{1,0:T(8,128)(2,1)} %all-gather.3.cloned.1.call-done, bf16[256,4096]{1,0:T(8,128)(2,1)S(1)} %select_select_fusion, bf16[256,4096]{1,0:T(8,128)(2,1)S(1)} %select_select_fusion.1, bf16[256,4096]{1,0:T(8,128)(2,1)S(1)} %select_select_fusion.2, ...), kind=kOutput, calls=%fused_computation.25 | convolution fusion | flops 8627683328 | bytes 18874368 | tf_op jit(solution)/shard_map/dot_general | solution.py:176
  638.3 11.9 %copy.8 = bf16[1,1024,4096]{2,1,0:T(8,128)(2,1)} copy(bf16[1,1024,4096]{1,2,0:T(8,128)(2,1)} %convert_bitcast_fusion) | data formatting | bytes 16777216
  (89 shorter events, 49.5 us)
Async XLA Ops:
  7.2 28.0 %all-gather.3.cloned.1.call-start = ((), (), s32[]{:S(2)}) async-start(), calls=%async_computation.6 | async-start | bytes 2621440 | tf_op jit(solution)/shard_map/all_gather | solution.py:118
  7.9 51.7 %all-gather.5.cloned.1.call-start = ((), (), s32[]{:S(2)}) async-start(), calls=%async_computation.7 | async-start | bytes 2621440 | tf_op jit(solution)/shard_map/all_gather | solution.py:120
  8.6 557.3 %reduce-scatter.7.cloned.1.call-start = ((), (), s32[]{:S(2)}) async-start(), calls=%async_computation.8 | async-start | bytes 5242880 | tf_op jit(solution)/shard_map/reduce_scatter | solution.py:142
  47.9 4.0 copy-start.2
  51.9 49.0 %collective-permute-start = (bf16[256,4096]{1,0:T(8,128)(2,1)}, bf16[256,4096]{1,0:T(8,128)(2,1)}, u32[]{:S(2)}, u32[]{:S(2)}) collective-permute-start(bf16[256,4096]{1,0:T(8,128)(2,1)} %get-tuple-element.33), channel_id=1, source_target_pairs={{0,4},{1,5},{2,6},{3,7},{16,20},{17,21},{18,22},{19,23}} | collective-permute-start | bytes 6291464 | tf_op jit(solution)/shard_map/ppermute | solution.py:100
  56.6 44.6 %collective-permute-start.1 = (bf16[256,4096]{1,0:T(8,128)(2,1)S(1)}, bf16[256,4096]{1,0:T(8,128)(2,1)}, u32[]{:S(2)}, u32[]{:S(2)}) collective-permute-start(bf16[256,4096]{1,0:T(8,128)(2,1)S(1)} %get-tuple-element.32), channel_id=1, source_target_pairs={{12,8},{13,9},{14,10},{15,11},{28,24},{29,25},{30,26},{31,27}} | collective-permute-start | bytes 6291464 | tf_op jit(solution)/shard_map/ppermute | solution.py:100
  100.9 3.4 copy-start.3
  107.7 49.8 %collective-permute-start.2 = (bf16[256,4096]{1,0:T(8,128)(2,1)}, bf16[256,4096]{1,0:T(8,128)(2,1)S(1)}, u32[]{:S(2)}, u32[]{:S(2)}) collective-permute-start(bf16[256,4096]{1,0:T(8,128)(2,1)} %get-tuple-element.30), channel_id=1, source_target_pairs={{0,4},{4,8},{1,5},{5,9},{2,6},{6,10},{3,7},{7,11},{16,20},{20,24},... | collective-permute-start | bytes 6291464 | tf_op jit(solution)/shard_map/ppermute | solution.py:100
  112.9 44.7 %collective-permute-start.4 = (bf16[256,4096]{1,0:T(8,128)(2,1)}, bf16[256,4096]{1,0:T(8,128)(2,1)}, u32[]{:S(2)}, u32[]{:S(2)}) collective-permute-start(bf16[256,4096]{1,0:T(8,128)(2,1)} %get-tuple-element.31), channel_id=1, source_target_pairs={{8,4},{12,8},{9,5},{13,9},{10,6},{14,10},{11,7},{15,11},{24,20},{2... | collective-permute-start | bytes 6291464 | tf_op jit(solution)/shard_map/ppermute | solution.py:100
  163.5 52.5 %collective-permute-start.5 = (bf16[256,4096]{1,0:T(8,128)(2,1)}, bf16[256,4096]{1,0:T(8,128)(2,1)S(1)}, u32[]{:S(2)}, u32[]{:S(2)}) collective-permute-start(bf16[256,4096]{1,0:T(8,128)(2,1)} %get-tuple-element.29), channel_id=1, source_target_pairs={{4,0},{8,4},{12,8},{5,1},{9,5},{13,9},{6,2},{10,6},{14,10},{7,3},{... | collective-permute-start | bytes 6291464 | tf_op jit(solution)/shard_map/ppermute | solution.py:100
  165.2 52.2 %collective-permute-start.3 = (bf16[256,4096]{1,0:T(8,128)(2,1)}, bf16[256,4096]{1,0:T(8,128)(2,1)}, u32[]{:S(2)}, u32[]{:S(2)}) collective-permute-start(bf16[256,4096]{1,0:T(8,128)(2,1)} %get-tuple-element.28), channel_id=1, source_target_pairs={{0,4},{4,8},{8,12},{1,5},{5,9},{9,13},{2,6},{6,10},{10,14},{3,7},{... | collective-permute-start | bytes 6291464 | tf_op jit(solution)/shard_map/ppermute | solution.py:100
  215.9 1.4 copy-start.4
  220.7 47.0 %collective-permute-start.6 = (bf16[256,4096]{1,0:T(8,128)(2,1)S(1)}, bf16[256,4096]{1,0:T(8,128)(2,1)}, u32[]{:S(2)}, u32[]{:S(2)}) collective-permute-start(bf16[256,4096]{1,0:T(8,128)(2,1)S(1)} %multiply_convert_fusion), channel_id=1, source_target_pairs={{0,4},{4,8},{8,12},{1,5},{5,9},{9,13},{2,6},{6,10},{10,14},{3,7},{... | collective-permute-start | bytes 6291464 | tf_op jit(solution)/shard_map/ppermute | solution.py:100
  226.6 46.6 %collective-permute-start.10 = (bf16[256,4096]{1,0:T(8,128)(2,1)S(1)}, bf16[256,4096]{1,0:T(8,128)(2,1)}, u32[]{:S(2)}, u32[]{:S(2)}) collective-permute-start(bf16[256,4096]{1,0:T(8,128)(2,1)S(1)} %multiply_convert_fusion), channel_id=1, source_target_pairs={{4,0},{8,4},{12,8},{5,1},{9,5},{13,9},{6,2},{10,6},{14,10},{7,3},{... | collective-permute-start | bytes 6291464 | tf_op jit(solution)/shard_map/ppermute | solution.py:100
  278.4 43.8 %collective-permute-start.7 = (bf16[256,4096]{1,0:T(8,128)(2,1)}, bf16[256,4096]{1,0:T(8,128)(2,1)}, u32[]{:S(2)}, u32[]{:S(2)}) collective-permute-start(bf16[256,4096]{1,0:T(8,128)(2,1)} %get-tuple-element.26), channel_id=1, source_target_pairs={{4,8},{8,12},{0,4},{5,9},{9,13},{1,5},{6,10},{10,14},{2,6},{7,11},... | collective-permute-start | bytes 6291464 | tf_op jit(solution)/shard_map/ppermute | solution.py:100
  282.4 45.3 %collective-permute-start.11 = (bf16[256,4096]{1,0:T(8,128)(2,1)}, bf16[256,4096]{1,0:T(8,128)(2,1)}, u32[]{:S(2)}, u32[]{:S(2)}) collective-permute-start(bf16[256,4096]{1,0:T(8,128)(2,1)} %get-tuple-element.27), channel_id=1, source_target_pairs={{4,0},{8,4},{12,8},{5,1},{9,5},{13,9},{6,2},{10,6},{14,10},{7,3},{... | collective-permute-start | bytes 6291464 | tf_op jit(solution)/shard_map/ppermute | solution.py:100
  333.4 41.6 %collective-permute-start.8 = (bf16[256,4096]{1,0:T(8,128)(2,1)}, bf16[256,4096]{1,0:T(8,128)(2,1)}, u32[]{:S(2)}, u32[]{:S(2)}) collective-permute-start(bf16[256,4096]{1,0:T(8,128)(2,1)} %get-tuple-element.24), channel_id=1, source_target_pairs={{8,12},{0,4},{4,8},{9,13},{1,5},{5,9},{10,14},{2,6},{6,10},{11,15}... | collective-permute-start | bytes 6291464 | tf_op jit(solution)/shard_map/ppermute | solution.py:100
  336.2 44.2 %collective-permute-start.12 = (bf16[256,4096]{1,0:T(8,128)(2,1)}, bf16[256,4096]{1,0:T(8,128)(2,1)}, u32[]{:S(2)}, u32[]{:S(2)}) collective-permute-start(bf16[256,4096]{1,0:T(8,128)(2,1)} %get-tuple-element.25), channel_id=1, source_target_pairs={{4,0},{8,4},{12,8},{5,1},{9,5},{13,9},{6,2},{10,6},{14,10},{7,3},{... | collective-permute-start | bytes 6291464 | tf_op jit(solution)/shard_map/ppermute | solution.py:100
  383.6 12.0 %copy-start.6 = (bf16[256,4096]{1,0:T(8,128)(2,1)}, bf16[256,4096]{1,0:T(8,128)(2,1)S(1)}, u32[]{:S(2)}) copy-start(bf16[256,4096]{1,0:T(8,128)(2,1)S(1)} %select_select_fusion.4) | copy-start | bytes 6291460
  387.6 8.0 %copy-start.7 = (bf16[256,4096]{1,0:T(8,128)(2,1)}, bf16[256,4096]{1,0:T(8,128)(2,1)S(1)}, u32[]{:S(2)}) copy-start(bf16[256,4096]{1,0:T(8,128)(2,1)S(1)} %select_select_fusion.5) | copy-start | bytes 6291460
  391.7 4.0 copy-start.8
  395.7 1.3 copy-start.9
  411.2 49.0 %copy-start.5 = (bf16[256,4096]{1,0:T(8,128)(2,1)S(1)}, bf16[256,4096]{1,0:T(8,128)(2,1)}, u32[]{:S(2)}) copy-start(bf16[256,4096]{1,0:T(8,128)(2,1)} %copy-done.4) | copy-start | bytes 6291460
  411.2 239.0 %reduce-scatter.9.cloned.1.call-start = ((), (), s32[]{:S(2)}) async-start(), calls=%async_computation.9 | async-start | bytes 1310720 | tf_op jit(solution)/shard_map/reduce_scatter | solution.py:174
  411.5 61.1 %slice-start = ((s8[8388608]{0:T(1024)(128)(4,1)}), s8[4194304]{0:T(1024)(128)(4,1)S(1)}, s32[]{:S(2)}) async-start(s8[8388608]{0:T(1024)(128)(4,1)} %bitcast.93), calls=%async_computation.14 | async-start | bytes 8388608
  415.7 43.0 %collective-permute-start.13 = (bf16[256,4096]{1,0:T(8,128)(2,1)S(1)}, bf16[256,4096]{1,0:T(8,128)(2,1)S(1)}, u32[]{:S(2)}, u32[]{:S(2)}) collective-permute-start(bf16[256,4096]{1,0:T(8,128)(2,1)S(1)} %get-tuple-element.23), channel_id=1, source_target_pairs={{4,0},{8,4},{12,8},{5,1},{9,5},{13,9},{6,2},{10,6},{14,10},{7,3},{... | collective-permute-start | bytes 6291464 | tf_op jit(solution)/shard_map/ppermute | solution.py:100
  417.0 55.5 %slice-start.1 = ((s8[8388608]{0:T(1024)(128)(4,1)}), s8[4194304]{0:T(1024)(128)(4,1)S(1)}, s32[]{:S(2)}) async-start(s8[8388608]{0:T(1024)(128)(4,1)} %bitcast.93), calls=%async_computation.15 | async-start | bytes 8388608
  417.0 43.1 %collective-permute-start.9 = (bf16[256,4096]{1,0:T(8,128)(2,1)S(1)}, bf16[256,4096]{1,0:T(8,128)(2,1)S(1)}, u32[]{:S(2)}, u32[]{:S(2)}) collective-permute-start(bf16[256,4096]{1,0:T(8,128)(2,1)S(1)} %get-tuple-element.22), channel_id=1, source_target_pairs={{0,4},{4,8},{8,12},{1,5},{5,9},{9,13},{2,6},{6,10},{10,14},{3,7},{... | collective-permute-start | bytes 6291464 | tf_op jit(solution)/shard_map/ppermute | solution.py:100
  466.4 42.4 %collective-permute-start.14 = (bf16[256,4096]{1,0:T(8,128)(2,1)}, bf16[256,4096]{1,0:T(8,128)(2,1)S(1)}, u32[]{:S(2)}, u32[]{:S(2)}) collective-permute-start(bf16[256,4096]{1,0:T(8,128)(2,1)} %fusion.37), channel_id=1, source_target_pairs={{0,4},{4,8},{8,12},{1,5},{5,9},{9,13},{2,6},{6,10},{10,14},{3,7},{... | collective-permute-start | bytes 6291464 | tf_op jit(solution)/shard_map/ppermute | solution.py:100
  471.2 41.8 %collective-permute-start.16 = (bf16[256,4096]{1,0:T(8,128)(2,1)}, bf16[256,4096]{1,0:T(8,128)(2,1)}, u32[]{:S(2)}, u32[]{:S(2)}) collective-permute-start(bf16[256,4096]{1,0:T(8,128)(2,1)} %fusion.37), channel_id=1, source_target_pairs={{4,0},{8,4},{12,8},{5,1},{9,5},{13,9},{6,2},{10,6},{14,10},{7,3},{... | collective-permute-start | bytes 6291464 | tf_op jit(solution)/shard_map/ppermute | solution.py:100
  477.5 172.7 %reduce-scatter.13.cloned.1.call-start = ((), (), s32[]{:S(2)}) async-start(), calls=%async_computation.11 | async-start | bytes 1310720 | tf_op jit(solution)/shard_map/reduce_scatter | solution.py:174
  510.3 36.3 %collective-permute-start.15 = (bf16[256,4096]{1,0:T(8,128)(2,1)}, bf16[256,4096]{1,0:T(8,128)(2,1)}, u32[]{:S(2)}, u32[]{:S(2)}) collective-permute-start(bf16[256,4096]{1,0:T(8,128)(2,1)} %broadcast_select_fusion.8), channel_id=1, source_target_pairs={{4,8},{8,12},{5,9},{9,13},{6,10},{10,14},{7,11},{11,15},{20,24},{2... | collective-permute-start | bytes 6291464 | tf_op jit(solution)/shard_map/ppermute | solution.py:100
  516.1 46.6 %collective-permute-start.17 = (bf16[256,4096]{1,0:T(8,128)(2,1)}, bf16[256,4096]{1,0:T(8,128)(2,1)}, u32[]{:S(2)}, u32[]{:S(2)}) collective-permute-start(bf16[256,4096]{1,0:T(8,128)(2,1)} %broadcast_select_fusion.2), channel_id=1, source_target_pairs={{4,0},{8,4},{5,1},{9,5},{6,2},{10,6},{7,3},{11,7},{20,16},{24,20},... | collective-permute-start | bytes 6291464 | tf_op jit(solution)/shard_map/ppermute | solution.py:100
  524.7 125.5 %reduce-scatter.11.cloned.1.call-start = ((), (), s32[]{:S(2)}) async-start(), calls=%async_computation.10 | async-start | bytes 1310720 | tf_op jit(solution)/shard_map/reduce_scatter | solution.py:174
  546.5 103.8 %reduce-scatter.15.cloned.1.call-start = ((), (), s32[]{:S(2)}) async-start(), calls=%async_computation.12 | async-start | bytes 1310720 | tf_op jit(solution)/shard_map/reduce_scatter | solution.py:174
  565.9 38.0 %collective-permute-start.19 = (bf16[256,4096]{1,0:T(8,128)(2,1)}, bf16[256,4096]{1,0:T(8,128)(2,1)}, u32[]{:S(2)}, u32[]{:S(2)}) collective-permute-start(bf16[256,4096]{1,0:T(8,128)(2,1)} %broadcast_select_fusion.6), channel_id=1, source_target_pairs={{4,0},{5,1},{6,2},{7,3},{20,16},{21,17},{22,18},{23,19}} | collective-permute-start | bytes 6291464 | tf_op jit(solution)/shard_map/ppermute | solution.py:100
  567.2 36.7 %collective-permute-start.18 = (bf16[256,4096]{1,0:T(8,128)(2,1)}, bf16[256,4096]{1,0:T(8,128)(2,1)}, u32[]{:S(2)}, u32[]{:S(2)}) collective-permute-start(bf16[256,4096]{1,0:T(8,128)(2,1)} %broadcast_select_fusion.10), channel_id=1, source_target_pairs={{8,12},{9,13},{10,14},{11,15},{24,28},{25,29},{26,30},{27,31}} | collective-permute-start | bytes 6291464 | tf_op jit(solution)/shard_map/ppermute | solution.py:100
  577.3 73.0 %reduce-scatter.17.cloned.1.call-start = ((), (), s32[]{:S(2)}) async-start(), calls=%async_computation.13 | async-start | bytes 1310720 | tf_op jit(solution)/shard_map/reduce_scatter | solution.py:174
  611.4 3.5 copy-start
  611.5 4.1 copy-start.1
  650.2 1.7 copy-start.10
  650.2 1.7 copy-start.11
  650.2 1.6 copy-start.12
  650.3 1.6 copy-start.13
  650.3 1.6 copy-start.14
Sparse Core Ops, SparseCore 0:
  9.6 25.5 all-gather.2
  36.7 22.8 all-gather.4
  411.3 41.7 reduce-scatter.6
  477.6 25.7 reduce-scatter.8
  524.9 30.9 reduce-scatter.12
  558.4 24.8 reduce-scatter.10
  585.8 24.9 reduce-scatter.14
  613.4 24.8 reduce-scatter.16

commit v8 on v4

--- a/solution.py
+++ b/solution.py
@@ -132,29 +132,20 @@
     for step in range(1, count - 1):
         run_slot([(up_sum, step)])
     preact = up_sum.result()
-    act_gather = LineGather(gelu_value(preact).astype(jnp.bfloat16))
-    if count > 1:
-        run_slot([(act_gather, 0)])
-    for step in range(1, count - 1):
-        run_slot([(act_gather, step), (grad_sum, step - 1)])
-    activation = act_gather.result()
+    act_shard = gelu_value(preact).astype(jnp.bfloat16)
+    act_shard, grad_sum.shares = lax.optimization_barrier((act_shard, grad_sum.shares))
+    activation = lax.all_gather(act_shard, "r", axis=0, tiled=True)
+    for step in range(count - 1):
+        run_slot([(grad_sum, step)])
     out_part = jnp.dot(activation, down_tile, preferred_element_type=jnp.float32)
     out_sum = lax.psum_scatter(out_part, "p", scatter_dimension=1, tiled=True)
     grad_down = lax.dot_general(
         activation, grad_rows, (((0,), (0,)), ((), ())), preferred_element_type=jnp.float32
     ).astype(jnp.bfloat16)
-    if count > 1:
-        run_slot([(grad_sum, count - 2)])
     act_grad = grad_sum.result()
-    pre_gather = LineGather((act_grad * gelu_slope(preact)).astype(jnp.bfloat16))
-    for step in range(count - 1):
-        run_slot([(pre_gather, step)])
-        if step == min(1, count - 2):
-            pre_gather.up_cur, pre_gather.down_cur, out_sum, grad_down = lax.optimization_barrier(
-                (pre_gather.up_cur, pre_gather.down_cur, out_sum, grad_down)
-            )
-            pre_gather.ups[-1], pre_gather.downs[-1] = pre_gather.up_cur, pre_gather.down_cur
-    pre_grad = pre_gather.result()
+    pre_grad = lax.all_gather(
+        (act_grad * gelu_slope(preact)).astype(jnp.bfloat16), "r", axis=0, tiled=True
+    )
     block_out = (hidden_in.astype(jnp.float32) + out_sum).astype(jnp.bfloat16)
     grad_up = lax.dot_general(
         x_rows, pre_grad, (((0,), (0,)), ((), ())), preferred_element_type=jnp.float32

time: 660 us -> 763 us (1.16)
  waiting for transfers between devices: 383 us -> 559 us
  other arithmetic: 72 us -> 30.7 us
  starting transfers between devices: 73.3 us -> 40.8 us
    all_gather x0 -> x2, waiting for transfers between devices: none -> 134 us  [the longest x1 134 us: on_device(): lax.all_gather((act_grad * gelu_slope(preact)).astype(jnp.bfloat16), 'r',...]
    select_n x14 -> x0, other arithmetic: 42.4 us -> none  [the longest x8 23.8 us: result(): pieces.append(lax.select_n(which.astype(jnp.int32), *cases))]
    ppermute x20 -> x12, starting transfers between devices: 73.1 us -> 40.4 us  [run_slot(): received.append(lax.ppermute(combined, 'r', pairs))]
    ppermute x20 -> x12, waiting for transfers between devices: 340 us -> 365 us  [run_slot(): received.append(lax.ppermute(combined, 'r', pairs))]
    reduce_scatter x1, waiting for transfers between devices: 13.7 us -> 30.9 us  [on_device(): lax.psum_scatter(back_part, 'p', scatter_dimension=1, tiled=True)]
    unnamed x43 -> x17, local copies, waits for them, and re-layouts: 21.1 us -> 15.8 us
    convert_element_type x3 -> x4, other arithmetic: 15.7 us -> 15.4 us  [payload(): return (up.astype(jnp.bfloat16), down.astype(jnp.bfloat16))]
  transfers between devices with their start and end apart: 24 -> 18, of which waited for: 18 -> 12; matrix products, arithmetic and copies ran while one was open for 17% -> 16% of each run, Pallas kernels for 0% -> 0%
where the time goes in v8:
time: 763 us; the launch traced here: 754 us
  waiting for transfers between devices  559 us (73%)
  matrix products  88.1 us (12%)
  starting transfers between devices  40.8 us (5%)
  other arithmetic  30.7 us (4%)
  local copies, waits for them, and re-layouts  20.7 us (3%)
  between operations  14.7 us (2%)
    ppermute x12, waiting for transfers between devices, run_slot(): received.append(lax.ppermute(combined, 'r', pairs))  365 us
    all_gather x1, waiting for transfers between devices, on_device(): lax.all_gather((act_grad * gelu_slope(preact)).astype(jnp.bfloat16), 'r',...  134 us
    ppermute x12, starting transfers between devices, run_slot(): received.append(lax.ppermute(combined, 'r', pairs))  40.4 us
    reduce_scatter x1, waiting for transfers between devices, on_device(): lax.psum_scatter(back_part, 'p', scatter_dimension=1, tiled=True)  30.9 us
    all_gather x1, waiting for transfers between devices, on_device(): x_rows = lax.all_gather(hidden_in, 'p', axis=1, tiled=True)  26.4 us
    unnamed x17, local copies, waits for them, and re-layouts  15.8 us
    dot_general x1, matrix products, on_device(): lax.dot_general(activation, grad_rows, (((0,), (0,)), ((), ())), preferre...  15.4 us
    convert_element_type x4, other arithmetic, payload(): return (up.astype(jnp.bfloat16), down.astype(jnp.bfloat16))  15.4 us
  transfers between devices with their start and end apart: 18, of which 12 were waited for; matrix products, arithmetic and copies ran while one was open for 16% of the time, Pallas kernels for 0%

profile of v8, /device:TPU:0, one launch (start us, length us, event | category | flops | bytes accessed | tf_op | source)
XLA Modules:
  0.0 753.6 jit_solution(3028282464989747171)
XLA Ops:
  7.2 0.7 all-gather.5.cloned.1.call-update
  7.9 0.7 all-gather.7.cloned.1.call-update
  8.7 26.4 %all-gather.5.cloned.1.call-done = bf16[1024,1024]{1,0:T(8,128)(2,1)} async-done(((bf16[1024,256]{1,0:T(8,128)(2,1)}), bf16[1024,1024]{1,0:T(8,128)(2,1)}) %all-gather.5.cloned.1.call-update) | async-done | bytes 2097168 | tf_op jit(solution)/shard_map/all_gather | solution.py:118
  35.1 12.8 %fusion.8 = bf16[1024,4096]{1,0:T(8,128)(2,1)S(1)} fusion(bf16[1024,1024]{1,0:T(8,128)(2,1)} %all-gather.5.cloned.1.call-done, bf16[1,1024,4096]{2,1,0:T(8,128)(2,1)} %param.5), kind=kOutput, calls=%fused_computation.10 | convolution fusion | flops 8594128896 | bytes 18874368 | tf_op jit(solution)/shard_map/dot_general | solution.py:119
  47.9 2.0 dynamic-slice_bitcast_fusion.2
  49.9 2.0 copy-done
  51.9 2.0 collective-permute-start.1
  54.0 4.7 collective-permute-start
  58.7 0.9 all-gather.7.cloned.1.call-done
  59.6 14.8 %fusion.11 = bf16[1024,4096]{1,0:T(8,128)(2,1)} fusion(bf16[1024,1024]{1,0:T(8,128)(2,1)} %all-gather.7.cloned.1.call-done, bf16[1,4096,1024]{2,1,0:T(8,128)(2,1)} %param.6), kind=kOutput, calls=%fused_computation.11 | convolution fusion | flops 8594128896 | bytes 18874368 | tf_op jit(solution)/shard_map/dot_general | solution.py:121
  74.4 0.3 select_convert_fusion
  74.7 28.0 %collective-permute-done = bf16[256,4096]{1,0:T(8,128)(2,1)} collective-permute-done((bf16[256,4096]{1,0:T(8,128)(2,1)S(1)}, bf16[256,4096]{1,0:T(8,128)(2,1)}, u32[]{:S(2)}, u32[]{:S(2)}) %collective-permute-start) | collective-permute-done | bytes 2097184 | tf_op jit(solution)/shard_map/ppermute | solution.py:100
  102.6 0.3 select_convert_fusion.1
  102.9 3.5 fusion.29
  106.4 6.2 collective-permute-start.2
  112.6 2.0 collective-permute-start.4
  114.7 42.6 %collective-permute-done.2 = bf16[256,4096]{1,0:T(8,128)(2,1)S(1)} collective-permute-done((bf16[256,4096]{1,0:T(8,128)(2,1)}, bf16[256,4096]{1,0:T(8,128)(2,1)S(1)}, u32[]{:S(2)}, u32[]{:S(2)}) %collective-permute-start.2) | collective-permute-done | bytes 2097184 | tf_op jit(solution)/shard_map/ppermute | solution.py:100
  157.3 5.9 fusion.28
  163.2 8.7 %collective-permute-start.3 = (bf16[256,4096]{1,0:T(8,128)(2,1)}, bf16[256,4096]{1,0:T(8,128)(2,1)S(1)}, u32[]{:S(2)}, u32[]{:S(2)}) collective-permute-start(bf16[256,4096]{1,0:T(8,128)(2,1)} %get-tuple-element.24), channel_id=1, source_target_pairs={{0,4},{4,8},{8,12},{1,5},{5,9},{9,13},{2,6},{6,10},{10,14},{3,7},{... | collective-permute-start | bytes 6291464 | tf_op jit(solution)/shard_map/ppermute | solution.py:100
  172.0 1.3 collective-permute-start.5
  173.3 42.2 %collective-permute-done.3 = bf16[256,4096]{1,0:T(8,128)(2,1)S(1)} collective-permute-done((bf16[256,4096]{1,0:T(8,128)(2,1)}, bf16[256,4096]{1,0:T(8,128)(2,1)S(1)}, u32[]{:S(2)}, u32[]{:S(2)}) %collective-permute-start.3) | collective-permute-done | bytes 2097184 | tf_op jit(solution)/shard_map/ppermute | solution.py:100
  215.4 4.2 collective-permute-done.5
  219.7 4.2 multiply_convert_fusion
  224.0 2.9 dynamic-slice_bitcast_fusion.1
  226.9 2.2 collective-permute-start.6
  229.1 0.9 collective-permute-start.9
  230.0 85.3 %collective-permute-done.6 = bf16[256,4096]{1,0:T(8,128)(2,1)S(1)} collective-permute-done((bf16[256,4096]{1,0:T(8,128)(2,1)S(1)}, bf16[256,4096]{1,0:T(8,128)(2,1)S(1)}, u32[]{:S(2)}, u32[]{:S(2)}) %collective-permute-start.6) | collective-permute-done | bytes 2097184 | tf_op jit(solution)/shard_map/ppermute | solution.py:100
  315.3 4.1 fusion.24
  319.4 0.8 collective-permute-start.10
  320.2 5.0 collective-permute-start.7
  325.2 87.9 %collective-permute-done.7 = bf16[256,4096]{1,0:T(8,128)(2,1)S(1)} collective-permute-done((bf16[256,4096]{1,0:T(8,128)(2,1)S(1)}, bf16[256,4096]{1,0:T(8,128)(2,1)S(1)}, u32[]{:S(2)}, u32[]{:S(2)}) %collective-permute-start.7) | collective-permute-done | bytes 2097184 | tf_op jit(solution)/shard_map/ppermute | solution.py:100
  413.2 1.9 fusion.23
  415.1 1.3 collective-permute-start.11
  416.4 5.1 collective-permute-start.8
  421.5 36.5 %collective-permute-done.11 = bf16[256,4096]{1,0:T(8,128)(2,1)S(1)} collective-permute-done((bf16[256,4096]{1,0:T(8,128)(2,1)S(1)}, bf16[256,4096]{1,0:T(8,128)(2,1)S(1)}, u32[]{:S(2)}, u32[]{:S(2)}) %collective-permute-start.11) | collective-permute-done | bytes 2097184 | tf_op jit(solution)/shard_map/ppermute | solution.py:100
  458.1 38.0 %collective-permute-done.8 = bf16[256,4096]{1,0:T(8,128)(2,1)S(1)} collective-permute-done((bf16[256,4096]{1,0:T(8,128)(2,1)S(1)}, bf16[256,4096]{1,0:T(8,128)(2,1)S(1)}, u32[]{:S(2)}, u32[]{:S(2)}) %collective-permute-start.8) | collective-permute-done | bytes 2097184 | tf_op jit(solution)/shard_map/ppermute | solution.py:100
  496.0 6.2 fusion.19
  502.3 15.1 %fusion = f32[1024,1024]{1,0:T(8,128)} fusion(bf16[1024,4096]{1,0:T(8,128)(2,1)} %all-gather.9.cloned.1.call-done, bf16[1,4096,1024]{2,1,0:T(8,128)(2,1)} %param.6), kind=kOutput, calls=%fused_computation | convolution fusion | flops 8589934592 | bytes 20971520 | tf_op jit(solution)/shard_map/dot_general | solution.py:140
  517.4 0.3 reduce-scatter.5.cloned.1.call-start
  517.7 134.3 %all-gather.11.cloned.1.call-done = bf16[1024,4096]{1,0:T(8,128)(2,1)} async-done(((bf16[256,4096]{1,0:T(8,128)(2,1)}), bf16[1024,4096]{1,0:T(8,128)(2,1)}) %all-gather.11.cloned.1.call-update) | async-done | bytes 8388624 | tf_op jit(solution)/shard_map/all_gather | solution.py:146
  651.9 15.1 %fusion.4 = f32[1024,1024]{1,0:T(8,128)} fusion(bf16[1024,4096]{1,0:T(8,128)(2,1)} %all-gather.11.cloned.1.call-done, bf16[1,1024,4096]{2,1,0:T(8,128)(2,1)} %param.5), kind=kOutput, calls=%fused_computation.4 | convolution fusion | flops 8589934592 | bytes 20971520 | tf_op jit(solution)/shard_map/dot_general | solution.py:153
  667.1 1.6 copy-done.5
  668.7 15.4 %convert_bitcast_fusion = bf16[1,4096,1024]{2,1,0:T(8,128)(2,1)} fusion(bf16[1024,4096]{1,0:T(8,128)(2,1)} %all-gather.9.cloned.1.call-done, bf16[1024,1024]{1,0:T(8,128)(2,1)S(1)} %copy-done.5), kind=kOutput, calls=%fused_computation.8 | convolution fusion | flops 8594128896 | bytes 18874368 | tf_op jit(solution)/shard_map/dot_general | solution.py:142
  684.1 14.9 %convert_bitcast_fusion.1 = bf16[1,1024,4096]{1,2,0:T(8,128)(2,1)} fusion(bf16[1024,4096]{1,0:T(8,128)(2,1)} %all-gather.11.cloned.1.call-done, bf16[1024,1024]{1,0:T(8,128)(2,1)S(1)} %copy-done.4), kind=kOutput, calls=%fused_computation.9 | convolution fusion | flops 8594128896 | bytes 18874368 | tf_op jit(solution)/shard_map/dot_general | solution.py:150
  699.0 12.2 %copy.8 = bf16[1,1024,4096]{2,1,0:T(8,128)(2,1)} copy(bf16[1,1024,4096]{1,2,0:T(8,128)(2,1)} %convert_bitcast_fusion.1) | data formatting | bytes 16777216
  711.2 2.1 add_convert_fusion.1
  713.3 30.9 %reduce-scatter.5.cloned.1.call-done = f32[1024,256]{1,0:T(8,128)} async-done(((f32[1024,1024]{1,0:T(8,128)}), f32[1024,256]{1,0:T(8,128)}) %reduce-scatter.5.cloned.1.call-update) | async-done | bytes 1048592 | tf_op jit(solution)/shard_map/reduce_scatter | solution.py:158
  744.2 2.1 add_convert_fusion
  (30 shorter events, 0.3 us)
Async XLA Ops:
  7.2 28.0 %all-gather.5.cloned.1.call-start = ((), (), s32[]{:S(2)}) async-start(), calls=%async_computation.2 | async-start | bytes 2621440 | tf_op jit(solution)/shard_map/all_gather | solution.py:118
  7.9 51.7 %all-gather.7.cloned.1.call-start = ((), (), s32[]{:S(2)}) async-start(), calls=%async_computation.3 | async-start | bytes 2621440 | tf_op jit(solution)/shard_map/all_gather | solution.py:120
  8.6 493.7 %all-gather.9.cloned.1.call-start = ((), (), s32[]{:S(2)}) async-start(), calls=%async_computation.4 | async-start | bytes 10485760 | tf_op jit(solution)/shard_map/all_gather | solution.py:137
  47.9 4.0 copy-start
  51.9 22.5 %collective-permute-start.1 = (bf16[256,4096]{1,0:T(8,128)(2,1)}, bf16[256,4096]{1,0:T(8,128)(2,1)}, u32[]{:S(2)}, u32[]{:S(2)}) collective-permute-start(bf16[256,4096]{1,0:T(8,128)(2,1)} %get-tuple-element.28), channel_id=1, source_target_pairs={{12,8},{13,9},{14,10},{15,11},{28,24},{29,25},{30,26},{31,27}} | collective-permute-start | bytes 6291464 | tf_op jit(solution)/shard_map/ppermute | solution.py:100
  54.0 48.7 %collective-permute-start = (bf16[256,4096]{1,0:T(8,128)(2,1)S(1)}, bf16[256,4096]{1,0:T(8,128)(2,1)}, u32[]{:S(2)}, u32[]{:S(2)}) collective-permute-start(bf16[256,4096]{1,0:T(8,128)(2,1)S(1)} %get-tuple-element.29), channel_id=1, source_target_pairs={{0,4},{1,5},{2,6},{3,7},{16,20},{17,21},{18,22},{19,23}} | collective-permute-start | bytes 6291464 | tf_op jit(solution)/shard_map/ppermute | solution.py:100
  74.4 28.5 %copy-start.1 = (bf16[1024,4096]{1,0:T(8,128)(2,1)S(1)}, bf16[1024,4096]{1,0:T(8,128)(2,1)}, u32[]{:S(2)}) copy-start(bf16[1024,4096]{1,0:T(8,128)(2,1)} %copy-done) | copy-start | bytes 25165828
  106.4 50.9 %collective-permute-start.2 = (bf16[256,4096]{1,0:T(8,128)(2,1)}, bf16[256,4096]{1,0:T(8,128)(2,1)S(1)}, u32[]{:S(2)}, u32[]{:S(2)}) collective-permute-start(bf16[256,4096]{1,0:T(8,128)(2,1)} %get-tuple-element.26), channel_id=1, source_target_pairs={{0,4},{4,8},{1,5},{5,9},{2,6},{6,10},{3,7},{7,11},{16,20},{20,24},... | collective-permute-start | bytes 6291464 | tf_op jit(solution)/shard_map/ppermute | solution.py:100
  112.6 44.7 %collective-permute-start.4 = (bf16[256,4096]{1,0:T(8,128)(2,1)}, bf16[256,4096]{1,0:T(8,128)(2,1)}, u32[]{:S(2)}, u32[]{:S(2)}) collective-permute-start(bf16[256,4096]{1,0:T(8,128)(2,1)} %get-tuple-element.27), channel_id=1, source_target_pairs={{8,4},{12,8},{9,5},{13,9},{10,6},{14,10},{11,7},{15,11},{24,20},{2... | collective-permute-start | bytes 6291464 | tf_op jit(solution)/shard_map/ppermute | solution.py:100
  163.2 52.2 %collective-permute-start.3 = (bf16[256,4096]{1,0:T(8,128)(2,1)}, bf16[256,4096]{1,0:T(8,128)(2,1)S(1)}, u32[]{:S(2)}, u32[]{:S(2)}) collective-permute-start(bf16[256,4096]{1,0:T(8,128)(2,1)} %get-tuple-element.24), channel_id=1, source_target_pairs={{0,4},{4,8},{8,12},{1,5},{5,9},{9,13},{2,6},{6,10},{10,14},{3,7},{... | collective-permute-start | bytes 6291464 | tf_op jit(solution)/shard_map/ppermute | solution.py:100
  172.0 47.7 %collective-permute-start.5 = (bf16[256,4096]{1,0:T(8,128)(2,1)}, bf16[256,4096]{1,0:T(8,128)(2,1)}, u32[]{:S(2)}, u32[]{:S(2)}) collective-permute-start(bf16[256,4096]{1,0:T(8,128)(2,1)} %get-tuple-element.25), channel_id=1, source_target_pairs={{4,0},{8,4},{12,8},{5,1},{9,5},{13,9},{6,2},{10,6},{14,10},{7,3},{... | collective-permute-start | bytes 6291464 | tf_op jit(solution)/shard_map/ppermute | solution.py:100
  223.9 428.0 %all-gather.11.cloned.1.call-start = ((), (), s32[]{:S(2)}) async-start(), calls=%async_computation.6 | async-start | bytes 10485760 | tf_op jit(solution)/shard_map/all_gather | solution.py:146
  224.0 189.2 %slice-start = ((s8[8388608]{0:T(1024)(128)(4,1)}), s8[4194304]{0:T(1024)(128)(4,1)S(1)}, s32[]{:S(2)}) async-start(s8[8388608]{0:T(1024)(128)(4,1)} %bitcast.85), calls=%async_computation.8 | async-start | bytes 8388608
  226.9 88.4 %collective-permute-start.6 = (bf16[256,4096]{1,0:T(8,128)(2,1)S(1)}, bf16[256,4096]{1,0:T(8,128)(2,1)S(1)}, u32[]{:S(2)}, u32[]{:S(2)}) collective-permute-start(bf16[256,4096]{1,0:T(8,128)(2,1)S(1)} %get-tuple-element.22), channel_id=1, source_target_pairs={{0,4},{1,5},{2,6},{3,7},{16,20},{17,21},{18,22},{19,23}} | collective-permute-start | bytes 6291464 | tf_op jit(solution)/shard_map/ppermute | solution.py:100
  229.1 184.1 %slice-start.1 = ((s8[8388608]{0:T(1024)(128)(4,1)}), s8[4194304]{0:T(1024)(128)(4,1)S(1)}, s32[]{:S(2)}) async-start(s8[8388608]{0:T(1024)(128)(4,1)} %bitcast.85), calls=%async_computation.9 | async-start | bytes 8388608
  229.1 86.2 %collective-permute-start.9 = (bf16[256,4096]{1,0:T(8,128)(2,1)S(1)}, bf16[256,4096]{1,0:T(8,128)(2,1)S(1)}, u32[]{:S(2)}, u32[]{:S(2)}) collective-permute-start(bf16[256,4096]{1,0:T(8,128)(2,1)S(1)} %get-tuple-element.23), channel_id=1, source_target_pairs={{12,8},{13,9},{14,10},{15,11},{28,24},{29,25},{30,26},{31,27}} | collective-permute-start | bytes 6291464 | tf_op jit(solution)/shard_map/ppermute | solution.py:100
  319.4 5.8 collective-permute-start.10
  320.2 92.9 %collective-permute-start.7 = (bf16[256,4096]{1,0:T(8,128)(2,1)S(1)}, bf16[256,4096]{1,0:T(8,128)(2,1)S(1)}, u32[]{:S(2)}, u32[]{:S(2)}) collective-permute-start(bf16[256,4096]{1,0:T(8,128)(2,1)S(1)} %get-tuple-element.20), channel_id=1, source_target_pairs={{0,4},{4,8},{1,5},{5,9},{2,6},{6,10},{3,7},{7,11},{16,20},{20,24},... | collective-permute-start | bytes 6291464 | tf_op jit(solution)/shard_map/ppermute | solution.py:100
  415.1 43.0 %collective-permute-start.11 = (bf16[256,4096]{1,0:T(8,128)(2,1)S(1)}, bf16[256,4096]{1,0:T(8,128)(2,1)S(1)}, u32[]{:S(2)}, u32[]{:S(2)}) collective-permute-start(bf16[256,4096]{1,0:T(8,128)(2,1)S(1)} %get-tuple-element.19), channel_id=1, source_target_pairs={{4,0},{8,4},{12,8},{5,1},{9,5},{13,9},{6,2},{10,6},{14,10},{7,3},{... | collective-permute-start | bytes 6291464 | tf_op jit(solution)/shard_map/ppermute | solution.py:100
  416.4 79.7 %collective-permute-start.8 = (bf16[256,4096]{1,0:T(8,128)(2,1)S(1)}, bf16[256,4096]{1,0:T(8,128)(2,1)S(1)}, u32[]{:S(2)}, u32[]{:S(2)}) collective-permute-start(bf16[256,4096]{1,0:T(8,128)(2,1)S(1)} %get-tuple-element.18), channel_id=1, source_target_pairs={{0,4},{4,8},{8,12},{1,5},{5,9},{9,13},{2,6},{6,10},{10,14},{3,7},{... | collective-permute-start | bytes 6291464 | tf_op jit(solution)/shard_map/ppermute | solution.py:100
  502.2 208.9 %reduce-scatter.3.cloned.1.call-start = ((), (), s32[]{:S(2)}) async-start(), calls=%async_computation.5 | async-start | bytes 5242880 | tf_op jit(solution)/shard_map/reduce_scatter | solution.py:141
  517.4 226.8 %reduce-scatter.5.cloned.1.call-start = ((), (), s32[]{:S(2)}) async-start(), calls=%async_computation.7 | async-start | bytes 5242880 | tf_op jit(solution)/shard_map/reduce_scatter | solution.py:158
  667.1 1.6 copy-start.5
  668.7 15.4 %copy-start.4 = (bf16[1024,1024]{1,0:T(8,128)(2,1)S(1)}, bf16[1024,1024]{1,0:T(8,128)(2,1)}, u32[]{:S(2)}) copy-start(bf16[1024,1024]{1,0:T(8,128)(2,1)} %all-gather.5.cloned.1.call-done) | copy-start | bytes 6291460
  699.0 12.2 %copy-start.2 = (bf16[1024,256]{1,0:T(8,128)(2,1)S(1)}, bf16[1024,256]{1,0:T(8,128)(2,1)}, u32[]{:S(2)}) copy-start(bf16[1024,256]{1,0:T(8,128)(2,1)} %param.4) | copy-start | bytes 1572868
  699.0 45.2 %copy-start.3 = (bf16[1024,256]{1,0:T(8,128)(2,1)S(1)}, bf16[1024,256]{1,0:T(8,128)(2,1)}, u32[]{:S(2)}) copy-start(bf16[1024,256]{1,0:T(8,128)(2,1)} %param.7) | copy-start | bytes 1572868
Sparse Core Ops, SparseCore 0:
  9.6 25.5 all-gather.4
  36.7 22.8 all-gather.6
  224.1 264.1 all-gather.8
  502.4 149.5 all-gather.10
  654.3 42.7 reduce-scatter.2
  699.6 44.5 reduce-scatter.4
